TPU v7x, 256 devices: a whole 4x4x8 slice. The times are simulated.
256 devices in a mesh: expert: 32 (over z_hi, y, core), dp: 8 (over z_lo, x).
Axes of the slice: x: 4, y: 4, z: 8 (z_hi: 4, z_lo: 2; z = z_hi * 2 + z_lo), core: 2. Of those that a mesh axis runs over, the one named last changes fastest.
Arguments:
- tokens: bfloat16 [2048, 196, 384], P(('expert', 'dp')), may hold values from -6 to 6
- router: bfloat16 [384, 64], replicated, may hold values from -1 to 65
- expert_in: bfloat16 [64, 384, 1536], P('expert'), may hold values from -2.5 to 2.5
- expert_out: bfloat16 [64, 1536, 384], P('expert'), may hold values from -0.15625 to 0.15625
- out_grad: bfloat16 [2048, 196, 384], P(('expert', 'dp')), may hold values from -6 to 6
Outputs:
- grad_tokens: bfloat16 [2048, 196, 384], P(('expert', 'dp'))
- grad_in: float32 [64, 384, 1536], P('expert', None, 'dp')
- grad_out: float32 [64, 1536, 384], P('expert', 'dp')
- grad_router: float32 [384, 64], replicated
All inputs are finite; a program needn't handle non-finite values.
Results may differ from a plain program's by a relative error of at most 0.017.
Values may be sent and summed in bfloat16 or wider, within the bound.
No kernel may reach another device: no remote copies, remote signals or barrier semaphores. Data moves between devices by JAX's collectives and lax.ppermute only.
A program may use at most 64 MiB of HBM per device.

v0:
```python
import jax
import jax.numpy as jnp
from jax import lax
from jax.sharding import PartitionSpec as P


def on_device(tokens, router, expert_in, expert_out, out_grad):
    logits = jnp.einsum("bpd,ds->bps", tokens, router, preferred_element_type=jnp.float32)
    dispatch = jax.nn.softmax(logits, axis=1)
    combine = jax.nn.softmax(logits, axis=2)
    dispatch_low = dispatch.astype(jnp.bfloat16)
    combine_low = combine.astype(jnp.bfloat16)
    slots = jnp.einsum(
        "bps,bpd->bsd", dispatch_low, tokens, preferred_element_type=jnp.float32
    ).astype(jnp.bfloat16)
    slot_grads = jnp.einsum(
        "bps,bpd->bsd", combine_low, out_grad, preferred_element_type=jnp.float32
    ).astype(jnp.bfloat16)
    slots_here, grads_here = (
        lax.all_to_all(slots, "expert", split_axis=1, concat_axis=0, tiled=True),
        lax.all_to_all(slot_grads, "expert", split_axis=1, concat_axis=0, tiled=True),
    )
    hidden = jnp.einsum("rjd,jdf->rjf", slots_here, expert_in, preferred_element_type=jnp.float32)
    activated, gelu_back = jax.vjp(jax.nn.gelu, hidden)
    activated_low = activated.astype(jnp.bfloat16)
    outputs_here = jnp.einsum(
        "rjf,jfd->rjd", activated_low, expert_out, preferred_element_type=jnp.float32
    ).astype(jnp.bfloat16)
    act_grad = jnp.einsum(
        "rjd,jfd->rjf", grads_here, expert_out, preferred_element_type=jnp.float32
    )
    hidden_grad = gelu_back(act_grad)[0].astype(jnp.bfloat16)
    input_grad_here = jnp.einsum(
        "rjf,jdf->rjd", hidden_grad, expert_in, preferred_element_type=jnp.float32
    ).astype(jnp.bfloat16)
    outputs, inputs_grad = (
        lax.all_to_all(outputs_here, "expert", split_axis=0, concat_axis=1, tiled=True),
        lax.all_to_all(input_grad_here, "expert", split_axis=0, concat_axis=1, tiled=True),
    )
    first_term = jnp.einsum(
        "rjd,rjf->jdf", slots_here, hidden_grad, preferred_element_type=jnp.float32
    )
    second_term = jnp.einsum(
        "rjf,rjd->jfd", activated_low, grads_here, preferred_element_type=jnp.float32
    )
    grad_in = lax.psum_scatter(
        first_term.astype(jnp.bfloat16), "dp", scatter_dimension=2, tiled=True
    ).astype(jnp.float32)
    grad_out = lax.psum_scatter(
        second_term.astype(jnp.bfloat16), "dp", scatter_dimension=1, tiled=True
    ).astype(jnp.float32)
    combine_grad = jnp.einsum("bpd,bsd->bps", out_grad, outputs, preferred_element_type=jnp.float32)
    dispatch_grad = jnp.einsum(
        "bpd,bsd->bps", tokens, inputs_grad, preferred_element_type=jnp.float32
    )
    logit_grad = dispatch * (
        dispatch_grad - jnp.sum(dispatch * dispatch_grad, axis=1, keepdims=True)
    )
    logit_grad = logit_grad + combine * (
        combine_grad - jnp.sum(combine * combine_grad, axis=2, keepdims=True)
    )
    logit_low = logit_grad.astype(jnp.bfloat16)
    first_part = jnp.einsum(
        "bps,bsd->bpd", dispatch_low, inputs_grad, preferred_element_type=jnp.float32
    )
    second_part = jnp.einsum("bps,ds->bpd", logit_low, router, preferred_element_type=jnp.float32)
    grad_tokens = (first_part + second_part).astype(jnp.bfloat16)
    router_term = jnp.einsum("bpd,bps->ds", tokens, logit_low, preferred_element_type=jnp.float32)
    grad_router = lax.psum(router_term, ("expert", "dp"))
    return (grad_tokens, grad_in, grad_out, grad_router)


def solution(mesh):
    placed = (
        P(("expert", "dp"), None, None),
        P(),
        P("expert", None, None),
        P("expert", None, None),
        P(("expert", "dp"), None, None),
    )
    return jax.shard_map(
        on_device,
        mesh=mesh,
        in_specs=placed,
        out_specs=(
            P(("expert", "dp"), None, None),
            P("expert", None, "dp"),
            P("expert", "dp", None),
            P(),
        ),
        check_vma=False,
    )
```

profile of v0, /device:TPU:32, one launch (start us, length us, event | category | flops | bytes accessed | tf_op | source)
XLA Modules:
  0.0 384.2 jit_solution(1332848046215882536)
XLA Ops:
  8.0 2.8 fusion.56
  10.9 1.5 copy.40
  12.6 1.8 convolution_convert_fusion.4
  15.5 10.6 %all-to-all-start.1 = ((bf16[8,64,384]{2,0,1:T(8,128)(2,1)}), bf16[8,64,384]{2,0,1:T(8,128)(2,1)S(1)}, u32[]{:S(2)}, u32[]{:S(2)}) async-start(bf16[8,64,384]{2,0,1:T(8,128)(2,1)} %copy.27), calls=%async_computation.1 | async-start | bytes 786432 | tf_op jit(solution)/shard_map/all_to_all | solution.py:20
  26.0 1.8 convolution_convert_fusion.5
  28.8 12.1 %all-to-all-done.1 = bf16[8,64,384]{2,0,1:T(8,128)(2,1)S(1)} async-done(((bf16[8,64,384]{2,0,1:T(8,128)(2,1)}), bf16[8,64,384]{2,0,1:T(8,128)(2,1)S(1)}, u32[]{:S(2)}, u32[]{:S(2)}) %all-to-all-start.1) | async-done | bytes 393248 | tf_op jit(solution)/shard_map/all_to_all | solution.py:20
  40.9 4.7 %all-to-all-start = ((bf16[8,64,384]{2,0,1:T(8,128)(2,1)}), bf16[8,64,384]{2,0,1:T(8,128)(2,1)}, u32[]{:S(2)}, u32[]{:S(2)}) async-start(bf16[8,64,384]{2,0,1:T(8,128)(2,1)} %copy.24), calls=%async_computation | async-start | bytes 786432 | tf_op jit(solution)/shard_map/all_to_all | solution.py:21
  45.7 4.3 %convolution_bitcast_fusion = f32[256,2,1536]{2,0,1:T(8,128)} fusion(bf16[2,384,1536]{2,1,0:T(8,128)(2,1)} %param.7, bf16[8,32,2,384]{3,0,2,1:T(8,128)(2,1)S(1)} %bitcast.59), kind=kOutput, calls=%fused_computation.6 | convolution fusion | flops 603979776 | bytes 5898240 | tf_op jit(solution)/shard_map/rjd,jdf->rjf/dot_general | solution.py:23
  50.0 9.8 %all-to-all-done = bf16[8,64,384]{2,0,1:T(8,128)(2,1)} async-done(((bf16[8,64,384]{2,0,1:T(8,128)(2,1)}), bf16[8,64,384]{2,0,1:T(8,128)(2,1)}, u32[]{:S(2)}, u32[]{:S(2)}) %all-to-all-start) | async-done | bytes 393248 | tf_op jit(solution)/shard_map/all_to_all | solution.py:21
  59.8 4.8 %convolution_convert_fusion = bf16[2,1536,384]{2,1,0:T(8,128)(2,1)} fusion(bf16[8,32,2,384]{3,0,2,1:T(8,128)(2,1)} %bitcast.1, f32[256,2,1536]{2,0,1:T(8,128)} %convolution_bitcast_fusion), kind=kOutput, calls=%fused_computation.4 | convolution fusion | flops 612237312 | bytes 5898240 | tf_op jit(solution)/shard_map/rjf,rjd->jfd/dot_general | solution.py:43
  64.7 4.2 %fusion.8 = bf16[256,2,1536]{2,0,1:T(8,128)(2,1)S(1)} fusion(f32[256,2,1536]{2,0,1:T(8,128)} %convolution_bitcast_fusion, bf16[2,1536,384]{2,1,0:T(8,128)(2,1)S(1)} %copy-done, bf16[8,32,2,384]{3,0,2,1:T(8,128)(2,1)} %bitcast.1), kind=kOutput, calls=%fused_computation.14 | convolution fusion | flops 619708416 | bytes 7471104 | tf_op jit(solution)/shard_map/rjd,jfd->rjf/dot_general | solution.py:29
  68.9 1.2 copy-done.2
  70.1 2.4 convolution_convert_fusion.1
  72.6 3.1 fusion.16
  76.9 5.9 %all-to-all-start.3 = ((bf16[256,2,384]{2,1,0:T(2,128)(2,1)}), bf16[256,2,384]{2,1,0:T(2,128)(2,1)S(1)}, u32[]{:S(2)}, u32[]{:S(2)}) async-start(bf16[256,2,384]{2,1,0:T(2,128)(2,1)} %copy.32), calls=%async_computation.3 | async-start | bytes 786432 | tf_op jit(solution)/shard_map/all_to_all | solution.py:37
  82.8 3.2 fusion.15
  87.1 15.3 %all-to-all-done.3 = bf16[256,2,384]{2,1,0:T(2,128)(2,1)S(1)} async-done(((bf16[256,2,384]{2,1,0:T(2,128)(2,1)}), bf16[256,2,384]{2,1,0:T(2,128)(2,1)S(1)}, u32[]{:S(2)}, u32[]{:S(2)}) %all-to-all-start.3) | async-done | bytes 393248 | tf_op jit(solution)/shard_map/all_to_all | solution.py:37
  102.4 4.6 %all-to-all-start.2 = ((bf16[256,2,384]{2,1,0:T(2,128)(2,1)}), bf16[256,2,384]{2,1,0:T(2,128)(2,1)}, u32[]{:S(2)}, u32[]{:S(2)}) async-start(bf16[256,2,384]{2,1,0:T(2,128)(2,1)} %copy.29), calls=%async_computation.2 | async-start | bytes 786432 | tf_op jit(solution)/shard_map/all_to_all | solution.py:38
  108.3 1.9 all_to_all.67
  110.2 14.4 %all-to-all-done.2 = bf16[256,2,384]{2,1,0:T(2,128)(2,1)} async-done(((bf16[256,2,384]{2,1,0:T(2,128)(2,1)}), bf16[256,2,384]{2,1,0:T(2,128)(2,1)}, u32[]{:S(2)}, u32[]{:S(2)}) %all-to-all-start.2) | async-done | bytes 393248 | tf_op jit(solution)/shard_map/all_to_all | solution.py:38
  124.5 2.0 copy.74
  127.7 2.0 convolution_bitcast_fusion.2
  131.2 1.4 convolution_bitcast_fusion.3
  132.7 5.2 %convolution_bitcast_fusion.4 = f32[384,64]{0,1:T(8,128)} fusion(f32[8,196,64]{1,2,0:T(8,128)} %fusion.13, f32[8,196,64]{1,2,0:T(8,128)} %convolution_bitcast_fusion.3, bf16[8,196,384]{2,0,1:T(8,128)(2,1)} %param.5, f32[8,196,64]{1,2,0:T(8,128)S(1)} %copy.40, f32[8,64]{1,0:T(8,128)S(1)} %get-tuple-element.15, f32[8,64]{1,0:T(8,128)S(1)} %get-tuple-element.13), kind=kOutput, calls=%fused_computation.31 | convolution fusion | flops 77974208 | bytes 2510848 | tf_op jit(solution)/shard_map/bpd,bps->ds/dot_general | solution.py:68
  137.9 2.5 fusion.40
  140.4 6.1 %add_convert_fusion = bf16[8,196,384]{2,1,0:T(8,128)(2,1)} fusion(f32[8,196,384]{2,1,0:T(8,128)} %fusion.40, f32[8,196,64]{1,2,0:T(8,128)} %fusion.13, f32[8,196,64]{1,2,0:T(8,128)} %convolution_bitcast_fusion.3, bf16[384,64]{0,1:T(8,128)(2,1)S(1)} %copy-done.3, f32[8,196,64]{1,2,0:T(8,128)S(1)} %copy.40, f32[8,64]{1,0:T(8,128)S(1)} %get-tuple-element.15, ...), kind=kOutput, calls=%fused_computation.16 | convolution fusion | flops 79178432 | bytes 4870144 | tf_op jit(solution)/shard_map/bps,ds->bpd/dot_general | solution.py:66
  146.5 2.5 copy.38
  149.0 1.8 convert_element_type.63
  150.8 17.7 %reduce-scatter.3.cloned.1.call-done = bf16[2,384,192]{1,2,0:T(8,128)(2,1)} async-done(((bf16[2,384,1536]{1,2,0:T(8,128)(2,1)}), bf16[2,384,192]{1,2,0:T(8,128)(2,1)}) %reduce-scatter.3.cloned.1.call-update) | async-done | bytes 294928 | tf_op jit(solution)/shard_map/reduce_scatter | solution.py:46
  168.5 1.8 convert_element_type.61
  170.3 205.0 %all-reduce.2.cloned.1.call-done = f32[384,64]{0,1:T(8,128)} async-done(((f32[384,64]{0,1:T(8,128)}), f32[384,64]{0,1:T(8,128)}) %all-reduce.2.cloned.1.call-update) | async-done | bytes 98320 | tf_op jit(solution)/shard_map/psum | solution.py:69
  375.3 1.5 copy.76
  (23 shorter events, 8.6 us)
Async XLA Ops:
  8.0 56.7 %copy-start = (bf16[2,1536,384]{2,1,0:T(8,128)(2,1)S(1)}, bf16[2,1536,384]{2,1,0:T(8,128)(2,1)}, u32[]{:S(2)}) copy-start(bf16[2,1536,384]{2,1,0:T(8,128)(2,1)} %param.8) | copy-start | bytes 7077892
  15.5 25.5 %all-to-all-start.1 = ((bf16[8,64,384]{2,0,1:T(8,128)(2,1)}), bf16[8,64,384]{2,0,1:T(8,128)(2,1)S(1)}, u32[]{:S(2)}, u32[]{:S(2)}) async-start(bf16[8,64,384]{2,0,1:T(8,128)(2,1)} %copy.27), calls=%async_computation.1 | async-start | bytes 786432 | tf_op jit(solution)/shard_map/all_to_all | solution.py:20
  40.9 18.9 %all-to-all-start = ((bf16[8,64,384]{2,0,1:T(8,128)(2,1)}), bf16[8,64,384]{2,0,1:T(8,128)(2,1)}, u32[]{:S(2)}, u32[]{:S(2)}) async-start(bf16[8,64,384]{2,0,1:T(8,128)(2,1)} %copy.24), calls=%async_computation | async-start | bytes 786432 | tf_op jit(solution)/shard_map/all_to_all | solution.py:21
  45.6 103.3 %reduce-scatter.5.cloned.1.call-start = ((), (), s32[]{:S(2)}) async-start(), calls=%async_computation.7 | async-start | bytes 2654208 | tf_op jit(solution)/shard_map/reduce_scatter | solution.py:49
  64.6 103.9 %reduce-scatter.3.cloned.1.call-start = ((), (), s32[]{:S(2)}) async-start(), calls=%async_computation.6 | async-start | bytes 2654208 | tf_op jit(solution)/shard_map/reduce_scatter | solution.py:46
  68.9 1.2 copy-start.2
  76.9 25.5 %all-to-all-start.3 = ((bf16[256,2,384]{2,1,0:T(2,128)(2,1)}), bf16[256,2,384]{2,1,0:T(2,128)(2,1)S(1)}, u32[]{:S(2)}, u32[]{:S(2)}) async-start(bf16[256,2,384]{2,1,0:T(2,128)(2,1)} %copy.32), calls=%async_computation.3 | async-start | bytes 786432 | tf_op jit(solution)/shard_map/all_to_all | solution.py:37
  102.4 22.2 %all-to-all-start.2 = ((bf16[256,2,384]{2,1,0:T(2,128)(2,1)}), bf16[256,2,384]{2,1,0:T(2,128)(2,1)}, u32[]{:S(2)}, u32[]{:S(2)}) async-start(bf16[256,2,384]{2,1,0:T(2,128)(2,1)} %copy.29), calls=%async_computation.2 | async-start | bytes 786432 | tf_op jit(solution)/shard_map/all_to_all | solution.py:38
  107.0 268.3 %all-reduce.2.cloned.1.call-start = ((), (), s32[]{:S(2)}) async-start(), calls=%async_computation.8 | async-start | bytes 196608 | tf_op jit(solution)/shard_map/psum | solution.py:69
  129.8 1.5 copy-start.1
  137.9 2.5 copy-start.3
Sparse Core Ops, SparseCore 0:
  64.7 53.0 reduce-scatter.4
  120.4 48.0 reduce-scatter.2
Sparse Core Ops, SparseCore 1:
  140.5 234.7 all-reduce.1
where the time goes:
time: 388 us; the launch traced here: 384 us
  waiting for transfers between devices  274 us (71%)
  matrix products  45.7 us (12%)
  starting transfers between devices  26.2 us (7%)
  local copies, waits for them, and re-layouts  17.6 us (5%)
  between operations  15.6 us (4%)
  other arithmetic  4.88 us (1%)
    psum x1, waiting for transfers between devices, on_device(): grad_router = lax.psum(router_term, ('expert', 'dp'))  205 us
    reduce_scatter x1, waiting for transfers between devices, on_device(): lax.psum_scatter(first_term.astype(jnp.bfloat16), 'dp', scatter_dimension...  17.7 us
    all_to_all x1, waiting for transfers between devices, on_device(): lax.all_to_all(outputs_here, 'expert', split_axis=0, concat_axis=1, tiled...  15.3 us
    all_to_all x1, waiting for transfers between devices, on_device(): lax.all_to_all(input_grad_here, 'expert', split_axis=0, concat_axis=1, ti...  14.4 us
    all_to_all x1, waiting for transfers between devices, on_device(): lax.all_to_all(slots, 'expert', split_axis=1, concat_axis=0, tiled=True)  12.1 us
    all_to_all x1, starting transfers between devices, on_device(): lax.all_to_all(slots, 'expert', split_axis=1, concat_axis=0, tiled=True)  10.6 us
    all_to_all x1, waiting for transfers between devices, on_device(): lax.all_to_all(slot_grads, 'expert', split_axis=1, concat_axis=0, tiled=T...  9.78 us
  transfers between devices with their start and end apart: 7, of which 6 were waited for; matrix products, arithmetic and copies ran while one was open for 13% of the time, Pallas kernels for 0%

commit v1 on v0

--- a/solution.py
+++ b/solution.py
@@ -2,6 +2,16 @@
 import jax.numpy as jnp
 from jax import lax
 from jax.sharding import PartitionSpec as P
+
+
+def _sum_everywhere(term, axes):
+    count = 1
+    for name in axes:
+        count *= lax.axis_size(name)
+    pieces = term.reshape(count, term.size // count)
+    mine = jnp.sum(lax.all_to_all(pieces, axes, 0, 0, tiled=True), axis=0, keepdims=True)
+    spread = jnp.broadcast_to(mine, pieces.shape)
+    return lax.all_to_all(spread, axes, 0, 0, tiled=True).reshape(term.shape)
 
 
 def on_device(tokens, router, expert_in, expert_out, out_grad):
@@ -66,7 +76,7 @@
     second_part = jnp.einsum("bps,ds->bpd", logit_low, router, preferred_element_type=jnp.float32)
     grad_tokens = (first_part + second_part).astype(jnp.bfloat16)
     router_term = jnp.einsum("bpd,bps->ds", tokens, logit_low, preferred_element_type=jnp.float32)
-    grad_router = lax.psum(router_term, ("expert", "dp"))
+    grad_router = _sum_everywhere(router_term, ("expert", "dp"))
     return (grad_tokens, grad_in, grad_out, grad_router)
 
 

time: 388 us -> 230 us (0.59)
  waiting for transfers between devices: 274 us -> 56.4 us
  other arithmetic: 4.88 us -> 50.4 us
  starting transfers between devices: 26.2 us -> 45.1 us
  matrix products: 45.7 us -> 36.9 us
  local copies, waits for them, and re-layouts: 17.6 us -> 24.4 us
    psum x1 -> x0, waiting for transfers between devices: 205 us -> none  [on_device(): grad_router = lax.psum(router_term, ('expert', 'dp'))]
    sub x0 -> x1, other arithmetic: none -> 31.9 us  [on_device(): combine = jax.nn.softmax(logits, axis=2)]
    all_to_all x0 -> x2, waiting for transfers between devices: none -> 19.1 us  [the longest x1 9.9 us: _sum_everywhere(): lax.all_to_all(pieces, axes, 0, 0, tiled=True)]
    reduce_scatter x1, waiting for transfers between devices: 17.7 us -> 0.01 us  [on_device(): lax.psum_scatter(first_term.astype(jnp.bfloat16), 'dp', scatter_dimension...]
    all_to_all x0 -> x2, starting transfers between devices: none -> 14.6 us  [the longest x1 8.16 us: _sum_everywhere(): lax.all_to_all(pieces, axes, 0, 0, tiled=True)]
    all_to_all x1, waiting for transfers between devices: 12.1 us -> 0.01 us  [on_device(): lax.all_to_all(slots, 'expert', split_axis=1, concat_axis=0, tiled=True)]
    sub x1, other arithmetic: 0.97 us -> 10.9 us  [on_device(): combine_grad - jnp.sum(combine * combine_grad, axis=2, keepdims=True)]
    all_to_all x1, starting transfers between devices: 4.72 us -> 9.9 us  [on_device(): lax.all_to_all(slot_grads, 'expert', split_axis=1, concat_axis=0, tiled=T...]
  transfers between devices with their start and end apart: 7 -> 8, of which waited for: 6 -> 5; matrix products, arithmetic and copies ran while one was open for 13% -> 38% of each run, Pallas kernels for 0% -> 0%
where the time goes in v1:
time: 230 us; the launch traced here: 228 us
  waiting for transfers between devices  56.4 us (25%)
  other arithmetic  50.4 us (22%)
  starting transfers between devices  45.1 us (20%)
  matrix products  36.9 us (16%)
  local copies, waits for them, and re-layouts  24.4 us (11%)
  between operations  14.3 us (6%)
    sub x1, other arithmetic, on_device(): combine = jax.nn.softmax(logits, axis=2)  31.9 us
    all_to_all x1, waiting for transfers between devices, on_device(): lax.all_to_all(input_grad_here, 'expert', split_axis=0, concat_axis=1, ti...  13.6 us
    all_to_all x1, waiting for transfers between devices, on_device(): lax.all_to_all(slot_grads, 'expert', split_axis=1, concat_axis=0, tiled=T...  12.2 us
    all_to_all x1, waiting for transfers between devices, on_device(): lax.all_to_all(outputs_here, 'expert', split_axis=0, concat_axis=1, tiled...  11.4 us
    sub x1, other arithmetic, on_device(): combine_grad - jnp.sum(combine * combine_grad, axis=2, keepdims=True)  10.9 us
    all_to_all x1, starting transfers between devices, on_device(): lax.all_to_all(slots, 'expert', split_axis=1, concat_axis=0, tiled=True)  10.6 us
    all_to_all x1, waiting for transfers between devices, _sum_everywhere(): lax.all_to_all(pieces, axes, 0, 0, tiled=True)  9.9 us
    all_to_all x1, starting transfers between devices, on_device(): lax.all_to_all(slot_grads, 'expert', split_axis=1, concat_axis=0, tiled=T...  9.9 us
  transfers between devices with their start and end apart: 8, of which 5 were waited for; matrix products, arithmetic and copies ran while one was open for 38% of the time, Pallas kernels for 0%

profile of v1, /device:TPU:32, one launch (start us, length us, event | category | flops | bytes accessed | tf_op | source)
XLA Modules:
  0.0 227.6 jit_solution(2560516155853773533)
XLA Ops:
  7.2 1.9 fusion.43
  12.4 1.9 convolution_convert_fusion.4
  15.3 10.6 %all-to-all-start.1 = ((bf16[8,64,384]{2,0,1:T(8,128)(2,1)}), bf16[8,64,384]{2,0,1:T(8,128)(2,1)S(1)}, u32[]{:S(2)}, u32[]{:S(2)}) async-start(bf16[8,64,384]{2,0,1:T(8,128)(2,1)} %copy.43), calls=%async_computation.1 | async-start | bytes 786432 | tf_op jit(solution)/shard_map/all_to_all | solution.py:30
  25.9 31.9 %fusion.44 = (f32[8,196]{0,1:T(8,128)S(1)}, f32[8,196,64]{2,0,1:T(8,128)S(1)}) fusion(f32[8,196,64]{2,0,1:T(8,128)S(1)} %get-tuple-element.17), kind=kOutput, calls=%fused_computation.64 | output fusion | flops 200767 | bytes 809088 | tf_op jit(solution)/shard_map/sub | solution.py:20
  60.7 9.9 %all-to-all-start = ((bf16[8,64,384]{2,0,1:T(8,128)(2,1)}), bf16[8,64,384]{2,0,1:T(8,128)(2,1)}, u32[]{:S(2)}, u32[]{:S(2)}) async-start(bf16[8,64,384]{2,0,1:T(8,128)(2,1)} %copy.39), calls=%async_computation | async-start | bytes 786432 | tf_op jit(solution)/shard_map/all_to_all | solution.py:31
  70.7 2.6 %convolution_bitcast_fusion = f32[256,2,1536]{2,0,1:T(8,128)} fusion(bf16[2,384,1536]{2,1,0:T(8,128)(2,1)S(1)} %copy-done, bf16[8,32,2,384]{3,0,2,1:T(8,128)(2,1)S(1)} %bitcast.76), kind=kOutput, calls=%fused_computation.6 | convolution fusion | flops 603979776 | bytes 5898240 | tf_op jit(solution)/shard_map/rjd,jdf->rjf/dot_general | solution.py:33
  73.3 12.2 %all-to-all-done = bf16[8,64,384]{2,0,1:T(8,128)(2,1)} async-done(((bf16[8,64,384]{2,0,1:T(8,128)(2,1)}), bf16[8,64,384]{2,0,1:T(8,128)(2,1)}, u32[]{:S(2)}, u32[]{:S(2)}) %all-to-all-start) | async-done | bytes 393248 | tf_op jit(solution)/shard_map/all_to_all | solution.py:31
  85.5 5.2 %fusion.8 = bf16[256,2,1536]{2,0,1:T(8,128)(2,1)S(1)} fusion(f32[256,2,1536]{2,0,1:T(8,128)} %convolution_bitcast_fusion, bf16[2,1536,384]{2,1,0:T(8,128)(2,1)} %param.8, bf16[8,32,2,384]{3,0,2,1:T(8,128)(2,1)} %bitcast.1), kind=kOutput, calls=%fused_computation.14 | convolution fusion | flops 619708416 | bytes 7471104 | tf_op jit(solution)/shard_map/rjd,jfd->rjf/dot_general | solution.py:39
  91.9 2.5 %convolution_convert_fusion.1 = bf16[2,384,1536]{1,2,0:T(8,128)(2,1)} fusion(bf16[256,2,1536]{2,0,1:T(8,128)(2,1)S(1)} %fusion.8, bf16[8,32,2,384]{3,0,2,1:T(8,128)(2,1)S(1)} %bitcast.77), kind=kOutput, calls=%fused_computation.5 | convolution fusion | flops 605159424 | bytes 4325376 | tf_op jit(solution)/shard_map/rjd,rjf->jdf/dot_general | solution.py:50
  94.5 4.8 %convolution_convert_fusion = bf16[2,1536,384]{2,1,0:T(8,128)(2,1)} fusion(bf16[8,32,2,384]{3,0,2,1:T(8,128)(2,1)} %bitcast.1, f32[256,2,1536]{2,0,1:T(8,128)} %convolution_bitcast_fusion), kind=kOutput, calls=%fused_computation.4 | convolution fusion | flops 612237312 | bytes 5898240 | tf_op jit(solution)/shard_map/rjf,rjd->jfd/dot_general | solution.py:53
  99.3 2.4 %fusion.15 = bf16[256,2,384]{2,0,1:T(8,128)(2,1)S(1)} fusion(bf16[256,2,1536]{2,0,1:T(8,128)(2,1)} %copy-done.7, bf16[2,384,1536]{2,1,0:T(8,128)(2,1)S(1)} %copy-done), kind=kOutput, calls=%fused_computation.27 | convolution fusion | flops 604176384 | bytes 4325376 | tf_op jit(solution)/shard_map/rjf,jdf->rjd/dot_general | solution.py:43
  102.8 4.8 %all-to-all-start.2 = ((bf16[256,2,384]{2,1,0:T(2,128)(2,1)}), bf16[256,2,384]{2,1,0:T(2,128)(2,1)S(1)}, u32[]{:S(2)}, u32[]{:S(2)}) async-start(bf16[256,2,384]{2,1,0:T(2,128)(2,1)} %copy.45), calls=%async_computation.2 | async-start | bytes 786432 | tf_op jit(solution)/shard_map/all_to_all | solution.py:48
  107.6 3.9 %fusion.16 = bf16[256,2,384]{2,0,1:T(8,128)(2,1)S(1)} fusion(bf16[2,1536,384]{2,1,0:T(8,128)(2,1)} %param.8, f32[256,2,1536]{2,0,1:T(8,128)} %convolution_bitcast_fusion), kind=kOutput, calls=%fused_computation.28 | convolution fusion | flops 611254272 | bytes 5898240 | tf_op jit(solution)/shard_map/rjf,jfd->rjd/dot_general | solution.py:36
  112.7 13.6 %all-to-all-done.2 = bf16[256,2,384]{2,1,0:T(2,128)(2,1)S(1)} async-done(((bf16[256,2,384]{2,1,0:T(2,128)(2,1)}), bf16[256,2,384]{2,1,0:T(2,128)(2,1)S(1)}, u32[]{:S(2)}, u32[]{:S(2)}) %all-to-all-start.2) | async-done | bytes 393248 | tf_op jit(solution)/shard_map/all_to_all | solution.py:48
  126.3 5.2 %all-to-all-start.3 = ((bf16[256,2,384]{2,1,0:T(2,128)(2,1)}), bf16[256,2,384]{2,1,0:T(2,128)(2,1)}, u32[]{:S(2)}, u32[]{:S(2)}) async-start(bf16[256,2,384]{2,1,0:T(2,128)(2,1)} %copy.50), calls=%async_computation.3 | async-start | bytes 786432 | tf_op jit(solution)/shard_map/all_to_all | solution.py:47
  133.7 2.7 %fusion.17 = f32[8,64,196]{2,1,0:T(8,128)} fusion(bf16[8,64,384]{2,1,0:T(8,128)(2,1)S(1)} %all_to_all.73, bf16[8,196,384]{2,0,1:T(8,128)(2,1)} %param.5), kind=kOutput, calls=%fused_computation.30 | convolution fusion | flops 77070336 | bytes 1998848 | tf_op jit(solution)/shard_map/bpd,bsd->bps/dot_general | solution.py:63
  136.5 2.4 %copy.49 = f32[8,64,196]{1,0,2:T(8,128)} copy(f32[8,64,196]{2,1,0:T(8,128)} %fusion.17) | data formatting | bytes 802816 | tf_op jit(solution)/shard_map/bpd,bsd->bps/dot_general | solution.py:63
  138.8 11.4 %all-to-all-done.3 = bf16[256,2,384]{2,1,0:T(2,128)(2,1)} async-done(((bf16[256,2,384]{2,1,0:T(2,128)(2,1)}), bf16[256,2,384]{2,1,0:T(2,128)(2,1)}, u32[]{:S(2)}, u32[]{:S(2)}) %all-to-all-start.3) | async-done | bytes 393248 | tf_op jit(solution)/shard_map/all_to_all | solution.py:47
  150.2 2.0 copy.97
  152.2 1.9 all_to_all.77
  154.1 2.8 %fusion.20 = f32[8,64,196]{2,1,0:T(8,128)} fusion(bf16[8,64,384]{2,1,0:T(8,128)(2,1)} %all_to_all.77, bf16[8,196,384]{2,0,1:T(8,128)(2,1)} %param.9), kind=kOutput, calls=%fused_computation.33 | convolution fusion | flops 77070336 | bytes 1998848 | tf_op jit(solution)/shard_map/bpd,bsd->bps/dot_general | solution.py:62
  157.0 2.3 %copy.53 = f32[8,64,196]{1,0,2:T(8,128)} copy(f32[8,64,196]{2,1,0:T(8,128)} %fusion.20) | data formatting | bytes 802816 | tf_op jit(solution)/shard_map/bpd,bsd->bps/dot_general | solution.py:62
  159.3 1.4 fusion.24
  160.6 10.9 %fusion.14 = bf16[8,196,64]{2,0,1:T(8,128)(2,1)S(1)} fusion(f32[8,64,196]{1,0,2:T(8,128)} %copy.53, f32[8,64,196]{1,0,2:T(8,128)} %copy.49, f32[8,64]{1,0:T(8,128)S(1)} %fusion.24, f32[8,196,64]{2,0,1:T(8,128)} %copy-done.3, f32[8,196]{0,1:T(8,128)} %copy-done.8, f32[8,64]{1,0:T(8,128)} %copy-done.11, f32[8,196,64]{2,0,1:T(8,128)S(1)} %get-tuple-element.17, ...), kind=kOutput, calls=%fused_computation.22 | output fusion | flops 1105503 | bytes 1818752 | tf_op jit(solution)/shard_map/sub | solution.py:70
  173.6 8.2 %all-to-all-start.4 = ((f32[256,1,96]{2,1,0:T(1,128)}), f32[256,1,96]{2,1,0:T(1,128)S(1)}, u32[]{:S(2)}, u32[]{:S(2)}) async-start(f32[256,1,96]{2,1,0:T(1,128)} %bitcast.21), calls=%async_computation.6 | async-start | bytes 262144 | tf_op jit(solution)/shard_map/all_to_all | solution.py:12
  181.7 3.0 %fusion.45 = f32[8,196,384]{2,1,0:T(8,128)} fusion(bf16[8,196,64]{1,2,0:T(8,128)(2,1)} %copy-done.4, bf16[8,64,384]{2,1,0:T(8,128)(2,1)S(1)} %all_to_all.73), kind=kOutput, calls=%fused_computation.65 | convolution fusion | flops 77070336 | bytes 3002368 | tf_op jit(solution)/shard_map/bps,bsd->bpd/dot_general | solution.py:73
  184.8 9.9 %all-to-all-done.4 = f32[256,1,96]{2,1,0:T(1,128)S(1)} async-done(((f32[256,1,96]{2,1,0:T(1,128)}), f32[256,1,96]{2,1,0:T(1,128)S(1)}, u32[]{:S(2)}, u32[]{:S(2)}) %all-to-all-start.4) | async-done | bytes 98336 | tf_op jit(solution)/shard_map/all_to_all | solution.py:12
  195.7 6.4 %all-to-all-start.5 = ((f32[256,1,96]{2,1,0:T(1,128)}), f32[256,1,96]{2,1,0:T(1,128)S(1)}, u32[]{:S(2)}, u32[]{:S(2)}) async-start(f32[256,1,96]{2,1,0:T(1,128)} %broadcast_in_dim.2), calls=%async_computation.7 | async-start | bytes 262144 | tf_op jit(solution)/shard_map/all_to_all | solution.py:14
  202.1 2.3 add_convert_fusion
  205.6 9.2 %all-to-all-done.5 = f32[256,1,96]{2,1,0:T(1,128)S(1)} async-done(((f32[256,1,96]{2,1,0:T(1,128)}), f32[256,1,96]{2,1,0:T(1,128)S(1)}, u32[]{:S(2)}, u32[]{:S(2)}) %all-to-all-start.5) | async-done | bytes 98336 | tf_op jit(solution)/shard_map/all_to_all | solution.py:14
  217.1 1.8 convert_element_type.61
  219.0 1.8 convert_element_type.63
  (52 shorter events, 19.5 us)
Async XLA Ops:
  7.2 63.5 %copy-start = (bf16[2,384,1536]{2,1,0:T(8,128)(2,1)S(1)}, bf16[2,384,1536]{2,1,0:T(8,128)(2,1)}, u32[]{:S(2)}) copy-start(bf16[2,384,1536]{2,1,0:T(8,128)(2,1)} %param.7) | copy-start | bytes 7077892
  9.1 0.6 copy-start.10
  9.7 0.6 copy-start.11
  12.4 2.9 %copy-start.4 = (bf16[8,196,64]{1,2,0:T(8,128)(2,1)}, bf16[8,196,64]{1,2,0:T(8,128)(2,1)S(1)}, u32[]{:S(2)}) copy-start(bf16[8,196,64]{1,2,0:T(8,128)(2,1)S(1)} %copy.47) | copy-start | bytes 602116
  15.3 45.4 %all-to-all-start.1 = ((bf16[8,64,384]{2,0,1:T(8,128)(2,1)}), bf16[8,64,384]{2,0,1:T(8,128)(2,1)S(1)}, u32[]{:S(2)}, u32[]{:S(2)}) async-start(bf16[8,64,384]{2,0,1:T(8,128)(2,1)} %copy.43), calls=%async_computation.1 | async-start | bytes 786432 | tf_op jit(solution)/shard_map/all_to_all | solution.py:30
  25.9 33.3 %copy-start.2 = (bf16[8,196,384]{2,0,1:T(8,128)(2,1)S(1)}, bf16[8,196,384]{2,0,1:T(8,128)(2,1)}, u32[]{:S(2)}) copy-start(bf16[8,196,384]{2,0,1:T(8,128)(2,1)} %param.9) | copy-start | bytes 3612676
  57.9 1.0 copy-start.3
  57.9 1.0 copy-start.8
  60.7 24.8 %all-to-all-start = ((bf16[8,64,384]{2,0,1:T(8,128)(2,1)}), bf16[8,64,384]{2,0,1:T(8,128)(2,1)}, u32[]{:S(2)}, u32[]{:S(2)}) async-start(bf16[8,64,384]{2,0,1:T(8,128)(2,1)} %copy.39), calls=%async_computation | async-start | bytes 786432 | tf_op jit(solution)/shard_map/all_to_all | solution.py:31
  70.6 146.5 %reduce-scatter.3.cloned.1.call-start = ((), (), s32[]{:S(2)}) async-start(), calls=%async_computation.8 | async-start | bytes 2654208 | tf_op jit(solution)/shard_map/reduce_scatter | solution.py:56
  90.7 1.2 copy-start.7
  94.4 124.5 %reduce-scatter.5.cloned.1.call-start = ((), (), s32[]{:S(2)}) async-start(), calls=%async_computation.9 | async-start | bytes 2654208 | tf_op jit(solution)/shard_map/reduce_scatter | solution.py:59
  102.8 23.5 %all-to-all-start.2 = ((bf16[256,2,384]{2,1,0:T(2,128)(2,1)}), bf16[256,2,384]{2,1,0:T(2,128)(2,1)S(1)}, u32[]{:S(2)}, u32[]{:S(2)}) async-start(bf16[256,2,384]{2,1,0:T(2,128)(2,1)} %copy.45), calls=%async_computation.2 | async-start | bytes 786432 | tf_op jit(solution)/shard_map/all_to_all | solution.py:48
  126.3 23.9 %all-to-all-start.3 = ((bf16[256,2,384]{2,1,0:T(2,128)(2,1)}), bf16[256,2,384]{2,1,0:T(2,128)(2,1)}, u32[]{:S(2)}, u32[]{:S(2)}) async-start(bf16[256,2,384]{2,1,0:T(2,128)(2,1)} %copy.50), calls=%async_computation.3 | async-start | bytes 786432 | tf_op jit(solution)/shard_map/all_to_all | solution.py:47
  160.6 11.6 %copy-start.1 = (bf16[8,196,384]{2,0,1:T(8,128)(2,1)S(1)}, bf16[8,196,384]{2,0,1:T(8,128)(2,1)}, u32[]{:S(2)}) copy-start(bf16[8,196,384]{2,0,1:T(8,128)(2,1)} %param.5) | copy-start | bytes 3612676
  171.5 0.8 copy-start.5
  172.3 29.8 %copy-start.9 = (bf16[384,64]{0,1:T(8,128)(2,1)S(1)}, bf16[384,64]{0,1:T(8,128)(2,1)}, u32[]{:S(2)}) copy-start(bf16[384,64]{0,1:T(8,128)(2,1)} %param.6) | copy-start | bytes 147460
  172.6 29.5 %copy-start.6 = (bf16[8,196,64]{2,0,1:T(8,128)(2,1)S(1)}, bf16[8,196,64]{2,0,1:T(8,128)(2,1)}, u32[]{:S(2)}) copy-start(bf16[8,196,64]{2,0,1:T(8,128)(2,1)} %copy-done.5) | copy-start | bytes 602116
  173.6 21.1 %all-to-all-start.4 = ((f32[256,1,96]{2,1,0:T(1,128)}), f32[256,1,96]{2,1,0:T(1,128)S(1)}, u32[]{:S(2)}, u32[]{:S(2)}) async-start(f32[256,1,96]{2,1,0:T(1,128)} %bitcast.21), calls=%async_computation.6 | async-start | bytes 262144 | tf_op jit(solution)/shard_map/all_to_all | solution.py:12
  195.7 19.1 %all-to-all-start.5 = ((f32[256,1,96]{2,1,0:T(1,128)}), f32[256,1,96]{2,1,0:T(1,128)S(1)}, u32[]{:S(2)}, u32[]{:S(2)}) async-start(f32[256,1,96]{2,1,0:T(1,128)} %broadcast_in_dim.2), calls=%async_computation.7 | async-start | bytes 262144 | tf_op jit(solution)/shard_map/all_to_all | solution.py:14
Sparse Core Ops, SparseCore 0:
  94.6 54.2 reduce-scatter.2
  151.5 46.7 reduce-scatter.4

commit v2 on v1

--- a/solution.py
+++ b/solution.py
@@ -14,10 +14,20 @@
     return lax.all_to_all(spread, axes, 0, 0, tiled=True).reshape(term.shape)
 
 
+def _reduced(value):
+    return lax.optimization_barrier(value)
+
+
+def _softmax(logits, axis):
+    top = _reduced(jnp.max(logits, axis=axis, keepdims=True))
+    raised = jnp.exp(logits - top)
+    return raised / _reduced(jnp.sum(raised, axis=axis, keepdims=True))
+
+
 def on_device(tokens, router, expert_in, expert_out, out_grad):
     logits = jnp.einsum("bpd,ds->bps", tokens, router, preferred_element_type=jnp.float32)
-    dispatch = jax.nn.softmax(logits, axis=1)
-    combine = jax.nn.softmax(logits, axis=2)
+    dispatch = _softmax(logits, 1)
+    combine = _softmax(logits, 2)
     dispatch_low = dispatch.astype(jnp.bfloat16)
     combine_low = combine.astype(jnp.bfloat16)
     slots = jnp.einsum(
@@ -64,10 +74,10 @@
         "bpd,bsd->bps", tokens, inputs_grad, preferred_element_type=jnp.float32
     )
     logit_grad = dispatch * (
-        dispatch_grad - jnp.sum(dispatch * dispatch_grad, axis=1, keepdims=True)
+        dispatch_grad - _reduced(jnp.sum(dispatch * dispatch_grad, axis=1, keepdims=True))
     )
     logit_grad = logit_grad + combine * (
-        combine_grad - jnp.sum(combine * combine_grad, axis=2, keepdims=True)
+        combine_grad - _reduced(jnp.sum(combine * combine_grad, axis=2, keepdims=True))
     )
     logit_low = logit_grad.astype(jnp.bfloat16)
     first_part = jnp.einsum(

time: 230 us -> 198 us (0.86)
  other arithmetic: 50.4 us -> 11.1 us
  waiting for transfers between devices: 56.4 us -> 68.3 us
  starting transfers between devices: 45.1 us -> 40.7 us
    sub x2 -> x0, other arithmetic: 42.8 us -> none  [the longest x1 31.9 us: on_device(): combine = jax.nn.softmax(logits, axis=2)]
    all_to_all x1, waiting for transfers between devices: 0.01 us -> 11.9 us  [on_device(): lax.all_to_all(slots, 'expert', split_axis=1, concat_axis=0, tiled=True)]
    all_to_all x1, starting transfers between devices: 9.9 us -> 4.71 us  [on_device(): lax.all_to_all(slot_grads, 'expert', split_axis=1, concat_axis=0, tiled=T...]
  transfers between devices with their start and end apart: 8 -> 8, of which waited for: 5 -> 6; matrix products, arithmetic and copies ran while one was open for 38% -> 25% of each run, Pallas kernels for 0% -> 0%
where the time goes in v2:
time: 198 us; the launch traced here: 195 us
  waiting for transfers between devices  68.3 us (34%)
  starting transfers between devices  40.7 us (21%)
  matrix products  38.4 us (19%)
  local copies, waits for them, and re-layouts  22.5 us (11%)
  between operations  14.3 us (7%)
  other arithmetic  11.1 us (6%)
    all_to_all x1, waiting for transfers between devices, on_device(): lax.all_to_all(input_grad_here, 'expert', split_axis=0, concat_axis=1, ti...  13.6 us
    all_to_all x1, waiting for transfers between devices, on_device(): lax.all_to_all(slot_grads, 'expert', split_axis=1, concat_axis=0, tiled=T...  12.3 us
    all_to_all x1, waiting for transfers between devices, on_device(): lax.all_to_all(slots, 'expert', split_axis=1, concat_axis=0, tiled=True)  11.9 us
    all_to_all x1, waiting for transfers between devices, on_device(): lax.all_to_all(outputs_here, 'expert', split_axis=0, concat_axis=1, tiled...  11.3 us
    all_to_all x1, starting transfers between devices, on_device(): lax.all_to_all(slots, 'expert', split_axis=1, concat_axis=0, tiled=True)  10.6 us
    all_to_all x1, waiting for transfers between devices, _sum_everywhere(): lax.all_to_all(pieces, axes, 0, 0, tiled=True)  9.99 us
    all_to_all x1, waiting for transfers between devices, _sum_everywhere(): return lax.all_to_all(spread, axes, 0, 0, tiled=True).reshape(term.shape)  9.16 us
    all_to_all x1, starting transfers between devices, _sum_everywhere(): lax.all_to_all(pieces, axes, 0, 0, tiled=True)  8.62 us
  transfers between devices with their start and end apart: 8, of which 6 were waited for; matrix products, arithmetic and copies ran while one was open for 25% of the time, Pallas kernels for 0%

profile of v2, /device:TPU:32, one launch (start us, length us, event | category | flops | bytes accessed | tf_op | source)
XLA Modules:
  0.0 195.4 jit_solution(1661859732492848365)
XLA Ops:
  7.2 2.0 %fusion.40 = (f32[8,196]{0,1:T(8,128)S(1)}, f32[8,64]{1,0:T(8,128)S(1)}, f32[8,196,64]{2,0,1:T(8,128)S(1)}) fusion(bf16[8,196,384]{2,0,1:T(8,128)(2,1)} %param.5, bf16[384,64]{0,1:T(8,128)(2,1)} %param.6), kind=kOutput, calls=%fused_computation.61 | convolution fusion | flops 77268960 | bytes 1663104 | tf_op jit(solution)/shard_map/bpd,ds->bps/dot_general | solution.py:28
  12.4 1.9 convolution_convert_fusion.4
  15.3 10.6 %all-to-all-start.1 = ((bf16[8,64,384]{2,0,1:T(8,128)(2,1)}), bf16[8,64,384]{2,0,1:T(8,128)(2,1)S(1)}, u32[]{:S(2)}, u32[]{:S(2)}) async-start(bf16[8,64,384]{2,0,1:T(8,128)(2,1)} %copy.43), calls=%async_computation.1 | async-start | bytes 786432 | tf_op jit(solution)/shard_map/all_to_all | solution.py:40
  25.9 2.0 %convolution_convert_fusion.5 = bf16[8,64,384]{2,1,0:T(8,128)(2,1)S(1)} fusion(bf16[8,196,384]{2,0,1:T(8,128)(2,1)} %param.9, bf16[8,196,64]{2,0,1:T(8,128)(2,1)} %get-tuple-element.22), kind=kOutput, calls=%fused_computation.18 | convolution fusion | flops 77266944 | bytes 1798144 | tf_op jit(solution)/shard_map/bps,bpd->bsd/dot_general | solution.py:36
  28.9 11.9 %all-to-all-done.1 = bf16[8,64,384]{2,0,1:T(8,128)(2,1)S(1)} async-done(((bf16[8,64,384]{2,0,1:T(8,128)(2,1)}), bf16[8,64,384]{2,0,1:T(8,128)(2,1)S(1)}, u32[]{:S(2)}, u32[]{:S(2)}) %all-to-all-start.1) | async-done | bytes 393248 | tf_op jit(solution)/shard_map/all_to_all | solution.py:40
  40.8 4.7 %all-to-all-start = ((bf16[8,64,384]{2,0,1:T(8,128)(2,1)}), bf16[8,64,384]{2,0,1:T(8,128)(2,1)}, u32[]{:S(2)}, u32[]{:S(2)}) async-start(bf16[8,64,384]{2,0,1:T(8,128)(2,1)} %copy.39), calls=%async_computation | async-start | bytes 786432 | tf_op jit(solution)/shard_map/all_to_all | solution.py:41
  45.6 2.6 %convolution_bitcast_fusion = f32[256,2,1536]{2,0,1:T(8,128)} fusion(bf16[2,384,1536]{2,1,0:T(8,128)(2,1)S(1)} %copy-done, bf16[8,32,2,384]{3,0,2,1:T(8,128)(2,1)S(1)} %bitcast.92), kind=kOutput, calls=%fused_computation.4 | convolution fusion | flops 603979776 | bytes 5898240 | tf_op jit(solution)/shard_map/rjd,jdf->rjf/dot_general | solution.py:43
  48.2 12.3 %all-to-all-done = bf16[8,64,384]{2,0,1:T(8,128)(2,1)} async-done(((bf16[8,64,384]{2,0,1:T(8,128)(2,1)}), bf16[8,64,384]{2,0,1:T(8,128)(2,1)}, u32[]{:S(2)}, u32[]{:S(2)}) %all-to-all-start) | async-done | bytes 393248 | tf_op jit(solution)/shard_map/all_to_all | solution.py:41
  60.5 5.2 %fusion.6 = bf16[256,2,1536]{2,0,1:T(8,128)(2,1)S(1)} fusion(f32[256,2,1536]{2,0,1:T(8,128)} %convolution_bitcast_fusion, bf16[2,1536,384]{2,1,0:T(8,128)(2,1)} %param.8, bf16[8,32,2,384]{3,0,2,1:T(8,128)(2,1)} %bitcast.9), kind=kOutput, calls=%fused_computation.12 | convolution fusion | flops 619708416 | bytes 7471104 | tf_op jit(solution)/shard_map/rjd,jfd->rjf/dot_general | solution.py:49
  66.9 2.5 %convolution_convert_fusion.1 = bf16[2,384,1536]{1,2,0:T(8,128)(2,1)} fusion(bf16[256,2,1536]{2,0,1:T(8,128)(2,1)S(1)} %fusion.6, bf16[8,32,2,384]{3,0,2,1:T(8,128)(2,1)S(1)} %bitcast.93), kind=kOutput, calls=%fused_computation.3 | convolution fusion | flops 605159424 | bytes 4325376 | tf_op jit(solution)/shard_map/rjd,rjf->jdf/dot_general | solution.py:60
  69.5 4.8 %convolution_convert_fusion = bf16[2,1536,384]{2,1,0:T(8,128)(2,1)} fusion(bf16[8,32,2,384]{3,0,2,1:T(8,128)(2,1)} %bitcast.9, f32[256,2,1536]{2,0,1:T(8,128)} %convolution_bitcast_fusion), kind=kOutput, calls=%fused_computation.2 | convolution fusion | flops 612237312 | bytes 5898240 | tf_op jit(solution)/shard_map/rjf,rjd->jfd/dot_general | solution.py:63
  74.3 2.4 %fusion.7 = bf16[256,2,384]{2,0,1:T(8,128)(2,1)S(1)} fusion(bf16[256,2,1536]{2,0,1:T(8,128)(2,1)} %copy-done.8, bf16[2,384,1536]{2,1,0:T(8,128)(2,1)S(1)} %copy-done), kind=kOutput, calls=%fused_computation.19 | convolution fusion | flops 604176384 | bytes 4325376 | tf_op jit(solution)/shard_map/rjf,jdf->rjd/dot_general | solution.py:53
  77.8 4.7 %all-to-all-start.2 = ((bf16[256,2,384]{2,1,0:T(2,128)(2,1)}), bf16[256,2,384]{2,1,0:T(2,128)(2,1)S(1)}, u32[]{:S(2)}, u32[]{:S(2)}) async-start(bf16[256,2,384]{2,1,0:T(2,128)(2,1)} %copy.45), calls=%async_computation.2 | async-start | bytes 786432 | tf_op jit(solution)/shard_map/all_to_all | solution.py:58
  82.5 3.9 %fusion.8 = bf16[256,2,384]{2,0,1:T(8,128)(2,1)S(1)} fusion(bf16[2,1536,384]{2,1,0:T(8,128)(2,1)} %param.8, f32[256,2,1536]{2,0,1:T(8,128)} %convolution_bitcast_fusion), kind=kOutput, calls=%fused_computation.20 | convolution fusion | flops 611254272 | bytes 5898240 | tf_op jit(solution)/shard_map/rjf,jfd->rjd/dot_general | solution.py:46
  87.6 13.6 %all-to-all-done.2 = bf16[256,2,384]{2,1,0:T(2,128)(2,1)S(1)} async-done(((bf16[256,2,384]{2,1,0:T(2,128)(2,1)}), bf16[256,2,384]{2,1,0:T(2,128)(2,1)S(1)}, u32[]{:S(2)}, u32[]{:S(2)}) %all-to-all-start.2) | async-done | bytes 393248 | tf_op jit(solution)/shard_map/all_to_all | solution.py:58
  101.2 5.3 %all-to-all-start.3 = ((bf16[256,2,384]{2,1,0:T(2,128)(2,1)}), bf16[256,2,384]{2,1,0:T(2,128)(2,1)}, u32[]{:S(2)}, u32[]{:S(2)}) async-start(bf16[256,2,384]{2,1,0:T(2,128)(2,1)} %copy.50), calls=%async_computation.3 | async-start | bytes 786432 | tf_op jit(solution)/shard_map/all_to_all | solution.py:57
  108.7 2.7 %fusion.9 = f32[8,64,196]{2,1,0:T(8,128)} fusion(bf16[8,64,384]{2,1,0:T(8,128)(2,1)S(1)} %all_to_all.73, bf16[8,196,384]{2,0,1:T(8,128)(2,1)} %param.5), kind=kOutput, calls=%fused_computation.22 | convolution fusion | flops 77070336 | bytes 1998848 | tf_op jit(solution)/shard_map/bpd,bsd->bps/dot_general | solution.py:73
  111.4 2.3 %copy.49 = f32[8,64,196]{1,0,2:T(8,128)} copy(f32[8,64,196]{2,1,0:T(8,128)} %fusion.9) | data formatting | bytes 802816 | tf_op jit(solution)/shard_map/bpd,bsd->bps/dot_general | solution.py:73
  113.7 11.3 %all-to-all-done.3 = bf16[256,2,384]{2,1,0:T(2,128)(2,1)} async-done(((bf16[256,2,384]{2,1,0:T(2,128)(2,1)}), bf16[256,2,384]{2,1,0:T(2,128)(2,1)}, u32[]{:S(2)}, u32[]{:S(2)}) %all-to-all-start.3) | async-done | bytes 393248 | tf_op jit(solution)/shard_map/all_to_all | solution.py:57
  125.0 2.0 %copy.97 = bf16[32,8,2,384]{3,2,0,1:T(2,128)(2,1)} copy(bf16[32,8,2,384]{3,2,1,0:T(2,128)(2,1)} %bitcast.24) | data formatting | bytes 786432 | tf_op jit(solution)/shard_map/all_to_all | solution.py:57
  127.0 1.9 all_to_all.77
  128.9 2.8 %fusion.12 = f32[8,64,196]{2,1,0:T(8,128)} fusion(bf16[8,64,384]{2,1,0:T(8,128)(2,1)} %all_to_all.77, bf16[8,196,384]{2,0,1:T(8,128)(2,1)} %param.9), kind=kOutput, calls=%fused_computation.25 | convolution fusion | flops 77070336 | bytes 1998848 | tf_op jit(solution)/shard_map/bpd,bsd->bps/dot_general | solution.py:72
  131.7 2.3 %copy.53 = f32[8,64,196]{1,0,2:T(8,128)} copy(f32[8,64,196]{2,1,0:T(8,128)} %fusion.12) | data formatting | bytes 802816 | tf_op jit(solution)/shard_map/bpd,bsd->bps/dot_general | solution.py:72
  134.0 2.3 %fusion.19 = (f32[8,64]{1,0:T(8,128)S(1)}, f32[8,196]{0,1:T(8,128)S(1)}) fusion(f32[8,64,196]{1,0,2:T(8,128)} %copy.49, f32[8,64]{1,0:T(8,128)} %copy-done.11, f32[8,196,64]{2,0,1:T(8,128)S(1)} %get-tuple-element.24, f32[8,64]{1,0:T(8,128)} %copy-done.10, f32[8,64,196]{1,0,2:T(8,128)} %copy.53, f32[8,196]{0,1:T(8,128)} %copy-done.7, f32[8,196]{0,1:T(8,128)} %copy-done.5), kind=kLoop, calls=%fused_computation.36 | loop fusion | flops 800736 | bytes 1229184 | tf_op jit(solution)/shard_map/reduce_sum | solution.py:77
  136.3 2.1 %fusion.18 = bf16[8,196,64]{2,0,1:T(8,128)(2,1)S(1)} fusion(f32[8,64,196]{1,0,2:T(8,128)} %copy.53, f32[8,64,196]{1,0,2:T(8,128)S(1)} %copy-done.2, f32[8,196]{0,1:T(8,128)S(1)} %get-tuple-element.17, f32[8,64]{1,0:T(8,128)S(1)} %get-tuple-element.16, f32[8,64]{1,0:T(8,128)} %copy-done.11, f32[8,196,64]{2,0,1:T(8,128)S(1)} %get-tuple-element.24, ...), kind=kLoop, calls=%fused_computation.33 | loop fusion | flops 1003520 | bytes 1429888 | tf_op jit(solution)/shard_map/convert_element_type | solution.py:82
  140.5 8.6 %all-to-all-start.4 = ((f32[256,1,96]{2,1,0:T(1,128)}), f32[256,1,96]{2,1,0:T(1,128)S(1)}, u32[]{:S(2)}, u32[]{:S(2)}) async-start(f32[256,1,96]{2,1,0:T(1,128)} %bitcast.33), calls=%async_computation.6 | async-start | bytes 262144 | tf_op jit(solution)/shard_map/all_to_all | solution.py:12
  149.1 3.0 %fusion.41 = f32[8,196,384]{2,1,0:T(8,128)} fusion(bf16[8,196,64]{1,2,0:T(8,128)(2,1)} %copy-done.6, bf16[8,64,384]{2,1,0:T(8,128)(2,1)S(1)} %all_to_all.73), kind=kOutput, calls=%fused_computation.62 | convolution fusion | flops 77070336 | bytes 3002368 | tf_op jit(solution)/shard_map/bps,bsd->bpd/dot_general | solution.py:83
  152.2 10.0 %all-to-all-done.4 = f32[256,1,96]{2,1,0:T(1,128)S(1)} async-done(((f32[256,1,96]{2,1,0:T(1,128)}), f32[256,1,96]{2,1,0:T(1,128)S(1)}, u32[]{:S(2)}, u32[]{:S(2)}) %all-to-all-start.4) | async-done | bytes 98336 | tf_op jit(solution)/shard_map/all_to_all | solution.py:12
  163.2 6.7 %all-to-all-start.5 = ((f32[256,1,96]{2,1,0:T(1,128)}), f32[256,1,96]{2,1,0:T(1,128)S(1)}, u32[]{:S(2)}, u32[]{:S(2)}) async-start(f32[256,1,96]{2,1,0:T(1,128)} %broadcast_in_dim.30), calls=%async_computation.7 | async-start | bytes 262144 | tf_op jit(solution)/shard_map/all_to_all | solution.py:14
  169.9 2.3 %add_convert_fusion = bf16[8,196,384]{2,1,0:T(8,128)(2,1)S(1)} fusion(f32[8,196,384]{2,1,0:T(8,128)} %fusion.41, bf16[8,196,64]{2,0,1:T(8,128)(2,1)S(1)} %copy-done.4, bf16[384,64]{0,1:T(8,128)(2,1)S(1)} %copy-done.9), kind=kOutput, calls=%fused_computation.14 | convolution fusion | flops 78274560 | bytes 3862528 | tf_op jit(solution)/shard_map/bps,ds->bpd/dot_general | solution.py:86
  173.4 9.2 %all-to-all-done.5 = f32[256,1,96]{2,1,0:T(1,128)S(1)} async-done(((f32[256,1,96]{2,1,0:T(1,128)}), f32[256,1,96]{2,1,0:T(1,128)S(1)}, u32[]{:S(2)}, u32[]{:S(2)}) %all-to-all-start.5) | async-done | bytes 98336 | tf_op jit(solution)/shard_map/all_to_all | solution.py:14
  184.9 1.8 convert_element_type.61
  (50 shorter events, 19.4 us)
Async XLA Ops:
  7.2 38.4 %copy-start = (bf16[2,384,1536]{2,1,0:T(8,128)(2,1)S(1)}, bf16[2,384,1536]{2,1,0:T(8,128)(2,1)}, u32[]{:S(2)}) copy-start(bf16[2,384,1536]{2,1,0:T(8,128)(2,1)} %param.7) | copy-start | bytes 7077892
  9.2 0.6 copy-start.5
  9.2 2.0 %copy-start.10 = (f32[8,64]{1,0:T(8,128)}, f32[8,64]{1,0:T(8,128)S(1)}, u32[]{:S(2)}) copy-start(f32[8,64]{1,0:T(8,128)S(1)} %get-tuple-element.21) | copy-start | bytes 6148
  9.7 1.4 copy-start.7
  9.7 1.4 copy-start.11
  12.4 2.9 %copy-start.6 = (bf16[8,196,64]{1,2,0:T(8,128)(2,1)}, bf16[8,196,64]{1,2,0:T(8,128)(2,1)S(1)}, u32[]{:S(2)}) copy-start(bf16[8,196,64]{1,2,0:T(8,128)(2,1)S(1)} %copy.47) | copy-start | bytes 602116
  15.3 25.5 %all-to-all-start.1 = ((bf16[8,64,384]{2,0,1:T(8,128)(2,1)}), bf16[8,64,384]{2,0,1:T(8,128)(2,1)S(1)}, u32[]{:S(2)}, u32[]{:S(2)}) async-start(bf16[8,64,384]{2,0,1:T(8,128)(2,1)} %copy.43), calls=%async_computation.1 | async-start | bytes 786432 | tf_op jit(solution)/shard_map/all_to_all | solution.py:40
  40.8 19.7 %all-to-all-start = ((bf16[8,64,384]{2,0,1:T(8,128)(2,1)}), bf16[8,64,384]{2,0,1:T(8,128)(2,1)}, u32[]{:S(2)}, u32[]{:S(2)}) async-start(bf16[8,64,384]{2,0,1:T(8,128)(2,1)} %copy.39), calls=%async_computation | async-start | bytes 786432 | tf_op jit(solution)/shard_map/all_to_all | solution.py:41
  45.5 139.4 %reduce-scatter.3.cloned.1.call-start = ((), (), s32[]{:S(2)}) async-start(), calls=%async_computation.8 | async-start | bytes 2654208 | tf_op jit(solution)/shard_map/reduce_scatter | solution.py:66
  65.7 1.2 copy-start.8
  69.4 117.3 %reduce-scatter.5.cloned.1.call-start = ((), (), s32[]{:S(2)}) async-start(), calls=%async_computation.9 | async-start | bytes 2654208 | tf_op jit(solution)/shard_map/reduce_scatter | solution.py:69
  77.8 23.4 %all-to-all-start.2 = ((bf16[256,2,384]{2,1,0:T(2,128)(2,1)}), bf16[256,2,384]{2,1,0:T(2,128)(2,1)S(1)}, u32[]{:S(2)}, u32[]{:S(2)}) async-start(bf16[256,2,384]{2,1,0:T(2,128)(2,1)} %copy.45), calls=%async_computation.2 | async-start | bytes 786432 | tf_op jit(solution)/shard_map/all_to_all | solution.py:58
  101.2 23.8 %all-to-all-start.3 = ((bf16[256,2,384]{2,1,0:T(2,128)(2,1)}), bf16[256,2,384]{2,1,0:T(2,128)(2,1)}, u32[]{:S(2)}, u32[]{:S(2)}) async-start(bf16[256,2,384]{2,1,0:T(2,128)(2,1)} %copy.50), calls=%async_computation.3 | async-start | bytes 786432 | tf_op jit(solution)/shard_map/all_to_all | solution.py:57
  134.0 2.3 %copy-start.2 = (f32[8,64,196]{1,0,2:T(8,128)S(1)}, f32[8,64,196]{1,0,2:T(8,128)}, u32[]{:S(2)}) copy-start(f32[8,64,196]{1,0,2:T(8,128)} %copy.49) | copy-start | bytes 1204228
  134.0 5.2 %copy-start.1 = (bf16[8,196,384]{2,0,1:T(8,128)(2,1)S(1)}, bf16[8,196,384]{2,0,1:T(8,128)(2,1)}, u32[]{:S(2)}) copy-start(bf16[8,196,384]{2,0,1:T(8,128)(2,1)} %param.5) | copy-start | bytes 3612676
  138.5 0.8 copy-start.3
  139.2 30.7 %copy-start.9 = (bf16[384,64]{0,1:T(8,128)(2,1)S(1)}, bf16[384,64]{0,1:T(8,128)(2,1)}, u32[]{:S(2)}) copy-start(bf16[384,64]{0,1:T(8,128)(2,1)} %param.6) | copy-start | bytes 147460
  139.6 30.3 %copy-start.4 = (bf16[8,196,64]{2,0,1:T(8,128)(2,1)S(1)}, bf16[8,196,64]{2,0,1:T(8,128)(2,1)}, u32[]{:S(2)}) copy-start(bf16[8,196,64]{2,0,1:T(8,128)(2,1)} %copy-done.3) | copy-start | bytes 602116
  140.5 21.6 %all-to-all-start.4 = ((f32[256,1,96]{2,1,0:T(1,128)}), f32[256,1,96]{2,1,0:T(1,128)S(1)}, u32[]{:S(2)}, u32[]{:S(2)}) async-start(f32[256,1,96]{2,1,0:T(1,128)} %bitcast.33), calls=%async_computation.6 | async-start | bytes 262144 | tf_op jit(solution)/shard_map/all_to_all | solution.py:12
  163.2 19.4 %all-to-all-start.5 = ((f32[256,1,96]{2,1,0:T(1,128)}), f32[256,1,96]{2,1,0:T(1,128)S(1)}, u32[]{:S(2)}, u32[]{:S(2)}) async-start(f32[256,1,96]{2,1,0:T(1,128)} %broadcast_in_dim.30), calls=%async_computation.7 | async-start | bytes 262144 | tf_op jit(solution)/shard_map/all_to_all | solution.py:14
Sparse Core Ops, SparseCore 0:
  69.6 54.6 reduce-scatter.2
  126.8 47.2 reduce-scatter.4

commit v3 on v2

--- a/solution.py
+++ b/solution.py
@@ -36,10 +36,10 @@
     slot_grads = jnp.einsum(
         "bps,bpd->bsd", combine_low, out_grad, preferred_element_type=jnp.float32
     ).astype(jnp.bfloat16)
-    slots_here, grads_here = (
-        lax.all_to_all(slots, "expert", split_axis=1, concat_axis=0, tiled=True),
-        lax.all_to_all(slot_grads, "expert", split_axis=1, concat_axis=0, tiled=True),
+    sent = lax.all_to_all(
+        jnp.stack([slots, slot_grads]), "expert", split_axis=2, concat_axis=1, tiled=True
     )
+    slots_here, grads_here = sent[0], sent[1]
     hidden = jnp.einsum("rjd,jdf->rjf", slots_here, expert_in, preferred_element_type=jnp.float32)
     activated, gelu_back = jax.vjp(jax.nn.gelu, hidden)
     activated_low = activated.astype(jnp.bfloat16)
@@ -53,10 +53,10 @@
     input_grad_here = jnp.einsum(
         "rjf,jdf->rjd", hidden_grad, expert_in, preferred_element_type=jnp.float32
     ).astype(jnp.bfloat16)
-    outputs, inputs_grad = (
-        lax.all_to_all(outputs_here, "expert", split_axis=0, concat_axis=1, tiled=True),
-        lax.all_to_all(input_grad_here, "expert", split_axis=0, concat_axis=1, tiled=True),
+    returned = lax.all_to_all(
+        jnp.stack([outputs_here, input_grad_here]), "expert", split_axis=1, concat_axis=2, tiled=True
     )
+    outputs, inputs_grad = returned[0], returned[1]
     first_term = jnp.einsum(
         "rjd,rjf->jdf", slots_here, hidden_grad, preferred_element_type=jnp.float32
     )

time: 198 us -> 186 us (0.939)
  blocking collectives: 0 us -> 69.7 us
  waiting for transfers between devices: 68.3 us -> 19.2 us
  starting transfers between devices: 40.7 us -> 15.9 us
  matrix products: 38.4 us -> 34 us
  local copies, waits for them, and re-layouts: 22.5 us -> 19.7 us
    all_to_all x0 -> x2, blocking collectives: none -> 69.7 us  [the longest x1 36 us: on_device(): lax.all_to_all(jnp.stack([outputs_here, input_grad_here]), 'expert', spli...]
    all_to_all x4 -> x0, waiting for transfers between devices: 49.1 us -> none  [the longest x1 13.6 us: on_device(): lax.all_to_all(input_grad_here, 'expert', split_axis=0, concat_axis=1, ti...]
    all_to_all x4 -> x0, starting transfers between devices: 25.3 us -> none  [the longest x1 10.6 us: on_device(): lax.all_to_all(slots, 'expert', split_axis=1, concat_axis=0, tiled=True)]
    all_to_all x4 -> x2, local copies, waits for them, and re-layouts: 6.1 us -> 0.8 us  [the longest x1 0.72 us: on_device(): lax.all_to_all(jnp.stack([outputs_here, input_grad_here]), 'expert', spli...]
    convert_element_type x4 -> x0, local copies, waits for them, and re-layouts: 4.26 us -> none  [the longest x1 1.15 us: on_device(): outputs_here = jnp.einsum('rjf,jfd->rjd', activated_low, expert_out, pref...]
    squeeze x0 -> x2, local copies, waits for them, and re-layouts: none -> 2.29 us  [on_device(): outputs, inputs_grad = (returned[0], returned[1])]
    unnamed x26 -> x34, local copies, waits for them, and re-layouts: 4.02 us -> 5.68 us
  transfers between devices with their start and end apart: 8 -> 4, of which waited for: 6 -> 2; matrix products, arithmetic and copies ran while one was open for 25% -> 25% of each run, Pallas kernels for 0% -> 0%
where the time goes in v3:
time: 186 us; the launch traced here: 184 us
  blocking collectives  69.7 us (37%)
  matrix products  34 us (18%)
  local copies, waits for them, and re-layouts  19.7 us (11%)
  waiting for transfers between devices  19.2 us (10%)
  starting transfers between devices  15.9 us (9%)
  between operations  14.4 us (8%)
  other arithmetic  11.3 us (6%)
    all_to_all x1, blocking collectives, on_device(): lax.all_to_all(jnp.stack([outputs_here, input_grad_here]), 'expert', spli...  36 us
    all_to_all x1, blocking collectives, on_device(): lax.all_to_all(jnp.stack([slots, slot_grads]), 'expert', split_axis=2, co...  33.8 us
    all_to_all x1, waiting for transfers between devices, _sum_everywhere(): lax.all_to_all(pieces, axes, 0, 0, tiled=True)  9.95 us
    all_to_all x1, waiting for transfers between devices, _sum_everywhere(): return lax.all_to_all(spread, axes, 0, 0, tiled=True).reshape(term.shape)  9.17 us
    all_to_all x1, starting transfers between devices, _sum_everywhere(): lax.all_to_all(pieces, axes, 0, 0, tiled=True)  9.11 us
    all_to_all x1, starting transfers between devices, _sum_everywhere(): return lax.all_to_all(spread, axes, 0, 0, tiled=True).reshape(term.shape)  6.56 us
    unnamed x34, local copies, waits for them, and re-layouts  5.68 us
    dot_general x1, matrix products, on_device(): jnp.einsum('rjd,jfd->rjf', grads_here, expert_out, preferred_element_type...  5.26 us
  transfers between devices with their start and end apart: 4, of which 2 were waited for; matrix products, arithmetic and copies ran while one was open for 25% of the time, Pallas kernels for 0%

profile of v3, /device:TPU:32, one launch (start us, length us, event | category | flops | bytes accessed | tf_op | source)
XLA Modules:
  0.0 184.2 jit_solution(8379403470042821304)
XLA Ops:
  7.2 2.0 %fusion.34 = (f32[8,196]{0,1:T(8,128)S(1)}, f32[8,64]{1,0:T(8,128)S(1)}, f32[8,196,64]{2,0,1:T(8,128)S(1)}) fusion(bf16[8,196,384]{2,0,1:T(8,128)(2,1)} %param.5, bf16[384,64]{0,1:T(8,128)(2,1)} %param.6), kind=kOutput, calls=%fused_computation.59 | convolution fusion | flops 77268960 | bytes 1663104 | tf_op jit(solution)/shard_map/bpd,ds->bps/dot_general | solution.py:28
  9.9 1.3 fusion.33
  11.2 1.3 copy.45
  12.5 1.9 %fusion.9 = bf16[1,8,64,384]{3,2,1,0:T(8,128)(2,1)S(1)} fusion(bf16[8,196,64]{1,2,0:T(8,128)(2,1)S(1)} %copy.45, bf16[8,196,384]{2,0,1:T(8,128)(2,1)} %param.5), kind=kOutput, calls=%fused_computation.21 | convolution fusion | flops 77266944 | bytes 1798144 | tf_op jit(solution)/shard_map/bps,bpd->bsd/dot_general | solution.py:33
  14.4 2.0 %fusion.10 = bf16[1,8,64,384]{3,2,1,0:T(8,128)(2,1)S(1)} fusion(bf16[8,196,384]{2,0,1:T(8,128)(2,1)} %param.9, bf16[8,196,64]{2,0,1:T(8,128)(2,1)} %get-tuple-element.22), kind=kOutput, calls=%fused_computation.22 | convolution fusion | flops 77266944 | bytes 1798144 | tf_op jit(solution)/shard_map/bps,bpd->bsd/dot_general | solution.py:36
  16.9 33.8 %all_to_all.45 = bf16[2,8,64,384]{3,1,0,2:T(8,128)(2,1)S(1)} all-to-all(bf16[2,8,64,384]{3,1,0,2:T(8,128)(2,1)S(1)} %copy.41), channel_id=1, replica_groups=mesh['expert'=32,'dp'=8] {'expert'}, dimensions={2} | all-to-all | bytes 1572864 | tf_op jit(solution)/shard_map/all_to_all | solution.py:39
  51.8 1.6 copy-done.7
  53.5 2.8 %convolution_convert_fusion = bf16[2,1536,384]{2,1,0:T(8,128)(2,1)} fusion(bf16[2,32,8,2,384]{4,2,1,3,0:T(8,128)(2,1)S(1)} %bitcast.93, f32[256,2,1536]{2,0,1:T(8,128)S(1)} %convolution_bitcast_fusion.1), kind=kOutput, calls=%fused_computation.2 | convolution fusion | flops 612237312 | bytes 5898240 | tf_op jit(solution)/shard_map/rjf,rjd->jfd/dot_general | solution.py:63
  56.6 5.3 %fusion.6 = bf16[256,2,1536]{2,0,1:T(8,128)(2,1)S(1)} fusion(f32[256,2,1536]{2,0,1:T(8,128)} %copy-done.7, bf16[2,1536,384]{2,1,0:T(8,128)(2,1)} %param.8, bf16[2,32,8,2,384]{4,2,1,3,0:T(8,128)(2,1)} %bitcast.94), kind=kOutput, calls=%fused_computation.12 | convolution fusion | flops 619708416 | bytes 7471104 | tf_op jit(solution)/shard_map/rjd,jfd->rjf/dot_general | solution.py:49
  61.8 1.2 copy-done.12
  63.1 2.4 %convolution_convert_fusion.1 = bf16[2,384,1536]{1,2,0:T(8,128)(2,1)} fusion(bf16[256,2,1536]{2,0,1:T(8,128)(2,1)S(1)} %fusion.6, bf16[2,32,8,2,384]{4,2,1,3,0:T(8,128)(2,1)S(1)} %bitcast.95), kind=kOutput, calls=%fused_computation.3 | convolution fusion | flops 605159424 | bytes 4325376 | tf_op jit(solution)/shard_map/rjd,rjf->jdf/dot_general | solution.py:60
  65.5 2.5 %fusion.8 = bf16[1,256,2,384]{3,1,2,0:T(8,128)(2,1)S(1)} fusion(bf16[256,2,1536]{2,0,1:T(8,128)(2,1)} %copy-done.12, bf16[2,384,1536]{2,1,0:T(8,128)(2,1)S(1)} %copy-done), kind=kOutput, calls=%fused_computation.20 | convolution fusion | flops 604176384 | bytes 4325376 | tf_op jit(solution)/shard_map/rjf,jdf->rjd/dot_general | solution.py:53
  68.1 3.0 %fusion.7 = bf16[1,256,2,384]{3,1,2,0:T(8,128)(2,1)S(1)} fusion(bf16[2,1536,384]{2,1,0:T(8,128)(2,1)} %param.8, f32[256,2,1536]{2,0,1:T(8,128)S(1)} %copy-done.8), kind=kOutput, calls=%fused_computation.19 | convolution fusion | flops 611254272 | bytes 5898240 | tf_op jit(solution)/shard_map/rjf,jfd->rjd/dot_general | solution.py:46
  72.0 36.0 %all_to_all.46 = bf16[2,256,2,384]{3,2,0,1:T(2,128)(2,1)S(1)} all-to-all(bf16[2,256,2,384]{3,2,0,1:T(2,128)(2,1)S(1)} %copy.43), channel_id=1, replica_groups=mesh['expert'=32,'dp'=8] {'expert'}, dimensions={1} | all-to-all | bytes 1572864 | tf_op jit(solution)/shard_map/all_to_all | solution.py:56
  108.7 1.6 fusion.35
  110.3 1.1 squeeze.15
  111.4 2.7 %fusion.11 = f32[8,64,196]{2,1,0:T(8,128)} fusion(bf16[8,64,384]{2,1,0:T(8,128)(2,1)S(1)} %squeeze.15, bf16[8,196,384]{2,0,1:T(8,128)(2,1)} %param.9), kind=kOutput, calls=%fused_computation.24 | convolution fusion | flops 77070336 | bytes 1998848 | tf_op jit(solution)/shard_map/bpd,bsd->bps/dot_general | solution.py:72
  114.1 2.3 %copy.49 = f32[8,64,196]{1,0,2:T(8,128)} copy(f32[8,64,196]{2,1,0:T(8,128)} %fusion.11) | data formatting | bytes 802816 | tf_op jit(solution)/shard_map/bpd,bsd->bps/dot_general | solution.py:72
  116.4 1.1 squeeze.14
  117.6 2.7 %fusion.14 = f32[8,64,196]{2,1,0:T(8,128)} fusion(bf16[8,64,384]{2,1,0:T(8,128)(2,1)S(1)} %squeeze.14, bf16[8,196,384]{2,0,1:T(8,128)(2,1)} %param.5), kind=kOutput, calls=%fused_computation.27 | convolution fusion | flops 77070336 | bytes 1998848 | tf_op jit(solution)/shard_map/bpd,bsd->bps/dot_general | solution.py:73
  120.3 2.3 %copy.47 = f32[8,64,196]{1,0,2:T(8,128)} copy(f32[8,64,196]{2,1,0:T(8,128)} %fusion.14) | data formatting | bytes 802816 | tf_op jit(solution)/shard_map/bpd,bsd->bps/dot_general | solution.py:73
  122.6 2.3 %fusion.21 = (f32[8,64]{1,0:T(8,128)S(1)}, f32[8,196]{0,1:T(8,128)S(1)}) fusion(f32[8,64,196]{1,0,2:T(8,128)} %copy.47, f32[8,64]{1,0:T(8,128)} %copy-done.15, f32[8,196,64]{2,0,1:T(8,128)S(1)} %get-tuple-element.26, f32[8,64]{1,0:T(8,128)} %copy-done.14, f32[8,64,196]{1,0,2:T(8,128)} %copy.49, f32[8,196]{0,1:T(8,128)} %copy-done.11, f32[8,196]{0,1:T(8,128)} %copy-done.9), kind=kLoop, calls=%fused_computation.38 | loop fusion | flops 800736 | bytes 1229184 | tf_op jit(solution)/shard_map/reduce_sum | solution.py:77
  124.9 2.1 %fusion.20 = bf16[8,196,64]{2,0,1:T(8,128)(2,1)S(1)} fusion(f32[8,64,196]{1,0,2:T(8,128)S(1)} %copy-done.2, f32[8,64,196]{1,0,2:T(8,128)} %copy.47, f32[8,196]{0,1:T(8,128)S(1)} %get-tuple-element.17, f32[8,64]{1,0:T(8,128)S(1)} %get-tuple-element.16, f32[8,64]{1,0:T(8,128)} %copy-done.15, f32[8,196,64]{2,0,1:T(8,128)S(1)} %get-tuple-element.26, ...), kind=kLoop, calls=%fused_computation.35 | loop fusion | flops 1003520 | bytes 1429888 | tf_op jit(solution)/shard_map/convert_element_type | solution.py:82
  129.0 9.1 %all-to-all-start.2 = ((f32[256,1,96]{2,1,0:T(1,128)}), f32[256,1,96]{2,1,0:T(1,128)S(1)}, u32[]{:S(2)}, u32[]{:S(2)}) async-start(f32[256,1,96]{2,1,0:T(1,128)} %bitcast.31), calls=%async_computation.4 | async-start | bytes 262144 | tf_op jit(solution)/shard_map/all_to_all | solution.py:12
  138.1 3.0 %fusion.36 = f32[8,196,384]{2,1,0:T(8,128)} fusion(bf16[8,196,64]{1,2,0:T(8,128)(2,1)} %copy-done.10, bf16[8,64,384]{2,1,0:T(8,128)(2,1)S(1)} %squeeze.14), kind=kOutput, calls=%fused_computation.61 | convolution fusion | flops 77070336 | bytes 3002368 | tf_op jit(solution)/shard_map/bps,bsd->bpd/dot_general | solution.py:83
  141.2 10.0 %all-to-all-done.2 = f32[256,1,96]{2,1,0:T(1,128)S(1)} async-done(((f32[256,1,96]{2,1,0:T(1,128)}), f32[256,1,96]{2,1,0:T(1,128)S(1)}, u32[]{:S(2)}, u32[]{:S(2)}) %all-to-all-start.2) | async-done | bytes 98336 | tf_op jit(solution)/shard_map/all_to_all | solution.py:12
  152.1 6.6 %all-to-all-start.3 = ((f32[256,1,96]{2,1,0:T(1,128)}), f32[256,1,96]{2,1,0:T(1,128)S(1)}, u32[]{:S(2)}, u32[]{:S(2)}) async-start(f32[256,1,96]{2,1,0:T(1,128)} %broadcast_in_dim.30), calls=%async_computation.5 | async-start | bytes 262144 | tf_op jit(solution)/shard_map/all_to_all | solution.py:14
  158.7 2.3 %add_convert_fusion = bf16[8,196,384]{2,1,0:T(8,128)(2,1)S(1)} fusion(f32[8,196,384]{2,1,0:T(8,128)} %fusion.36, bf16[8,196,64]{2,0,1:T(8,128)(2,1)S(1)} %copy-done.4, bf16[384,64]{0,1:T(8,128)(2,1)S(1)} %copy-done.13), kind=kOutput, calls=%fused_computation.14 | convolution fusion | flops 78274560 | bytes 3862528 | tf_op jit(solution)/shard_map/bps,ds->bpd/dot_general | solution.py:86
  161.0 1.2 copy.57
  162.2 9.2 %all-to-all-done.3 = f32[256,1,96]{2,1,0:T(1,128)S(1)} async-done(((f32[256,1,96]{2,1,0:T(1,128)}), f32[256,1,96]{2,1,0:T(1,128)S(1)}, u32[]{:S(2)}, u32[]{:S(2)}) %all-to-all-start.3) | async-done | bytes 98336 | tf_op jit(solution)/shard_map/all_to_all | solution.py:14
  173.7 1.8 convert_element_type.63
  175.5 1.8 convert_element_type.61
  (53 shorter events, 9.6 us)
Async XLA Ops:
  7.2 43.6 %copy-start = (bf16[2,384,1536]{2,1,0:T(8,128)(2,1)S(1)}, bf16[2,384,1536]{2,1,0:T(8,128)(2,1)}, u32[]{:S(2)}) copy-start(bf16[2,384,1536]{2,1,0:T(8,128)(2,1)} %param.7) | copy-start | bytes 7077892
  7.2 166.6 %reduce-scatter.5.cloned.1.call-start = ((), (), s32[]{:S(2)}) async-start(), calls=%async_computation.7 | async-start | bytes 2654208 | tf_op jit(solution)/shard_map/reduce_scatter | solution.py:69
  9.2 0.6 copy-start.9
  9.3 2.0 %copy-start.14 = (f32[8,64]{1,0:T(8,128)}, f32[8,64]{1,0:T(8,128)S(1)}, u32[]{:S(2)}) copy-start(f32[8,64]{1,0:T(8,128)S(1)} %get-tuple-element.21) | copy-start | bytes 6148
  9.8 1.4 copy-start.11
  9.8 1.4 copy-start.15
  12.5 4.4 %copy-start.10 = (bf16[8,196,64]{1,2,0:T(8,128)(2,1)}, bf16[8,196,64]{1,2,0:T(8,128)(2,1)S(1)}, u32[]{:S(2)}) copy-start(bf16[8,196,64]{1,2,0:T(8,128)(2,1)S(1)} %copy.45) | copy-start | bytes 602116
  50.8 1.0 copy-start.5
  51.8 1.7 copy-start.7
  56.3 119.2 %reduce-scatter.3.cloned.1.call-start = ((), (), s32[]{:S(2)}) async-start(), calls=%async_computation.6 | async-start | bytes 2654208 | tf_op jit(solution)/shard_map/reduce_scatter | solution.py:66
  56.6 6.5 %copy-start.6 = (bf16[2,8,32,2,384]{4,1,2,3,0:T(8,128)(2,1)S(1)}, bf16[2,8,32,2,384]{4,1,2,3,0:T(8,128)(2,1)}, u32[]{:S(2)}) copy-start(bf16[2,8,32,2,384]{4,1,2,3,0:T(8,128)(2,1)} %copy-done.5) | copy-start | bytes 2359300
  61.8 1.2 copy-start.12
  65.5 2.6 %copy-start.8 = (f32[256,2,1536]{2,0,1:T(8,128)S(1)}, f32[256,2,1536]{2,0,1:T(8,128)}, u32[]{:S(2)}) copy-start(f32[256,2,1536]{2,0,1:T(8,128)} %copy-done.7) | copy-start | bytes 9437188
  122.6 2.3 %copy-start.2 = (f32[8,64,196]{1,0,2:T(8,128)S(1)}, f32[8,64,196]{1,0,2:T(8,128)}, u32[]{:S(2)}) copy-start(f32[8,64,196]{1,0,2:T(8,128)} %copy.49) | copy-start | bytes 1204228
  122.6 5.2 %copy-start.1 = (bf16[8,196,384]{2,0,1:T(8,128)(2,1)S(1)}, bf16[8,196,384]{2,0,1:T(8,128)(2,1)}, u32[]{:S(2)}) copy-start(bf16[8,196,384]{2,0,1:T(8,128)(2,1)} %param.5) | copy-start | bytes 3612676
  127.0 0.8 copy-start.3
  127.7 31.0 %copy-start.13 = (bf16[384,64]{0,1:T(8,128)(2,1)S(1)}, bf16[384,64]{0,1:T(8,128)(2,1)}, u32[]{:S(2)}) copy-start(bf16[384,64]{0,1:T(8,128)(2,1)} %param.6) | copy-start | bytes 147460
  128.1 30.6 %copy-start.4 = (bf16[8,196,64]{2,0,1:T(8,128)(2,1)S(1)}, bf16[8,196,64]{2,0,1:T(8,128)(2,1)}, u32[]{:S(2)}) copy-start(bf16[8,196,64]{2,0,1:T(8,128)(2,1)} %copy-done.3) | copy-start | bytes 602116
  129.0 22.1 %all-to-all-start.2 = ((f32[256,1,96]{2,1,0:T(1,128)}), f32[256,1,96]{2,1,0:T(1,128)S(1)}, u32[]{:S(2)}, u32[]{:S(2)}) async-start(f32[256,1,96]{2,1,0:T(1,128)} %bitcast.31), calls=%async_computation.4 | async-start | bytes 262144 | tf_op jit(solution)/shard_map/all_to_all | solution.py:12
  152.1 19.2 %all-to-all-start.3 = ((f32[256,1,96]{2,1,0:T(1,128)}), f32[256,1,96]{2,1,0:T(1,128)S(1)}, u32[]{:S(2)}, u32[]{:S(2)}) async-start(f32[256,1,96]{2,1,0:T(1,128)} %broadcast_in_dim.30), calls=%async_computation.5 | async-start | bytes 262144 | tf_op jit(solution)/shard_map/all_to_all | solution.py:14
Sparse Core Ops, SparseCore 0:
  56.4 55.0 reduce-scatter.4
  114.1 48.3 reduce-scatter.2

commit v4 on v3

--- a/solution.py
+++ b/solution.py
@@ -24,7 +24,7 @@
     return raised / _reduced(jnp.sum(raised, axis=axis, keepdims=True))
 
 
-def on_device(tokens, router, expert_in, expert_out, out_grad):
+def _token_forward(tokens, router, out_grad):
     logits = jnp.einsum("bpd,ds->bps", tokens, router, preferred_element_type=jnp.float32)
     dispatch = _softmax(logits, 1)
     combine = _softmax(logits, 2)
@@ -39,6 +39,10 @@
     sent = lax.all_to_all(
         jnp.stack([slots, slot_grads]), "expert", split_axis=2, concat_axis=1, tiled=True
     )
+    return (dispatch, combine, dispatch_low), sent
+
+
+def _expert_side(sent, expert_in, expert_out):
     slots_here, grads_here = sent[0], sent[1]
     hidden = jnp.einsum("rjd,jdf->rjf", slots_here, expert_in, preferred_element_type=jnp.float32)
     activated, gelu_back = jax.vjp(jax.nn.gelu, hidden)
@@ -56,19 +60,18 @@
     returned = lax.all_to_all(
         jnp.stack([outputs_here, input_grad_here]), "expert", split_axis=1, concat_axis=2, tiled=True
     )
-    outputs, inputs_grad = returned[0], returned[1]
     first_term = jnp.einsum(
         "rjd,rjf->jdf", slots_here, hidden_grad, preferred_element_type=jnp.float32
     )
     second_term = jnp.einsum(
         "rjf,rjd->jfd", activated_low, grads_here, preferred_element_type=jnp.float32
     )
-    grad_in = lax.psum_scatter(
-        first_term.astype(jnp.bfloat16), "dp", scatter_dimension=2, tiled=True
-    ).astype(jnp.float32)
-    grad_out = lax.psum_scatter(
-        second_term.astype(jnp.bfloat16), "dp", scatter_dimension=1, tiled=True
-    ).astype(jnp.float32)
+    return returned, first_term, second_term
+
+
+def _token_backward(tokens, router, out_grad, kept, returned):
+    dispatch, combine, dispatch_low = kept
+    outputs, inputs_grad = returned[0], returned[1]
     combine_grad = jnp.einsum("bpd,bsd->bps", out_grad, outputs, preferred_element_type=jnp.float32)
     dispatch_grad = jnp.einsum(
         "bpd,bsd->bps", tokens, inputs_grad, preferred_element_type=jnp.float32
@@ -86,6 +89,31 @@
     second_part = jnp.einsum("bps,ds->bpd", logit_low, router, preferred_element_type=jnp.float32)
     grad_tokens = (first_part + second_part).astype(jnp.bfloat16)
     router_term = jnp.einsum("bpd,bps->ds", tokens, logit_low, preferred_element_type=jnp.float32)
+    return grad_tokens, router_term
+
+
+CHUNKS = 2
+
+
+def on_device(tokens, router, expert_in, expert_out, out_grad):
+    size = tokens.shape[0] // CHUNKS
+    pieces = [slice(c * size, (c + 1) * size) for c in range(CHUNKS)]
+    forward = [_token_forward(tokens[c], router, out_grad[c]) for c in pieces]
+    experts = [_expert_side(sent, expert_in, expert_out) for _, sent in forward]
+    backward = [
+        _token_backward(tokens[c], router, out_grad[c], kept, returned)
+        for c, (kept, _), (returned, _, _) in zip(pieces, forward, experts)
+    ]
+    first_term = sum(e[1] for e in experts)
+    second_term = sum(e[2] for e in experts)
+    grad_in = lax.psum_scatter(
+        first_term.astype(jnp.bfloat16), "dp", scatter_dimension=2, tiled=True
+    ).astype(jnp.float32)
+    grad_out = lax.psum_scatter(
+        second_term.astype(jnp.bfloat16), "dp", scatter_dimension=1, tiled=True
+    ).astype(jnp.float32)
+    grad_tokens = jnp.concatenate([b[0] for b in backward], axis=0)
+    router_term = sum(b[1] for b in backward)
     grad_router = _sum_everywhere(router_term, ("expert", "dp"))
     return (grad_tokens, grad_in, grad_out, grad_router)
 

time: 186 us -> 196 us (1.054)
  blocking collectives: 69.7 us -> 0 us
  waiting for transfers between devices: 19.2 us -> 60.3 us
  starting transfers between devices: 15.9 us -> 40.8 us
  local copies, waits for them, and re-layouts: 19.7 us -> 33.9 us
  other arithmetic: 11.3 us -> 6.88 us
  matrix products: 34 us -> 36.6 us
    all_to_all x2 -> x0, blocking collectives: 69.7 us -> none  [the longest x1 36 us: on_device(): lax.all_to_all(jnp.stack([outputs_here, input_grad_here]), 'expert', spli...]
    all_to_all x0 -> x4, waiting for transfers between devices: none -> 43.4 us  [the longest x2 23.3 us: _token_forward(): lax.all_to_all(jnp.stack([slots, slot_grads]), 'expert', split_axis=2, co...]
    all_to_all x0 -> x4, starting transfers between devices: none -> 24.8 us  [the longest x2 15.3 us: _token_forward(): lax.all_to_all(jnp.stack([slots, slot_grads]), 'expert', split_axis=2, co...]
    squeeze x2 -> x8, local copies, waits for them, and re-layouts: 2.29 us -> 8.64 us  [the longest x4 6.76 us: _token_backward(): outputs, inputs_grad = (returned[0], returned[1])]
    slice x1 -> x6, local copies, waits for them, and re-layouts: 1.58 us -> 6.53 us  [the longest x2 3.53 us: on_device(): forward = [_token_forward(tokens[c], router, out_grad[c]) for c in pieces]]
    dot_general x3 -> x0, local copies, waits for them, and re-layouts: 4.69 us -> none  [the longest x1 2.29 us: on_device(): jnp.einsum('bpd,bsd->bps', tokens, inputs_grad, preferred_element_type=jn...]
    another operation x2 -> x4, local copies, waits for them, and re-layouts: 1.27 us -> 4.41 us  [the longest x2 2.3 us: _expert_side(): jnp.stack([outputs_here, input_grad_here])]
    all_to_all x2 -> x4, local copies, waits for them, and re-layouts: 0.8 us -> 3.93 us  [the longest x2 2.66 us: _expert_side(): lax.all_to_all(jnp.stack([outputs_here, input_grad_here]), 'expert', spli...]
  transfers between devices with their start and end apart: 4 -> 8, of which waited for: 2 -> 6; matrix products, arithmetic and copies ran while one was open for 25% -> 30% of each run, Pallas kernels for 0% -> 0%
where the time goes in v4:
time: 196 us; the launch traced here: 193 us
  waiting for transfers between devices  60.3 us (31%)
  starting transfers between devices  40.8 us (21%)
  matrix products  36.6 us (19%)
  local copies, waits for them, and re-layouts  33.9 us (17%)
  between operations  14.8 us (8%)
  other arithmetic  6.88 us (4%)
    all_to_all x2, waiting for transfers between devices, _token_forward(): lax.all_to_all(jnp.stack([slots, slot_grads]), 'expert', split_axis=2, co...  23.3 us
    all_to_all x2, waiting for transfers between devices, _expert_side(): lax.all_to_all(jnp.stack([outputs_here, input_grad_here]), 'expert', spli...  20.1 us
    all_to_all x2, starting transfers between devices, _token_forward(): lax.all_to_all(jnp.stack([slots, slot_grads]), 'expert', split_axis=2, co...  15.3 us
    all_to_all x1, waiting for transfers between devices, _sum_everywhere(): return lax.all_to_all(spread, axes, 0, 0, tiled=True).reshape(term.shape)  9.62 us
    all_to_all x2, starting transfers between devices, _expert_side(): lax.all_to_all(jnp.stack([outputs_here, input_grad_here]), 'expert', spli...  9.55 us
    all_to_all x1, starting transfers between devices, _sum_everywhere(): lax.all_to_all(pieces, axes, 0, 0, tiled=True)  8.86 us
    all_to_all x1, waiting for transfers between devices, _sum_everywhere(): lax.all_to_all(pieces, axes, 0, 0, tiled=True)  7.24 us
    unnamed x82, local copies, waits for them, and re-layouts  7.21 us
  transfers between devices with their start and end apart: 8, of which 6 were waited for; matrix products, arithmetic and copies ran while one was open for 30% of the time, Pallas kernels for 0%

profile of v4, /device:TPU:32, one launch (start us, length us, event | category | flops | bytes accessed | tf_op | source)
XLA Modules:
  0.0 193.2 jit_solution(16834889026913712171)
XLA Ops:
  7.2 2.3 %fusion.69 = (bf16[4,196,384]{2,0,1:T(4,128)(2,1)S(1)}, bf16[4,196,384]{2,0,1:T(4,128)(2,1)S(1)}) fusion(bf16[8,196,384]{2,0,1:T(8,128)(2,1)} %param.5), kind=kLoop, calls=%fused_computation.110 | loop fusion | bytes 2408448 | tf_op jit(solution)/shard_map/slice | solution.py:101
  14.7 10.7 %all-to-all-start = ((bf16[2,4,64,384]{3,1,0,2:T(4,128)(2,1)}), bf16[2,4,64,384]{3,1,0,2:T(4,128)(2,1)}, u32[]{:S(2)}, u32[]{:S(2)}) async-start(bf16[2,4,64,384]{3,1,0,2:T(4,128)(2,1)} %copy.47), calls=%async_computation | async-start | bytes 786432 | tf_op jit(solution)/shard_map/all_to_all | solution.py:39
  29.0 11.4 %all-to-all-done = bf16[2,4,64,384]{3,1,0,2:T(4,128)(2,1)} async-done(((bf16[2,4,64,384]{3,1,0,2:T(4,128)(2,1)}), bf16[2,4,64,384]{3,1,0,2:T(4,128)(2,1)}, u32[]{:S(2)}, u32[]{:S(2)}) %all-to-all-start) | async-done | bytes 393248 | tf_op jit(solution)/shard_map/all_to_all | solution.py:39
  40.3 4.6 %all-to-all-start.2 = ((bf16[2,4,64,384]{3,1,0,2:T(4,128)(2,1)}), bf16[2,4,64,384]{3,1,0,2:T(4,128)(2,1)S(1)}, u32[]{:S(2)}, u32[]{:S(2)}) async-start(bf16[2,4,64,384]{3,1,0,2:T(4,128)(2,1)} %copy.53), calls=%async_computation.2 | async-start | bytes 786432 | tf_op jit(solution)/shard_map/all_to_all | solution.py:39
  48.0 11.9 %all-to-all-done.2 = bf16[2,4,64,384]{3,1,0,2:T(4,128)(2,1)S(1)} async-done(((bf16[2,4,64,384]{3,1,0,2:T(4,128)(2,1)}), bf16[2,4,64,384]{3,1,0,2:T(4,128)(2,1)S(1)}, u32[]{:S(2)}, u32[]{:S(2)}) %all-to-all-start.2) | async-done | bytes 393248 | tf_op jit(solution)/shard_map/all_to_all | solution.py:39
  64.4 2.3 %add_convert_fusion = bf16[2,1536,384]{2,1,0:T(8,128)(2,1)} fusion(f32[2,1536,384]{2,1,0:T(8,128)S(1)} %fusion.66, bf16[128,2,384]{2,0,1:T(8,128)(2,1)S(1)} %copy-done.25, f32[128,2,1536]{2,0,1:T(8,128)S(1)} %convolution_bitcast_fusion.1), kind=kOutput, calls=%fused_computation | convolution fusion | flops 307888128 | bytes 8847360 | tf_op jit(solution)/shard_map/rjf,rjd->jfd/dot_general | solution.py:66
  67.0 3.7 %fusion.18 = bf16[1,128,2,384]{3,1,2,0:T(8,128)(2,1)} fusion(bf16[2,1536,384]{2,1,0:T(8,128)(2,1)} %param.8, f32[128,2,1536]{2,0,1:T(8,128)} %copy-done.4), kind=kOutput, calls=%fused_computation.45 | convolution fusion | flops 305627136 | bytes 4128768 | tf_op jit(solution)/shard_map/rjf,jfd->rjd/dot_general | solution.py:50
  70.7 1.4 fusion.6
  75.8 2.3 %add_convert_fusion.1 = bf16[2,384,1536]{1,2,0:T(8,128)(2,1)} fusion(f32[2,384,1536]{1,2,0:T(8,128)S(1)} %fusion.75, bf16[128,2,384]{2,0,1:T(8,128)(2,1)S(1)} %copy-done.18, bf16[128,2,1536]{2,0,1:T(8,128)(2,1)S(1)} %fusion.13), kind=kOutput, calls=%fused_computation.1 | convolution fusion | flops 304349184 | bytes 8060928 | tf_op jit(solution)/shard_map/rjd,rjf->jdf/dot_general | solution.py:63
  78.2 2.0 %fusion.19 = bf16[1,128,2,384]{3,1,2,0:T(8,128)(2,1)S(1)} fusion(bf16[128,2,1536]{2,0,1:T(8,128)(2,1)} %copy-done.6, bf16[2,384,1536]{2,1,0:T(8,128)(2,1)S(1)} %copy-done), kind=kOutput, calls=%fused_computation.46 | convolution fusion | flops 302088192 | bytes 3342336 | tf_op jit(solution)/shard_map/rjf,jdf->rjd/dot_general | solution.py:57
  81.4 4.7 %all-to-all-start.3 = ((bf16[2,128,2,384]{3,2,0,1:T(2,128)(2,1)}), bf16[2,128,2,384]{3,2,0,1:T(2,128)(2,1)}, u32[]{:S(2)}, u32[]{:S(2)}) async-start(bf16[2,128,2,384]{3,2,0,1:T(2,128)(2,1)} %copy.55), calls=%async_computation.3 | async-start | bytes 786432 | tf_op jit(solution)/shard_map/all_to_all | solution.py:60
  87.5 2.4 %fusion.16 = bf16[1,128,2,384]{3,1,2,0:T(8,128)(2,1)S(1)} fusion(bf16[2,1536,384]{2,1,0:T(8,128)(2,1)} %param.8, f32[128,2,1536]{2,0,1:T(8,128)S(1)} %copy-done.3), kind=kOutput, calls=%fused_computation.43 | convolution fusion | flops 305627136 | bytes 4128768 | tf_op jit(solution)/shard_map/rjf,jfd->rjd/dot_general | solution.py:50
  91.1 13.9 %all-to-all-done.3 = bf16[2,128,2,384]{3,2,0,1:T(2,128)(2,1)} async-done(((bf16[2,128,2,384]{3,2,0,1:T(2,128)(2,1)}), bf16[2,128,2,384]{3,2,0,1:T(2,128)(2,1)}, u32[]{:S(2)}, u32[]{:S(2)}) %all-to-all-start.3) | async-done | bytes 393248 | tf_op jit(solution)/shard_map/all_to_all | solution.py:60
  105.0 4.9 %all-to-all-start.1 = ((bf16[2,128,2,384]{3,2,0,1:T(2,128)(2,1)}), bf16[2,128,2,384]{3,2,0,1:T(2,128)(2,1)}, u32[]{:S(2)}, u32[]{:S(2)}) async-start(bf16[2,128,2,384]{3,2,0,1:T(2,128)(2,1)} %copy.49), calls=%async_computation.1 | async-start | bytes 786432 | tf_op jit(solution)/shard_map/all_to_all | solution.py:60
  112.2 1.7 squeeze.31
  113.9 1.7 squeeze.30
  115.6 1.5 convolution_bitcast_fusion.4
  117.2 2.2 %multiply_reduce_fusion.1 = (f32[4,64]{1,0:T(4,128)S(1)}, f32[4,196]{1,0:T(4,128)S(1)}, f32[4,196,64]{1,2,0:T(8,128)}) fusion(f32[4,64]{1,0:T(4,128)S(1)} %get-tuple-element.24, f32[4,196,64]{1,2,0:T(8,128)} %copy-done.13, f32[4,64]{1,0:T(4,128)S(1)} %get-tuple-element.26, f32[4,196,64]{1,2,0:T(8,128)S(1)} %convolution_bitcast_fusion.4, ...), kind=kOutput, calls=%fused_computation.79 | convolution fusion | flops 38935536 | bytes 1413312 | tf_op jit(solution)/shard_map/bpd,bsd->bps/dot_general | solution.py:76
  119.5 6.2 %all-to-all-done.1 = bf16[2,128,2,384]{3,2,0,1:T(2,128)(2,1)} async-done(((bf16[2,128,2,384]{3,2,0,1:T(2,128)(2,1)}), bf16[2,128,2,384]{3,2,0,1:T(2,128)(2,1)}, u32[]{:S(2)}, u32[]{:S(2)}) %all-to-all-start.1) | async-done | bytes 393248 | tf_op jit(solution)/shard_map/all_to_all | solution.py:60
  128.1 1.7 squeeze.27
  129.8 1.7 squeeze.26
  131.4 1.5 convolution_bitcast_fusion.6
  133.1 1.5 multiply_reduce_fusion.3
  138.2 8.9 %all-to-all-start.4 = ((f32[256,1,96]{2,1,0:T(1,128)}), f32[256,1,96]{2,1,0:T(1,128)}, u32[]{:S(2)}, u32[]{:S(2)}) async-start(f32[256,1,96]{2,1,0:T(1,128)} %bitcast.56), calls=%async_computation.6 | async-start | bytes 262144 | tf_op jit(solution)/shard_map/all_to_all | solution.py:12
  147.1 1.7 fusion.50
  150.0 1.7 fusion.53
  151.7 7.2 %all-to-all-done.4 = f32[256,1,96]{2,1,0:T(1,128)} async-done(((f32[256,1,96]{2,1,0:T(1,128)}), f32[256,1,96]{2,1,0:T(1,128)}, u32[]{:S(2)}, u32[]{:S(2)}) %all-to-all-start.4) | async-done | bytes 98336 | tf_op jit(solution)/shard_map/all_to_all | solution.py:12
  160.9 6.8 %all-to-all-start.5 = ((f32[256,1,96]{2,1,0:T(1,128)}), f32[256,1,96]{2,1,0:T(1,128)S(1)}, u32[]{:S(2)}, u32[]{:S(2)}) async-start(f32[256,1,96]{2,1,0:T(1,128)} %broadcast_in_dim.54), calls=%async_computation.7 | async-start | bytes 262144 | tf_op jit(solution)/shard_map/all_to_all | solution.py:14
  167.8 1.7 fusion.14
  170.8 9.6 %all-to-all-done.5 = f32[256,1,96]{2,1,0:T(1,128)S(1)} async-done(((f32[256,1,96]{2,1,0:T(1,128)}), f32[256,1,96]{2,1,0:T(1,128)S(1)}, u32[]{:S(2)}, u32[]{:S(2)}) %all-to-all-start.5) | async-done | bytes 98336 | tf_op jit(solution)/shard_map/all_to_all | solution.py:14
  182.8 1.8 convert_element_type.111
  184.6 1.8 convert_element_type.109
  (136 shorter events, 39.0 us)
Async XLA Ops:
  7.2 53.8 %copy-start = (bf16[2,384,1536]{2,1,0:T(8,128)(2,1)S(1)}, bf16[2,384,1536]{2,1,0:T(8,128)(2,1)}, u32[]{:S(2)}) copy-start(bf16[2,384,1536]{2,1,0:T(8,128)(2,1)} %param.7) | copy-start | bytes 7077892
  7.2 2.3 %copy-start.29 = (bf16[384,64]{0,1:T(8,128)(2,1)S(1)}, bf16[384,64]{0,1:T(8,128)(2,1)}, u32[]{:S(2)}) copy-start(bf16[384,64]{0,1:T(8,128)(2,1)} %param.6) | copy-start | bytes 147460
  9.5 3.0 %copy-start.7 = (bf16[4,196,384]{2,0,1:T(4,128)(2,1)}, bf16[4,196,384]{2,0,1:T(4,128)(2,1)S(1)}, u32[]{:S(2)}) copy-start(bf16[4,196,384]{2,0,1:T(4,128)(2,1)S(1)} %get-tuple-element.28) | copy-start | bytes 1806340
  9.5 18.0 %copy-start.9 = (bf16[4,196,384]{2,0,1:T(4,128)(2,1)}, bf16[4,196,384]{2,0,1:T(4,128)(2,1)S(1)}, u32[]{:S(2)}) copy-start(bf16[4,196,384]{2,0,1:T(4,128)(2,1)S(1)} %get-tuple-element.29) | copy-start | bytes 1806340
  9.5 1.7 copy-start.19
  10.0 123.0 %copy-start.31 = (f32[4,196]{1,0:T(4,128)}, f32[4,196]{1,0:T(4,128)S(1)}, u32[]{:S(2)}) copy-start(f32[4,196]{1,0:T(4,128)S(1)} %get-tuple-element.21) | copy-start | bytes 9412
  10.2 122.8 %copy-start.33 = (f32[4,196]{1,0:T(4,128)}, f32[4,196]{1,0:T(4,128)S(1)}, u32[]{:S(2)}) copy-start(f32[4,196]{1,0:T(4,128)S(1)} %get-tuple-element.19) | copy-start | bytes 9412
  14.7 25.6 %all-to-all-start = ((bf16[2,4,64,384]{3,1,0,2:T(4,128)(2,1)}), bf16[2,4,64,384]{3,1,0,2:T(4,128)(2,1)}, u32[]{:S(2)}, u32[]{:S(2)}) async-start(bf16[2,4,64,384]{3,1,0,2:T(4,128)(2,1)} %copy.47), calls=%async_computation | async-start | bytes 786432 | tf_op jit(solution)/shard_map/all_to_all | solution.py:39
  25.9 1.9 copy-start.13
  25.9 91.2 %copy-start.35 = (f32[4,196]{1,0:T(4,128)}, f32[4,196]{1,0:T(4,128)S(1)}, u32[]{:S(2)}) copy-start(f32[4,196]{1,0:T(4,128)S(1)} %get-tuple-element.27) | copy-start | bytes 9412
  26.1 91.1 %copy-start.37 = (f32[4,196]{1,0:T(4,128)}, f32[4,196]{1,0:T(4,128)S(1)}, u32[]{:S(2)}) copy-start(f32[4,196]{1,0:T(4,128)S(1)} %get-tuple-element.25) | copy-start | bytes 9412
  40.3 19.6 %all-to-all-start.2 = ((bf16[2,4,64,384]{3,1,0,2:T(4,128)(2,1)}), bf16[2,4,64,384]{3,1,0,2:T(4,128)(2,1)S(1)}, u32[]{:S(2)}, u32[]{:S(2)}) async-start(bf16[2,4,64,384]{3,1,0,2:T(4,128)(2,1)} %copy.53), calls=%async_computation.2 | async-start | bytes 786432 | tf_op jit(solution)/shard_map/all_to_all | solution.py:39
  44.9 137.8 %reduce-scatter.5.cloned.1.call-start = ((), (), s32[]{:S(2)}) async-start(), calls=%async_computation.9 | async-start | bytes 2654208 | tf_op jit(solution)/shard_map/reduce_scatter | solution.py:112
  47.0 15.3 %copy-start.22 = (bf16[128,2,384]{2,0,1:T(8,128)(2,1)}, bf16[128,2,384]{2,0,1:T(8,128)(2,1)S(1)}, u32[]{:S(2)}) copy-start(bf16[128,2,384]{2,0,1:T(8,128)(2,1)S(1)} %squeeze.25) | copy-start | bytes 589828
  48.0 13.6 %copy-start.15 = (bf16[128,2,384]{2,0,1:T(8,128)(2,1)}, bf16[128,2,384]{2,0,1:T(8,128)(2,1)S(1)}, u32[]{:S(2)}) copy-start(bf16[128,2,384]{2,0,1:T(8,128)(2,1)S(1)} %squeeze.24) | copy-start | bytes 589828
  61.7 2.6 %copy-start.4 = (f32[128,2,1536]{2,0,1:T(8,128)}, f32[128,2,1536]{2,0,1:T(8,128)S(1)}, u32[]{:S(2)}) copy-start(f32[128,2,1536]{2,0,1:T(8,128)S(1)} %convolution_bitcast_fusion.1) | copy-start | bytes 4718596
  66.7 117.8 %reduce-scatter.3.cloned.1.call-start = ((), (), s32[]{:S(2)}) async-start(), calls=%async_computation.8 | async-start | bytes 2654208 | tf_op jit(solution)/shard_map/reduce_scatter | solution.py:109
  67.0 3.7 %copy-start.2 = (f32[128,2,1536]{2,0,1:T(8,128)S(1)}, f32[128,2,1536]{2,0,1:T(8,128)}, u32[]{:S(2)}) copy-start(f32[128,2,1536]{2,0,1:T(8,128)} %copy-done.1) | copy-start | bytes 4718596
  67.0 3.7 %copy-start.23 = (bf16[128,2,384]{2,0,1:T(8,128)(2,1)S(1)}, bf16[128,2,384]{2,0,1:T(8,128)(2,1)}, u32[]{:S(2)}) copy-start(bf16[128,2,384]{2,0,1:T(8,128)(2,1)} %copy-done.22) | copy-start | bytes 589828
  67.0 3.7 %copy-start.39 = (bf16[2,1536,384]{2,1,0:T(8,128)(2,1)S(1)}, bf16[2,1536,384]{2,1,0:T(8,128)(2,1)}, u32[]{:S(2)}) copy-start(bf16[2,1536,384]{2,1,0:T(8,128)(2,1)} %param.8) | copy-start | bytes 7077892
  73.5 2.3 %copy-start.18 = (bf16[128,2,384]{2,0,1:T(8,128)(2,1)S(1)}, bf16[128,2,384]{2,0,1:T(8,128)(2,1)}, u32[]{:S(2)}) copy-start(bf16[128,2,384]{2,0,1:T(8,128)(2,1)} %copy-done.17) | copy-start | bytes 589828
  78.1 2.0 %copy-start.28 = (bf16[1,128,2,384]{3,1,2,0:T(8,128)(2,1)S(1)}, bf16[1,128,2,384]{3,1,2,0:T(8,128)(2,1)}, u32[]{:S(2)}) copy-start(bf16[1,128,2,384]{3,1,2,0:T(8,128)(2,1)} %fusion.18) | copy-start | bytes 589828
  81.4 23.6 %all-to-all-start.3 = ((bf16[2,128,2,384]{3,2,0,1:T(2,128)(2,1)}), bf16[2,128,2,384]{3,2,0,1:T(2,128)(2,1)}, u32[]{:S(2)}, u32[]{:S(2)}) async-start(bf16[2,128,2,384]{3,2,0,1:T(2,128)(2,1)} %copy.55), calls=%async_computation.3 | async-start | bytes 786432 | tf_op jit(solution)/shard_map/all_to_all | solution.py:60
  105.0 20.7 %all-to-all-start.1 = ((bf16[2,128,2,384]{3,2,0,1:T(2,128)(2,1)}), bf16[2,128,2,384]{3,2,0,1:T(2,128)(2,1)}, u32[]{:S(2)}, u32[]{:S(2)}) async-start(bf16[2,128,2,384]{3,2,0,1:T(2,128)(2,1)} %copy.49), calls=%async_computation.1 | async-start | bytes 786432 | tf_op jit(solution)/shard_map/all_to_all | solution.py:60
  109.9 7.3 %copy-start.10 = (bf16[4,196,384]{2,0,1:T(4,128)(2,1)S(1)}, bf16[4,196,384]{2,0,1:T(4,128)(2,1)}, u32[]{:S(2)}) copy-start(bf16[4,196,384]{2,0,1:T(4,128)(2,1)} %copy-done.9) | copy-start | bytes 1806340
  117.2 2.3 %copy-start.20 = (f32[4,196,64]{1,2,0:T(8,128)}, f32[4,196,64]{1,2,0:T(8,128)S(1)}, u32[]{:S(2)}) copy-start(f32[4,196,64]{1,2,0:T(8,128)S(1)} %convolution_bitcast_fusion.4) | copy-start | bytes 602116
  125.7 7.3 %copy-start.8 = (bf16[4,196,384]{2,0,1:T(4,128)(2,1)S(1)}, bf16[4,196,384]{2,0,1:T(4,128)(2,1)}, u32[]{:S(2)}) copy-start(bf16[4,196,384]{2,0,1:T(4,128)(2,1)} %copy-done.7) | copy-start | bytes 1806340
  133.1 1.8 copy-start.11
  138.2 20.7 %all-to-all-start.4 = ((f32[256,1,96]{2,1,0:T(1,128)}), f32[256,1,96]{2,1,0:T(1,128)}, u32[]{:S(2)}, u32[]{:S(2)}) async-start(f32[256,1,96]{2,1,0:T(1,128)} %bitcast.56), calls=%async_computation.6 | async-start | bytes 262144 | tf_op jit(solution)/shard_map/all_to_all | solution.py:12
  147.1 2.9 %copy-start.24 = (bf16[4,64,384]{2,1,0:T(8,128)(2,1)S(1)}, bf16[4,64,384]{2,1,0:T(8,128)(2,1)}, u32[]{:S(2)}) copy-start(bf16[4,64,384]{2,1,0:T(8,128)(2,1)} %squeeze.26) | copy-start | bytes 589828
  150.0 17.7 %copy-start.30 = (bf16[384,64]{0,1:T(8,128)(2,1)S(1)}, bf16[384,64]{0,1:T(8,128)(2,1)}, u32[]{:S(2)}) copy-start(bf16[384,64]{0,1:T(8,128)(2,1)} %param.6) | copy-start | bytes 147460
  160.9 19.5 %all-to-all-start.5 = ((f32[256,1,96]{2,1,0:T(1,128)}), f32[256,1,96]{2,1,0:T(1,128)S(1)}, u32[]{:S(2)}, u32[]{:S(2)}) async-start(f32[256,1,96]{2,1,0:T(1,128)} %broadcast_in_dim.54), calls=%async_computation.7 | async-start | bytes 262144 | tf_op jit(solution)/shard_map/all_to_all | solution.py:14
  (16 other events, 19.6 us)
Sparse Core Ops, SparseCore 0:
  66.9 48.3 reduce-scatter.4
  117.8 50.8 reduce-scatter.2

commit v5 on v3

--- a/solution.py
+++ b/solution.py
@@ -36,10 +36,11 @@
     slot_grads = jnp.einsum(
         "bps,bpd->bsd", combine_low, out_grad, preferred_element_type=jnp.float32
     ).astype(jnp.bfloat16)
+    width = slots.shape[-1]
     sent = lax.all_to_all(
-        jnp.stack([slots, slot_grads]), "expert", split_axis=2, concat_axis=1, tiled=True
+        jnp.concatenate([slots, slot_grads], axis=-1), "expert", split_axis=1, concat_axis=0, tiled=True
     )
-    slots_here, grads_here = sent[0], sent[1]
+    slots_here, grads_here = sent[..., :width], sent[..., width:]
     hidden = jnp.einsum("rjd,jdf->rjf", slots_here, expert_in, preferred_element_type=jnp.float32)
     activated, gelu_back = jax.vjp(jax.nn.gelu, hidden)
     activated_low = activated.astype(jnp.bfloat16)
@@ -54,9 +55,10 @@
         "rjf,jdf->rjd", hidden_grad, expert_in, preferred_element_type=jnp.float32
     ).astype(jnp.bfloat16)
     returned = lax.all_to_all(
-        jnp.stack([outputs_here, input_grad_here]), "expert", split_axis=1, concat_axis=2, tiled=True
+        jnp.concatenate([outputs_here, input_grad_here], axis=-1),
+        "expert", split_axis=0, concat_axis=1, tiled=True,
     )
-    outputs, inputs_grad = returned[0], returned[1]
+    outputs, inputs_grad = returned[..., :width], returned[..., width:]
     first_term = jnp.einsum(
         "rjd,rjf->jdf", slots_here, hidden_grad, preferred_element_type=jnp.float32
     )

time: 186 us -> 188 us (1.011)
    all_to_all x2 -> x3, local copies, waits for them, and re-layouts: 0.8 us -> 4.52 us  [the longest x2 4.47 us: on_device(): lax.all_to_all(jnp.concatenate([outputs_here, input_grad_here], axis=-1),...]
    squeeze x2 -> x0, local copies, waits for them, and re-layouts: 2.29 us -> none  [on_device(): outputs, inputs_grad = (returned[0], returned[1])]
    unnamed x34 -> x28, local copies, waits for them, and re-layouts: 5.68 us -> 5.61 us
  transfers between devices with their start and end apart: 4 -> 4, of which waited for: 2 -> 2; matrix products, arithmetic and copies ran while one was open for 25% -> 23% of each run, Pallas kernels for 0% -> 0%
where the time goes in v5:
time: 188 us; the launch traced here: 186 us
  blocking collectives  69.7 us (37%)
  matrix products  33.4 us (18%)
  local copies, waits for them, and re-layouts  21.1 us (11%)
  waiting for transfers between devices  18.9 us (10%)
  starting transfers between devices  17.1 us (9%)
  between operations  14.3 us (8%)
  other arithmetic  11.9 us (6%)
    all_to_all x1, blocking collectives, on_device(): lax.all_to_all(jnp.concatenate([outputs_here, input_grad_here], axis=-1),...  36 us
    all_to_all x1, blocking collectives, on_device(): lax.all_to_all(jnp.concatenate([slots, slot_grads], axis=-1), 'expert', s...  33.7 us
    all_to_all x1, starting transfers between devices, _sum_everywhere(): lax.all_to_all(pieces, axes, 0, 0, tiled=True)  10.3 us
    all_to_all x1, waiting for transfers between devices, _sum_everywhere(): lax.all_to_all(pieces, axes, 0, 0, tiled=True)  9.8 us
    all_to_all x1, waiting for transfers between devices, _sum_everywhere(): return lax.all_to_all(spread, axes, 0, 0, tiled=True).reshape(term.shape)  9.02 us
    all_to_all x1, starting transfers between devices, _sum_everywhere(): return lax.all_to_all(spread, axes, 0, 0, tiled=True).reshape(term.shape)  6.63 us
    unnamed x28, local copies, waits for them, and re-layouts  5.61 us
    dot_general x1, matrix products, on_device(): jnp.einsum('rjd,jfd->rjf', grads_here, expert_out, preferred_element_type...  5.26 us
  transfers between devices with their start and end apart: 4, of which 2 were waited for; matrix products, arithmetic and copies ran while one was open for 23% of the time, Pallas kernels for 0%

profile of v5, /device:TPU:32, one launch (start us, length us, event | category | flops | bytes accessed | tf_op | source)
XLA Modules:
  0.0 186.4 jit_solution(7922565339358121004)
XLA Ops:
  7.2 2.0 %fusion.40 = (f32[8,196]{0,1:T(8,128)S(1)}, f32[8,64]{1,0:T(8,128)S(1)}, f32[8,196,64]{2,0,1:T(8,128)S(1)}) fusion(bf16[8,196,384]{2,0,1:T(8,128)(2,1)} %param.5, bf16[384,64]{0,1:T(8,128)(2,1)} %param.6), kind=kOutput, calls=%fused_computation.63 | convolution fusion | flops 77268960 | bytes 1663104 | tf_op jit(solution)/shard_map/bpd,ds->bps/dot_general | solution.py:28
  9.8 1.3 fusion.39
  11.1 1.3 copy.41
  12.4 1.8 convolution_convert_fusion.5
  14.2 2.0 %convolution_convert_fusion.4 = bf16[8,64,384]{2,1,0:T(8,128)(2,1)S(1)} fusion(bf16[8,196,384]{2,0,1:T(8,128)(2,1)} %param.9, bf16[8,196,64]{2,0,1:T(8,128)(2,1)} %get-tuple-element.22), kind=kOutput, calls=%fused_computation.17 | convolution fusion | flops 77266944 | bytes 1798144 | tf_op jit(solution)/shard_map/bps,bpd->bsd/dot_general | solution.py:36
  16.7 33.7 %all_to_all.51 = bf16[8,64,768]{2,0,1:T(8,128)(2,1)S(1)} all-to-all(bf16[8,64,768]{2,0,1:T(8,128)(2,1)S(1)} %copy.37), channel_id=1, replica_groups=mesh['expert'=32,'dp'=8] {'expert'}, dimensions={1} | all-to-all | bytes 1572864 | tf_op jit(solution)/shard_map/all_to_all | solution.py:40
  51.5 1.7 copy-done.7
  53.1 2.9 %convolution_convert_fusion = bf16[2,1536,384]{2,1,0:T(8,128)(2,1)} fusion(bf16[256,2,768]{2,0,1:T(8,128)(2,1)S(1)} %bitcast.76, f32[256,2,1536]{2,0,1:T(8,128)S(1)} %convolution_bitcast_fusion.1), kind=kOutput, calls=%fused_computation.2 | convolution fusion | flops 612237312 | bytes 5898240 | tf_op jit(solution)/shard_map/rjf,rjd->jfd/dot_general | solution.py:65
  56.2 5.3 %fusion.6 = bf16[256,2,1536]{2,0,1:T(8,128)(2,1)S(1)} fusion(f32[256,2,1536]{2,0,1:T(8,128)} %copy-done.7, bf16[2,1536,384]{2,1,0:T(8,128)(2,1)} %param.8, bf16[256,2,768]{2,0,1:T(8,128)(2,1)} %bitcast.77), kind=kOutput, calls=%fused_computation.12 | convolution fusion | flops 619708416 | bytes 7471104 | tf_op jit(solution)/shard_map/rjd,jfd->rjf/dot_general | solution.py:50
  61.5 1.2 copy-done.11
  62.7 2.4 %convolution_convert_fusion.1 = bf16[2,384,1536]{1,2,0:T(8,128)(2,1)} fusion(bf16[256,2,1536]{2,0,1:T(8,128)(2,1)S(1)} %fusion.6, bf16[256,2,768]{2,0,1:T(8,128)(2,1)S(1)} %bitcast.78), kind=kOutput, calls=%fused_computation.3 | convolution fusion | flops 605159424 | bytes 4325376 | tf_op jit(solution)/shard_map/rjd,rjf->jdf/dot_general | solution.py:62
  65.2 2.5 %fusion.8 = bf16[256,2,384]{2,0,1:T(8,128)(2,1)S(1)} fusion(bf16[256,2,1536]{2,0,1:T(8,128)(2,1)} %copy-done.11, bf16[2,384,1536]{2,1,0:T(8,128)(2,1)S(1)} %copy-done), kind=kOutput, calls=%fused_computation.20 | convolution fusion | flops 604176384 | bytes 4325376 | tf_op jit(solution)/shard_map/rjf,jdf->rjd/dot_general | solution.py:54
  67.8 3.0 %fusion.7 = bf16[256,2,384]{2,0,1:T(8,128)(2,1)S(1)} fusion(bf16[2,1536,384]{2,1,0:T(8,128)(2,1)} %param.8, f32[256,2,1536]{2,0,1:T(8,128)S(1)} %copy-done.8), kind=kOutput, calls=%fused_computation.19 | convolution fusion | flops 611254272 | bytes 5898240 | tf_op jit(solution)/shard_map/rjf,jfd->rjd/dot_general | solution.py:47
  71.6 36.0 %all_to_all.52 = bf16[256,2,768]{2,1,0:T(2,128)(2,1)S(1)} all-to-all(bf16[256,2,768]{2,1,0:T(2,128)(2,1)S(1)} %copy.39), channel_id=1, replica_groups=mesh['expert'=32,'dp'=8] {'expert'}, dimensions={0} | all-to-all | bytes 1572864 | tf_op jit(solution)/shard_map/all_to_all | solution.py:57
  107.6 1.5 copy.73
  109.1 3.0 %all_to_all.43 = bf16[8,64,768]{2,1,0:T(8,128)(2,1)} reshape(bf16[8,32,2,768]{3,2,1,0:T(2,128)(2,1)} %bitcast.81) | data formatting | bytes 1572864 | tf_op jit(solution)/shard_map/all_to_all | solution.py:57
  112.1 2.8 %fusion.12 = f32[8,64,196]{2,1,0:T(8,128)} fusion(bf16[8,196,384]{2,0,1:T(8,128)(2,1)} %param.5, bf16[8,64,768]{2,1,0:T(8,128)(2,1)} %all_to_all.43), kind=kOutput, calls=%fused_computation.25 | convolution fusion | flops 77070336 | bytes 1998848 | tf_op jit(solution)/shard_map/bpd,bsd->bps/dot_general | solution.py:75
  114.9 2.3 %copy.43 = f32[8,64,196]{1,0,2:T(8,128)} copy(f32[8,64,196]{2,1,0:T(8,128)} %fusion.12) | data formatting | bytes 802816 | tf_op jit(solution)/shard_map/bpd,bsd->bps/dot_general | solution.py:75
  117.2 2.8 %fusion.9 = f32[8,64,196]{2,1,0:T(8,128)} fusion(bf16[8,196,384]{2,0,1:T(8,128)(2,1)} %param.9, bf16[8,64,768]{2,1,0:T(8,128)(2,1)} %all_to_all.43), kind=kOutput, calls=%fused_computation.22 | convolution fusion | flops 77070336 | bytes 1998848 | tf_op jit(solution)/shard_map/bpd,bsd->bps/dot_general | solution.py:74
  120.0 2.3 %copy.45 = f32[8,64,196]{1,0,2:T(8,128)} copy(f32[8,64,196]{2,1,0:T(8,128)} %fusion.9) | data formatting | bytes 802816 | tf_op jit(solution)/shard_map/bpd,bsd->bps/dot_general | solution.py:74
  122.3 2.2 %fusion.19 = (f32[8,64]{1,0:T(8,128)S(1)}, f32[8,196]{0,1:T(8,128)S(1)}) fusion(f32[8,64,196]{1,0,2:T(8,128)} %copy.43, f32[8,64]{1,0:T(8,128)S(1)} %get-tuple-element.19, f32[8,196,64]{2,0,1:T(8,128)S(1)} %get-tuple-element.24, f32[8,64]{1,0:T(8,128)S(1)} %get-tuple-element.21, f32[8,64,196]{1,0,2:T(8,128)} %copy.45, f32[8,196]{0,1:T(8,128)} %copy-done.9, ...), kind=kLoop, calls=%fused_computation.36 | loop fusion | flops 800736 | bytes 1229184 | tf_op jit(solution)/shard_map/reduce_sum | solution.py:79
  124.6 1.9 %fusion.18 = bf16[8,196,64]{2,0,1:T(8,128)(2,1)S(1)} fusion(f32[8,64,196]{1,0,2:T(8,128)} %copy.45, f32[8,64,196]{1,0,2:T(8,128)S(1)} %copy-done.2, f32[8,196]{0,1:T(8,128)S(1)} %get-tuple-element.17, f32[8,64]{1,0:T(8,128)S(1)} %get-tuple-element.16, f32[8,64]{1,0:T(8,128)S(1)} %get-tuple-element.19, f32[8,196,64]{2,0,1:T(8,128)S(1)} %get-tuple-element.24, ...), kind=kLoop, calls=%fused_computation.33 | loop fusion | flops 1003520 | bytes 1429888 | tf_op jit(solution)/shard_map/convert_element_type | solution.py:84
  128.4 1.7 all_to_all.44
  130.2 10.3 %all-to-all-start.2 = ((f32[256,1,96]{2,1,0:T(1,128)}), f32[256,1,96]{2,1,0:T(1,128)}, u32[]{:S(2)}, u32[]{:S(2)}) async-start(f32[256,1,96]{2,1,0:T(1,128)} %bitcast.82), calls=%async_computation.4 | async-start | bytes 262144 | tf_op jit(solution)/shard_map/all_to_all | solution.py:12
  140.4 2.1 %fusion.29 = f32[8,196,384]{2,1,0:T(8,128)} fusion(bf16[8,196,64]{1,2,0:T(8,128)(2,1)S(1)} %copy.41, bf16[8,64,768]{2,1,0:T(8,128)(2,1)S(1)} %copy-done.3), kind=kOutput, calls=%fused_computation.52 | convolution fusion | flops 77070336 | bytes 3063808 | tf_op jit(solution)/shard_map/bps,bsd->bpd/dot_general | solution.py:85
  142.5 9.8 %all-to-all-done.2 = f32[256,1,96]{2,1,0:T(1,128)} async-done(((f32[256,1,96]{2,1,0:T(1,128)}), f32[256,1,96]{2,1,0:T(1,128)}, u32[]{:S(2)}, u32[]{:S(2)}) %all-to-all-start.2) | async-done | bytes 98336 | tf_op jit(solution)/shard_map/all_to_all | solution.py:12
  152.3 1.2 reduce_sum.49
  154.2 6.6 %all-to-all-start.3 = ((f32[256,1,96]{2,1,0:T(1,128)}), f32[256,1,96]{2,1,0:T(1,128)S(1)}, u32[]{:S(2)}, u32[]{:S(2)}) async-start(f32[256,1,96]{2,1,0:T(1,128)} %broadcast_in_dim.30), calls=%async_computation.5 | async-start | bytes 262144 | tf_op jit(solution)/shard_map/all_to_all | solution.py:14
  160.9 2.4 %add_convert_fusion = bf16[8,196,384]{2,1,0:T(8,128)(2,1)S(1)} fusion(f32[8,196,384]{2,1,0:T(8,128)} %fusion.29, bf16[8,196,64]{2,0,1:T(8,128)(2,1)} %copy-done.4, bf16[384,64]{0,1:T(8,128)(2,1)S(1)} %copy-done.12), kind=kOutput, calls=%fused_computation.14 | convolution fusion | flops 78274560 | bytes 3862528 | tf_op jit(solution)/shard_map/bps,ds->bpd/dot_general | solution.py:88
  164.5 9.0 %all-to-all-done.3 = f32[256,1,96]{2,1,0:T(1,128)S(1)} async-done(((f32[256,1,96]{2,1,0:T(1,128)}), f32[256,1,96]{2,1,0:T(1,128)S(1)}, u32[]{:S(2)}, u32[]{:S(2)}) %all-to-all-start.3) | async-done | bytes 98336 | tf_op jit(solution)/shard_map/all_to_all | solution.py:14
  175.9 1.8 convert_element_type.63
  177.7 1.8 convert_element_type.61
  (45 shorter events, 9.4 us)
Async XLA Ops:
  7.2 43.3 %copy-start = (bf16[2,384,1536]{2,1,0:T(8,128)(2,1)S(1)}, bf16[2,384,1536]{2,1,0:T(8,128)(2,1)}, u32[]{:S(2)}) copy-start(bf16[2,384,1536]{2,1,0:T(8,128)(2,1)} %param.7) | copy-start | bytes 7077892
  7.2 168.7 %reduce-scatter.5.cloned.1.call-start = ((), (), s32[]{:S(2)}) async-start(), calls=%async_computation.7 | async-start | bytes 2654208 | tf_op jit(solution)/shard_map/reduce_scatter | solution.py:71
  9.8 1.3 copy-start.9
  50.5 1.0 copy-start.5
  51.5 1.7 copy-start.7
  56.0 121.7 %reduce-scatter.3.cloned.1.call-start = ((), (), s32[]{:S(2)}) async-start(), calls=%async_computation.6 | async-start | bytes 2654208 | tf_op jit(solution)/shard_map/reduce_scatter | solution.py:68
  56.2 6.5 %copy-start.6 = (bf16[8,32,2,768]{3,0,1,2:T(8,128)(2,1)S(1)}, bf16[8,32,2,768]{3,0,1,2:T(8,128)(2,1)}, u32[]{:S(2)}) copy-start(bf16[8,32,2,768]{3,0,1,2:T(8,128)(2,1)} %copy-done.5) | copy-start | bytes 2359300
  61.5 1.2 copy-start.11
  65.2 2.6 %copy-start.8 = (f32[256,2,1536]{2,0,1:T(8,128)S(1)}, f32[256,2,1536]{2,0,1:T(8,128)}, u32[]{:S(2)}) copy-start(f32[256,2,1536]{2,0,1:T(8,128)} %copy-done.7) | copy-start | bytes 9437188
  122.3 2.3 %copy-start.2 = (f32[8,64,196]{1,0,2:T(8,128)S(1)}, f32[8,64,196]{1,0,2:T(8,128)}, u32[]{:S(2)}) copy-start(f32[8,64,196]{1,0,2:T(8,128)} %copy.43) | copy-start | bytes 1204228
  122.3 2.3 %copy-start.10 = (f32[8,196]{0,1:T(8,128)S(1)}, f32[8,196]{0,1:T(8,128)}, u32[]{:S(2)}) copy-start(f32[8,196]{0,1:T(8,128)} %copy-done.9) | copy-start | bytes 18820
  122.3 4.9 %copy-start.1 = (bf16[8,196,384]{2,0,1:T(8,128)(2,1)S(1)}, bf16[8,196,384]{2,0,1:T(8,128)(2,1)}, u32[]{:S(2)}) copy-start(bf16[8,196,384]{2,0,1:T(8,128)(2,1)} %param.5) | copy-start | bytes 3612676
  126.5 0.8 copy-start.4
  127.3 13.2 %copy-start.3 = (bf16[8,64,768]{2,1,0:T(8,128)(2,1)S(1)}, bf16[8,64,768]{2,1,0:T(8,128)(2,1)}, u32[]{:S(2)}) copy-start(bf16[8,64,768]{2,1,0:T(8,128)(2,1)} %all_to_all.43) | copy-start | bytes 2359300
  128.4 32.4 %copy-start.12 = (bf16[384,64]{0,1:T(8,128)(2,1)S(1)}, bf16[384,64]{0,1:T(8,128)(2,1)}, u32[]{:S(2)}) copy-start(bf16[384,64]{0,1:T(8,128)(2,1)} %param.6) | copy-start | bytes 147460
  130.2 22.2 %all-to-all-start.2 = ((f32[256,1,96]{2,1,0:T(1,128)}), f32[256,1,96]{2,1,0:T(1,128)}, u32[]{:S(2)}, u32[]{:S(2)}) async-start(f32[256,1,96]{2,1,0:T(1,128)} %bitcast.82), calls=%async_computation.4 | async-start | bytes 262144 | tf_op jit(solution)/shard_map/all_to_all | solution.py:12
  154.2 19.3 %all-to-all-start.3 = ((f32[256,1,96]{2,1,0:T(1,128)}), f32[256,1,96]{2,1,0:T(1,128)S(1)}, u32[]{:S(2)}, u32[]{:S(2)}) async-start(f32[256,1,96]{2,1,0:T(1,128)} %broadcast_in_dim.30), calls=%async_computation.5 | async-start | bytes 262144 | tf_op jit(solution)/shard_map/all_to_all | solution.py:14
Sparse Core Ops, SparseCore 0:
  56.1 55.1 reduce-scatter.4
  113.8 47.9 reduce-scatter.2

commit v6 on v3

--- a/solution.py
+++ b/solution.py
@@ -8,10 +8,20 @@
     count = 1
     for name in axes:
         count *= lax.axis_size(name)
-    pieces = term.reshape(count, term.size // count)
-    mine = jnp.sum(lax.all_to_all(pieces, axes, 0, 0, tiled=True), axis=0, keepdims=True)
-    spread = jnp.broadcast_to(mine, pieces.shape)
-    return lax.all_to_all(spread, axes, 0, 0, tiled=True).reshape(term.shape)
+    bits = count.bit_length() - 1
+    assert 1 << bits == count
+    low = 0
+    while low < bits:
+        width = min(2, bits - low)
+        got = [term] + [
+            lax.ppermute(term, axes, [(i, i ^ (m << low)) for i in range(count)])
+            for m in range(1, 1 << width)
+        ]
+        while len(got) > 1:
+            got = [got[2 * j] + got[2 * j + 1] for j in range(len(got) // 2)]
+        term = got[0]
+        low += width
+    return term
 
 
 def _reduced(value):

time: 186 us -> 177 us (0.952)
  local copies, waits for them, and re-layouts: 19.7 us -> 10.1 us
  waiting for transfers between devices: 19.2 us -> 28.7 us
  matrix products: 34 us -> 28.4 us
  other arithmetic: 11.3 us -> 6.17 us
    ppermute x0 -> x12, waiting for transfers between devices: none -> 28 us  [_sum_everywhere(): lax.ppermute(term, axes, [(i, i ^ m << low) for i in range(count)])]
    all_to_all x2 -> x0, waiting for transfers between devices: 19.1 us -> none  [the longest x1 9.95 us: _sum_everywhere(): lax.all_to_all(pieces, axes, 0, 0, tiled=True)]
    ppermute x0 -> x12, starting transfers between devices: none -> 17.3 us  [_sum_everywhere(): lax.ppermute(term, axes, [(i, i ^ m << low) for i in range(count)])]
    all_to_all x2 -> x0, starting transfers between devices: 15.7 us -> none  [the longest x1 9.11 us: _sum_everywhere(): lax.all_to_all(pieces, axes, 0, 0, tiled=True)]
    dot_general x3 -> x1, local copies, waits for them, and re-layouts: 4.69 us -> 1.47 us  [on_device(): jnp.einsum('bpd,ds->bps', tokens, router, preferred_element_type=jnp.floa...]
    unnamed x34 -> x16, local copies, waits for them, and re-layouts: 5.68 us -> 3.06 us
    reduce_sum x2 -> x0, other arithmetic: 2.57 us -> none  [the longest x1 2.29 us: on_device(): jnp.sum(dispatch * dispatch_grad, axis=1, keepdims=True)]
    dot_general x1, matrix products: 3.02 us -> 1.03 us  [on_device(): jnp.einsum('bps,bsd->bpd', dispatch_low, inputs_grad, preferred_element_t...]
  transfers between devices with their start and end apart: 4 -> 14, of which waited for: 2 -> 9; matrix products, arithmetic and copies ran while one was open for 25% -> 17% of each run, Pallas kernels for 0% -> 0%
where the time goes in v6:
time: 177 us; the launch traced here: 175 us
  blocking collectives  69.8 us (39%)
  waiting for transfers between devices  28.7 us (16%)
  matrix products  28.4 us (16%)
  starting transfers between devices  17.4 us (10%)
  between operations  14.3 us (8%)
  local copies, waits for them, and re-layouts  10.1 us (6%)
  other arithmetic  6.17 us (3%)
    all_to_all x1, blocking collectives, on_device(): lax.all_to_all(jnp.stack([outputs_here, input_grad_here]), 'expert', spli...  36.1 us
    all_to_all x1, blocking collectives, on_device(): lax.all_to_all(jnp.stack([slots, slot_grads]), 'expert', split_axis=2, co...  33.7 us
    ppermute x12, waiting for transfers between devices, _sum_everywhere(): lax.ppermute(term, axes, [(i, i ^ m << low) for i in range(count)])  28 us
    ppermute x12, starting transfers between devices, _sum_everywhere(): lax.ppermute(term, axes, [(i, i ^ m << low) for i in range(count)])  17.3 us
    dot_general x1, matrix products, on_device(): jnp.einsum('rjd,jfd->rjf', grads_here, expert_out, preferred_element_type...  5.2 us
    dot_general x1, matrix products, on_device(): jnp.einsum('rjf,jfd->rjd', activated_low, expert_out, preferred_element_t...  4.63 us
  transfers between devices with their start and end apart: 14, of which 9 were waited for; matrix products, arithmetic and copies ran while one was open for 17% of the time, Pallas kernels for 0%

profile of v6, /device:TPU:32, one launch (start us, length us, event | category | flops | bytes accessed | tf_op | source)
XLA Modules:
  0.0 174.9 jit_solution(3772284920249330646)
XLA Ops:
  7.2 2.8 %fusion.30 = (f32[8,64]{1,0:T(8,128)S(1)}, f32[8,196]{0,1:T(8,128)S(1)}, f32[8,196,64]{2,0,1:T(8,128)}) fusion(bf16[8,196,384]{2,0,1:T(8,128)(2,1)} %param.5, bf16[384,64]{0,1:T(8,128)(2,1)} %param.6), kind=kOutput, calls=%fused_computation.57 | convolution fusion | flops 77268960 | bytes 1663104 | tf_op jit(solution)/shard_map/bpd,ds->bps/dot_general | solution.py:38
  10.1 1.5 copy.36
  11.9 1.9 %fusion.9 = bf16[1,8,64,384]{3,2,1,0:T(8,128)(2,1)S(1)} fusion(bf16[8,196,384]{2,0,1:T(8,128)(2,1)} %param.5, f32[8,196,64]{1,2,0:T(8,128)S(1)} %copy.36, f32[8,64]{1,0:T(8,128)S(1)} %get-tuple-element.16, f32[8,64]{1,0:T(8,128)S(1)} %get-tuple-element.12), kind=kOutput, calls=%fused_computation.23 | convolution fusion | flops 77568000 | bytes 2002944 | tf_op jit(solution)/shard_map/bps,bpd->bsd/dot_general | solution.py:43
  14.8 33.7 %all_to_all.30 = bf16[2,8,64,384]{3,1,0,2:T(8,128)(2,1)S(1)} all-to-all(bf16[2,8,64,384]{3,1,0,2:T(8,128)(2,1)S(1)} %copy.25), channel_id=1, replica_groups=mesh['expert'=32,'dp'=8] {'expert'}, dimensions={2} | all-to-all | bytes 1572864 | tf_op jit(solution)/shard_map/all_to_all | solution.py:49
  49.7 1.6 copy-done.3
  51.3 2.8 %convolution_convert_fusion = bf16[2,1536,384]{2,1,0:T(8,128)(2,1)} fusion(bf16[2,32,8,2,384]{4,2,1,3,0:T(8,128)(2,1)S(1)} %bitcast.74, f32[256,2,1536]{2,0,1:T(8,128)S(1)} %convolution_bitcast_fusion.1), kind=kOutput, calls=%fused_computation.2 | convolution fusion | flops 612237312 | bytes 5898240 | tf_op jit(solution)/shard_map/rjf,rjd->jfd/dot_general | solution.py:73
  54.2 5.2 %fusion.6 = bf16[256,2,1536]{2,0,1:T(8,128)(2,1)S(1)} fusion(f32[256,2,1536]{2,0,1:T(8,128)} %copy-done.3, bf16[2,1536,384]{2,1,0:T(8,128)(2,1)} %param.8, bf16[2,32,8,2,384]{4,2,1,3,0:T(8,128)(2,1)} %bitcast.75), kind=kOutput, calls=%fused_computation.12 | convolution fusion | flops 619708416 | bytes 7471104 | tf_op jit(solution)/shard_map/rjd,jfd->rjf/dot_general | solution.py:59
  59.4 1.0 fusion.8
  60.5 2.5 %convolution_convert_fusion.1 = bf16[2,384,1536]{1,2,0:T(8,128)(2,1)} fusion(bf16[256,2,1536]{2,0,1:T(8,128)(2,1)S(1)} %fusion.6, bf16[2,32,8,2,384]{4,2,1,3,0:T(8,128)(2,1)S(1)} %bitcast.76), kind=kOutput, calls=%fused_computation.3 | convolution fusion | flops 605159424 | bytes 4325376 | tf_op jit(solution)/shard_map/rjd,rjf->jdf/dot_general | solution.py:70
  63.0 4.6 %fusion.7 = bf16[1,256,2,384]{3,1,2,0:T(8,128)(2,1)} fusion(bf16[2,1536,384]{2,1,0:T(8,128)(2,1)} %param.8, f32[256,2,1536]{2,0,1:T(8,128)} %copy-done.3), kind=kOutput, calls=%fused_computation.21 | convolution fusion | flops 611254272 | bytes 5898240 | tf_op jit(solution)/shard_map/rjf,jfd->rjd/dot_general | solution.py:56
  67.7 1.1 pad_maximum_fusion.1
  69.6 36.1 %all_to_all.31 = bf16[2,256,2,384]{3,2,0,1:T(2,128)(2,1)S(1)} all-to-all(bf16[2,256,2,384]{3,2,0,1:T(2,128)(2,1)S(1)} %copy.27), channel_id=1, replica_groups=mesh['expert'=32,'dp'=8] {'expert'}, dimensions={1} | all-to-all | bytes 1572864 | tf_op jit(solution)/shard_map/all_to_all | solution.py:66
  106.4 1.5 fusion.31
  108.7 1.1 squeeze.14
  109.9 2.0 %convolution_bitcast_fusion.2 = f32[8,196,64]{1,2,0:T(8,128)S(1)} fusion(bf16[8,64,384]{2,1,0:T(8,128)(2,1)} %squeeze.15, bf16[8,196,384]{2,0,1:T(8,128)(2,1)} %param.9), kind=kOutput, calls=%fused_computation.19 | convolution fusion | flops 77070336 | bytes 1998848 | tf_op jit(solution)/shard_map/bpd,bsd->bps/dot_general | solution.py:82
  111.9 2.1 %multiply_reduce_fusion.1 = (f32[8,64]{1,0:T(8,128)S(1)}, f32[8,196]{1,0:T(8,128)S(1)}, f32[8,196,64]{1,2,0:T(8,128)S(1)}) fusion(f32[8,64]{1,0:T(8,128)S(1)} %get-tuple-element.16, f32[8,196,64]{1,2,0:T(8,128)S(1)} %copy.36, f32[8,64]{1,0:T(8,128)S(1)} %get-tuple-element.12, f32[8,196,64]{1,2,0:T(8,128)S(1)} %convolution_bitcast_fusion.2, ...), kind=kOutput, calls=%fused_computation.37 | convolution fusion | flops 77871072 | bytes 2826624 | tf_op jit(solution)/shard_map/bpd,bsd->bps/dot_general | solution.py:83
  114.8 3.3 %collective-permute-start.2 = (f32[384,64]{0,1:T(8,128)S(1)}, f32[384,64]{0,1:T(8,128)S(1)}, u32[]{:S(2)}, u32[]{:S(2)}) collective-permute-start(f32[384,64]{0,1:T(8,128)S(1)} %convolution_bitcast_fusion.4), channel_id=1, source_target_pairs={{0,3},{1,2},{2,1},{3,0},{4,7},{5,6},{6,5},{7,4},{8,11},{9,10},{10,... | collective-permute-start | bytes 294920 | tf_op jit(solution)/shard_map/ppermute | solution.py:17
  119.1 3.5 %collective-permute-done.2 = f32[384,64]{0,1:T(8,128)S(1)} collective-permute-done((f32[384,64]{0,1:T(8,128)S(1)}, f32[384,64]{0,1:T(8,128)S(1)}, u32[]{:S(2)}, u32[]{:S(2)}) %collective-permute-start.2) | collective-permute-done | bytes 98336 | tf_op jit(solution)/shard_map/ppermute | solution.py:17
  122.6 2.6 %collective-permute-done.1 = f32[384,64]{0,1:T(8,128)S(1)} collective-permute-done((f32[384,64]{0,1:T(8,128)S(1)}, f32[384,64]{0,1:T(8,128)S(1)}, u32[]{:S(2)}, u32[]{:S(2)}) %collective-permute-start.1) | collective-permute-done | bytes 98336 | tf_op jit(solution)/shard_map/ppermute | solution.py:17
  126.2 1.3 collective-permute-start.3
  127.5 2.9 %collective-permute-done.5 = f32[384,64]{0,1:T(8,128)S(1)} collective-permute-done((f32[384,64]{0,1:T(8,128)S(1)}, f32[384,64]{0,1:T(8,128)S(1)}, u32[]{:S(2)}, u32[]{:S(2)}) %collective-permute-start.5) | collective-permute-done | bytes 98336 | tf_op jit(solution)/shard_map/ppermute | solution.py:17
  130.4 3.9 %collective-permute-done.3 = f32[384,64]{0,1:T(8,128)S(1)} collective-permute-done((f32[384,64]{0,1:T(8,128)S(1)}, f32[384,64]{0,1:T(8,128)S(1)}, u32[]{:S(2)}, u32[]{:S(2)}) %collective-permute-start.3) | collective-permute-done | bytes 98336 | tf_op jit(solution)/shard_map/ppermute | solution.py:17
  134.3 2.8 %collective-permute-start.8 = (f32[384,64]{0,1:T(8,128)S(1)}, f32[384,64]{0,1:T(8,128)S(1)}, u32[]{:S(2)}, u32[]{:S(2)}) collective-permute-start(f32[384,64]{0,1:T(8,128)S(1)} %add_add_fusion.2), channel_id=1, source_target_pairs={{0,48},{1,49},{2,50},{3,51},{4,52},{5,53},{6,54},{7,55},{8,56},{9,... | collective-permute-start | bytes 294920 | tf_op jit(solution)/shard_map/ppermute | solution.py:17
  138.5 1.0 fusion.21
  139.5 2.1 %collective-permute-done.8 = f32[384,64]{0,1:T(8,128)S(1)} collective-permute-done((f32[384,64]{0,1:T(8,128)S(1)}, f32[384,64]{0,1:T(8,128)S(1)}, u32[]{:S(2)}, u32[]{:S(2)}) %collective-permute-start.8) | collective-permute-done | bytes 98336 | tf_op jit(solution)/shard_map/ppermute | solution.py:17
  141.6 2.6 %collective-permute-done.7 = f32[384,64]{0,1:T(8,128)S(1)} collective-permute-done((f32[384,64]{0,1:T(8,128)S(1)}, f32[384,64]{0,1:T(8,128)S(1)}, u32[]{:S(2)}, u32[]{:S(2)}) %collective-permute-start.7) | collective-permute-done | bytes 98336 | tf_op jit(solution)/shard_map/ppermute | solution.py:17
  144.9 4.1 %collective-permute-start.10 = (f32[384,64]{0,1:T(8,128)S(1)}, f32[384,64]{0,1:T(8,128)S(1)}, u32[]{:S(2)}, u32[]{:S(2)}) collective-permute-start(f32[384,64]{0,1:T(8,128)S(1)} %add_add_fusion.1), channel_id=1, source_target_pairs={{0,128},{1,129},{2,130},{3,131},{4,132},{5,133},{6,134},{7,135},{8... | collective-permute-start | bytes 294920 | tf_op jit(solution)/shard_map/ppermute | solution.py:17
  148.9 1.9 %collective-permute-start.9 = (f32[384,64]{0,1:T(8,128)S(1)}, f32[384,64]{0,1:T(8,128)S(1)}, u32[]{:S(2)}, u32[]{:S(2)}) collective-permute-start(f32[384,64]{0,1:T(8,128)S(1)} %add_add_fusion.1), channel_id=1, source_target_pairs={{0,64},{1,65},{2,66},{3,67},{4,68},{5,69},{6,70},{7,71},{8,72},{9,... | collective-permute-start | bytes 294920 | tf_op jit(solution)/shard_map/ppermute | solution.py:17
  151.5 1.2 copy.34
  152.6 10.0 %collective-permute-done.10 = f32[384,64]{0,1:T(8,128)S(1)} collective-permute-done((f32[384,64]{0,1:T(8,128)S(1)}, f32[384,64]{0,1:T(8,128)S(1)}, u32[]{:S(2)}, u32[]{:S(2)}) %collective-permute-start.10) | collective-permute-done | bytes 98336 | tf_op jit(solution)/shard_map/ppermute | solution.py:17
  163.7 1.8 %convert_element_type.63 = f32[2,192,384]{2,1,0:T(8,128)} convert(bf16[2,192,384]{2,1,0:T(8,128)(2,1)} %reduce-scatter.5.cloned.1.call-done) | non-fusion elementwise | flops 147456 | bytes 884736 | tf_op jit(solution)/shard_map/convert_element_type | solution.py:81
  166.2 1.8 %convert_element_type.61 = f32[2,384,192]{1,2,0:T(8,128)} convert(bf16[2,384,192]{1,2,0:T(8,128)(2,1)} %reduce-scatter.3.cloned.1.call-done) | non-fusion elementwise | flops 147456 | bytes 884736 | tf_op jit(solution)/shard_map/convert_element_type | solution.py:78
  (48 shorter events, 12.2 us)
Async XLA Ops:
  7.2 41.5 %copy-start = (bf16[2,384,1536]{2,1,0:T(8,128)(2,1)S(1)}, bf16[2,384,1536]{2,1,0:T(8,128)(2,1)}, u32[]{:S(2)}) copy-start(bf16[2,384,1536]{2,1,0:T(8,128)(2,1)} %param.7) | copy-start | bytes 7077892
  7.2 156.5 %reduce-scatter.5.cloned.1.call-start = ((), (), s32[]{:S(2)}) async-start(), calls=%async_computation.5 | async-start | bytes 2654208 | tf_op jit(solution)/shard_map/reduce_scatter | solution.py:79
  11.6 2.2 %copy-start.4 = (bf16[8,196,384]{2,0,1:T(8,128)(2,1)S(1)}, bf16[8,196,384]{2,0,1:T(8,128)(2,1)}, u32[]{:S(2)}) copy-start(bf16[8,196,384]{2,0,1:T(8,128)(2,1)} %param.9) | copy-start | bytes 3612676
  48.7 1.0 copy-start.1
  49.7 1.7 copy-start.3
  54.2 112.0 %reduce-scatter.3.cloned.1.call-start = ((), (), s32[]{:S(2)}) async-start(), calls=%async_computation.4 | async-start | bytes 2654208 | tf_op jit(solution)/shard_map/reduce_scatter | solution.py:76
  59.4 1.1 copy-start.2
  111.9 2.5 %copy-start.5 = (bf16[8,196,384]{2,0,1:T(8,128)(2,1)S(1)}, bf16[8,196,384]{2,0,1:T(8,128)(2,1)}, u32[]{:S(2)}) copy-start(bf16[8,196,384]{2,0,1:T(8,128)(2,1)} %param.5) | copy-start | bytes 3612676
  114.8 36.0 %copy-start.6 = (bf16[384,64]{0,1:T(8,128)(2,1)S(1)}, bf16[384,64]{0,1:T(8,128)(2,1)}, u32[]{:S(2)}) copy-start(bf16[384,64]{0,1:T(8,128)(2,1)} %param.6) | copy-start | bytes 147460
  114.8 7.8 %collective-permute-start.2 = (f32[384,64]{0,1:T(8,128)S(1)}, f32[384,64]{0,1:T(8,128)S(1)}, u32[]{:S(2)}, u32[]{:S(2)}) collective-permute-start(f32[384,64]{0,1:T(8,128)S(1)} %convolution_bitcast_fusion.4), channel_id=1, source_target_pairs={{0,3},{1,2},{2,1},{3,0},{4,7},{5,6},{6,5},{7,4},{8,11},{9,10},{10,... | collective-permute-start | bytes 294920 | tf_op jit(solution)/shard_map/ppermute | solution.py:17
  118.2 7.1 %collective-permute-start.1 = (f32[384,64]{0,1:T(8,128)S(1)}, f32[384,64]{0,1:T(8,128)S(1)}, u32[]{:S(2)}, u32[]{:S(2)}) collective-permute-start(f32[384,64]{0,1:T(8,128)S(1)} %convolution_bitcast_fusion.4), channel_id=1, source_target_pairs={{0,2},{1,3},{2,0},{3,1},{4,6},{5,7},{6,4},{7,5},{8,10},{9,11},{10,... | collective-permute-start | bytes 294920 | tf_op jit(solution)/shard_map/ppermute | solution.py:17
  118.2 7.1 %collective-permute-start = (f32[384,64]{0,1:T(8,128)S(1)}, f32[384,64]{0,1:T(8,128)S(1)}, u32[]{:S(2)}, u32[]{:S(2)}) collective-permute-start(f32[384,64]{0,1:T(8,128)S(1)} %convolution_bitcast_fusion.4), channel_id=1, source_target_pairs={{0,1},{1,0},{2,3},{3,2},{4,5},{5,4},{6,7},{7,6},{8,9},{9,8},{10,11... | collective-permute-start | bytes 294920 | tf_op jit(solution)/shard_map/ppermute | solution.py:17
  125.3 5.2 %collective-permute-start.5 = (f32[384,64]{0,1:T(8,128)S(1)}, f32[384,64]{0,1:T(8,128)S(1)}, u32[]{:S(2)}, u32[]{:S(2)}) collective-permute-start(f32[384,64]{0,1:T(8,128)S(1)} %add_add_fusion.3), channel_id=1, source_target_pairs={{0,12},{1,13},{2,14},{3,15},{4,8},{5,9},{6,10},{7,11},{8,4},{9,5},... | collective-permute-start | bytes 294920 | tf_op jit(solution)/shard_map/ppermute | solution.py:17
  125.4 5.1 %collective-permute-start.4 = (f32[384,64]{0,1:T(8,128)S(1)}, f32[384,64]{0,1:T(8,128)S(1)}, u32[]{:S(2)}, u32[]{:S(2)}) collective-permute-start(f32[384,64]{0,1:T(8,128)S(1)} %add_add_fusion.3), channel_id=1, source_target_pairs={{0,8},{1,9},{2,10},{3,11},{4,12},{5,13},{6,14},{7,15},{8,0},{9,1},... | collective-permute-start | bytes 294920 | tf_op jit(solution)/shard_map/ppermute | solution.py:17
  126.2 8.1 %collective-permute-start.3 = (f32[384,64]{0,1:T(8,128)S(1)}, f32[384,64]{0,1:T(8,128)S(1)}, u32[]{:S(2)}, u32[]{:S(2)}) collective-permute-start(f32[384,64]{0,1:T(8,128)S(1)} %add_add_fusion.3), channel_id=1, source_target_pairs={{0,4},{1,5},{2,6},{3,7},{4,0},{5,1},{6,2},{7,3},{8,12},{9,13},{10,... | collective-permute-start | bytes 294920 | tf_op jit(solution)/shard_map/ppermute | solution.py:17
  134.3 7.3 %collective-permute-start.8 = (f32[384,64]{0,1:T(8,128)S(1)}, f32[384,64]{0,1:T(8,128)S(1)}, u32[]{:S(2)}, u32[]{:S(2)}) collective-permute-start(f32[384,64]{0,1:T(8,128)S(1)} %add_add_fusion.2), channel_id=1, source_target_pairs={{0,48},{1,49},{2,50},{3,51},{4,52},{5,53},{6,54},{7,55},{8,56},{9,... | collective-permute-start | bytes 294920 | tf_op jit(solution)/shard_map/ppermute | solution.py:17
  137.1 7.1 %collective-permute-start.7 = (f32[384,64]{0,1:T(8,128)S(1)}, f32[384,64]{0,1:T(8,128)S(1)}, u32[]{:S(2)}, u32[]{:S(2)}) collective-permute-start(f32[384,64]{0,1:T(8,128)S(1)} %add_add_fusion.2), channel_id=1, source_target_pairs={{0,32},{1,33},{2,34},{3,35},{4,36},{5,37},{6,38},{7,39},{8,40},{9,... | collective-permute-start | bytes 294920 | tf_op jit(solution)/shard_map/ppermute | solution.py:17
  138.0 6.2 %collective-permute-start.6 = (f32[384,64]{0,1:T(8,128)S(1)}, f32[384,64]{0,1:T(8,128)S(1)}, u32[]{:S(2)}, u32[]{:S(2)}) collective-permute-start(f32[384,64]{0,1:T(8,128)S(1)} %add_add_fusion.2), channel_id=1, source_target_pairs={{0,16},{1,17},{2,18},{3,19},{4,20},{5,21},{6,22},{7,23},{8,24},{9,... | collective-permute-start | bytes 294920 | tf_op jit(solution)/shard_map/ppermute | solution.py:17
  144.2 8.4 %collective-permute-start.11 = (f32[384,64]{0,1:T(8,128)S(1)}, f32[384,64]{0,1:T(8,128)S(1)}, u32[]{:S(2)}, u32[]{:S(2)}) collective-permute-start(f32[384,64]{0,1:T(8,128)S(1)} %add_add_fusion.1), channel_id=1, source_target_pairs={{0,192},{1,193},{2,194},{3,195},{4,196},{5,197},{6,198},{7,199},{8... | collective-permute-start | bytes 294920 | tf_op jit(solution)/shard_map/ppermute | solution.py:17
  144.9 17.8 %collective-permute-start.10 = (f32[384,64]{0,1:T(8,128)S(1)}, f32[384,64]{0,1:T(8,128)S(1)}, u32[]{:S(2)}, u32[]{:S(2)}) collective-permute-start(f32[384,64]{0,1:T(8,128)S(1)} %add_add_fusion.1), channel_id=1, source_target_pairs={{0,128},{1,129},{2,130},{3,131},{4,132},{5,133},{6,134},{7,135},{8... | collective-permute-start | bytes 294920 | tf_op jit(solution)/shard_map/ppermute | solution.py:17
  148.9 14.1 %collective-permute-start.9 = (f32[384,64]{0,1:T(8,128)S(1)}, f32[384,64]{0,1:T(8,128)S(1)}, u32[]{:S(2)}, u32[]{:S(2)}) collective-permute-start(f32[384,64]{0,1:T(8,128)S(1)} %add_add_fusion.1), channel_id=1, source_target_pairs={{0,64},{1,65},{2,66},{3,67},{4,68},{5,69},{6,70},{7,71},{8,72},{9,... | collective-permute-start | bytes 294920 | tf_op jit(solution)/shard_map/ppermute | solution.py:17
Sparse Core Ops, SparseCore 0:
  54.3 55.0 reduce-scatter.4
  111.9 54.2 reduce-scatter.2

commit v7 on v6

--- a/solution.py
+++ b/solution.py
@@ -35,16 +35,16 @@
 
 
 def on_device(tokens, router, expert_in, expert_out, out_grad):
-    logits = jnp.einsum("bpd,ds->bps", tokens, router, preferred_element_type=jnp.float32)
-    dispatch = _softmax(logits, 1)
-    combine = _softmax(logits, 2)
+    logits = jnp.einsum("bpd,ds->bsp", tokens, router, preferred_element_type=jnp.float32)
+    dispatch = _softmax(logits, 2)
+    combine = _softmax(logits, 1)
     dispatch_low = dispatch.astype(jnp.bfloat16)
     combine_low = combine.astype(jnp.bfloat16)
     slots = jnp.einsum(
-        "bps,bpd->bsd", dispatch_low, tokens, preferred_element_type=jnp.float32
+        "bsp,bpd->bsd", dispatch_low, tokens, preferred_element_type=jnp.float32
     ).astype(jnp.bfloat16)
     slot_grads = jnp.einsum(
-        "bps,bpd->bsd", combine_low, out_grad, preferred_element_type=jnp.float32
+        "bsp,bpd->bsd", combine_low, out_grad, preferred_element_type=jnp.float32
     ).astype(jnp.bfloat16)
     sent = lax.all_to_all(
         jnp.stack([slots, slot_grads]), "expert", split_axis=2, concat_axis=1, tiled=True
@@ -79,23 +79,23 @@
     grad_out = lax.psum_scatter(
         second_term.astype(jnp.bfloat16), "dp", scatter_dimension=1, tiled=True
     ).astype(jnp.float32)
-    combine_grad = jnp.einsum("bpd,bsd->bps", out_grad, outputs, preferred_element_type=jnp.float32)
+    combine_grad = jnp.einsum("bpd,bsd->bsp", out_grad, outputs, preferred_element_type=jnp.float32)
     dispatch_grad = jnp.einsum(
-        "bpd,bsd->bps", tokens, inputs_grad, preferred_element_type=jnp.float32
+        "bpd,bsd->bsp", tokens, inputs_grad, preferred_element_type=jnp.float32
     )
     logit_grad = dispatch * (
-        dispatch_grad - _reduced(jnp.sum(dispatch * dispatch_grad, axis=1, keepdims=True))
+        dispatch_grad - _reduced(jnp.sum(dispatch * dispatch_grad, axis=2, keepdims=True))
     )
     logit_grad = logit_grad + combine * (
-        combine_grad - _reduced(jnp.sum(combine * combine_grad, axis=2, keepdims=True))
+        combine_grad - _reduced(jnp.sum(combine * combine_grad, axis=1, keepdims=True))
     )
     logit_low = logit_grad.astype(jnp.bfloat16)
     first_part = jnp.einsum(
-        "bps,bsd->bpd", dispatch_low, inputs_grad, preferred_element_type=jnp.float32
+        "bsp,bsd->bpd", dispatch_low, inputs_grad, preferred_element_type=jnp.float32
     )
-    second_part = jnp.einsum("bps,ds->bpd", logit_low, router, preferred_element_type=jnp.float32)
+    second_part = jnp.einsum("bsp,ds->bpd", logit_low, router, preferred_element_type=jnp.float32)
     grad_tokens = (first_part + second_part).astype(jnp.bfloat16)
-    router_term = jnp.einsum("bpd,bps->ds", tokens, logit_low, preferred_element_type=jnp.float32)
+    router_term = jnp.einsum("bpd,bsp->ds", tokens, logit_low, preferred_element_type=jnp.float32)
     grad_router = _sum_everywhere(router_term, ("expert", "dp"))
     return (grad_tokens, grad_in, grad_out, grad_router)
 

time: 177 us -> 175 us (0.989)
  no operation moved by 1% of the time
where the time goes in v7:
time: 175 us; the launch traced here: 173 us
  blocking collectives  70 us (40%)
  waiting for transfers between devices  28.8 us (16%)
  matrix products  27.8 us (16%)
  starting transfers between devices  17.2 us (10%)
  between operations  14.3 us (8%)
  local copies, waits for them, and re-layouts  8.57 us (5%)
  other arithmetic  6.18 us (4%)
    all_to_all x1, blocking collectives, on_device(): lax.all_to_all(jnp.stack([outputs_here, input_grad_here]), 'expert', spli...  36.2 us
    all_to_all x1, blocking collectives, on_device(): lax.all_to_all(jnp.stack([slots, slot_grads]), 'expert', split_axis=2, co...  33.7 us
    ppermute x12, waiting for transfers between devices, _sum_everywhere(): lax.ppermute(term, axes, [(i, i ^ m << low) for i in range(count)])  28.1 us
    ppermute x12, starting transfers between devices, _sum_everywhere(): lax.ppermute(term, axes, [(i, i ^ m << low) for i in range(count)])  17.2 us
    dot_general x1, matrix products, on_device(): jnp.einsum('rjd,jfd->rjf', grads_here, expert_out, preferred_element_type...  5.2 us
    dot_general x1, matrix products, on_device(): jnp.einsum('rjf,jfd->rjd', activated_low, expert_out, preferred_element_t...  4.62 us
  transfers between devices with their start and end apart: 14, of which 9 were waited for; matrix products, arithmetic and copies ran while one was open for 17% of the time, Pallas kernels for 0%

profile of v7, /device:TPU:32, one launch (start us, length us, event | category | flops | bytes accessed | tf_op | source)
XLA Modules:
  0.0 172.9 jit_solution(17974045177599685051)
XLA Ops:
  7.2 2.2 %fusion.32 = (f32[8,64]{1,0:T(8,128)S(1)}, f32[8,196]{1,0:T(8,128)S(1)}, f32[8,64,196]{2,1,0:T(8,128)S(1)}) fusion(bf16[8,196,384]{2,0,1:T(8,128)(2,1)} %param.5, bf16[384,64]{0,1:T(8,128)(2,1)} %param.6), kind=kOutput, calls=%fused_computation.58 | convolution fusion | flops 77268960 | bytes 1663104 | tf_op jit(solution)/shard_map/bpd,ds->bsp/dot_general | solution.py:38
  9.7 1.9 %fusion.9 = bf16[1,8,64,384]{3,2,1,0:T(8,128)(2,1)S(1)} fusion(bf16[8,196,384]{2,0,1:T(8,128)(2,1)} %param.5, f32[8,64,196]{2,1,0:T(8,128)S(1)} %get-tuple-element.20, f32[8,64]{1,0:T(8,128)S(1)} %get-tuple-element.14, f32[8,64]{1,0:T(8,128)S(1)} %get-tuple-element.16), kind=kOutput, calls=%fused_computation.22 | convolution fusion | flops 77568000 | bytes 2002944 | tf_op jit(solution)/shard_map/bsp,bpd->bsd/dot_general | solution.py:43
  12.7 33.7 %all_to_all.30 = bf16[2,8,64,384]{3,1,0,2:T(8,128)(2,1)S(1)} all-to-all(bf16[2,8,64,384]{3,1,0,2:T(8,128)(2,1)S(1)} %copy.25), channel_id=1, replica_groups=mesh['expert'=32,'dp'=8] {'expert'}, dimensions={2} | all-to-all | bytes 1572864 | tf_op jit(solution)/shard_map/all_to_all | solution.py:49
  47.5 1.6 copy-done.3
  49.2 2.8 %convolution_convert_fusion = bf16[2,1536,384]{2,1,0:T(8,128)(2,1)} fusion(bf16[2,32,8,2,384]{4,2,1,3,0:T(8,128)(2,1)S(1)} %bitcast.71, f32[256,2,1536]{2,0,1:T(8,128)S(1)} %convolution_bitcast_fusion.1), kind=kOutput, calls=%fused_computation.2 | convolution fusion | flops 612237312 | bytes 5898240 | tf_op jit(solution)/shard_map/rjf,rjd->jfd/dot_general | solution.py:73
  52.1 5.2 %fusion.6 = bf16[256,2,1536]{2,0,1:T(8,128)(2,1)S(1)} fusion(f32[256,2,1536]{2,0,1:T(8,128)} %copy-done.3, bf16[2,1536,384]{2,1,0:T(8,128)(2,1)} %param.8, bf16[2,32,8,2,384]{4,2,1,3,0:T(8,128)(2,1)} %bitcast.72), kind=kOutput, calls=%fused_computation.12 | convolution fusion | flops 619708416 | bytes 7471104 | tf_op jit(solution)/shard_map/rjd,jfd->rjf/dot_general | solution.py:59
  57.3 1.0 fusion.8
  58.4 2.5 %convolution_convert_fusion.1 = bf16[2,384,1536]{1,2,0:T(8,128)(2,1)} fusion(bf16[256,2,1536]{2,0,1:T(8,128)(2,1)S(1)} %fusion.6, bf16[2,32,8,2,384]{4,2,1,3,0:T(8,128)(2,1)S(1)} %bitcast.73), kind=kOutput, calls=%fused_computation.3 | convolution fusion | flops 605159424 | bytes 4325376 | tf_op jit(solution)/shard_map/rjd,rjf->jdf/dot_general | solution.py:70
  60.9 4.6 %fusion.7 = bf16[1,256,2,384]{3,1,2,0:T(8,128)(2,1)} fusion(bf16[2,1536,384]{2,1,0:T(8,128)(2,1)} %param.8, f32[256,2,1536]{2,0,1:T(8,128)} %copy-done.3), kind=kOutput, calls=%fused_computation.20 | convolution fusion | flops 611254272 | bytes 5898240 | tf_op jit(solution)/shard_map/rjf,jfd->rjd/dot_general | solution.py:56
  65.5 1.1 pad_maximum_fusion.1
  67.4 36.2 %all_to_all.31 = bf16[2,256,2,384]{3,2,0,1:T(2,128)(2,1)S(1)} all-to-all(bf16[2,256,2,384]{3,2,0,1:T(2,128)(2,1)S(1)} %copy.27), channel_id=1, replica_groups=mesh['expert'=32,'dp'=8] {'expert'}, dimensions={1} | all-to-all | bytes 1572864 | tf_op jit(solution)/shard_map/all_to_all | solution.py:66
  104.4 1.5 fusion.33
  106.7 1.1 squeeze.14
  107.9 2.0 %fusion.11 = f32[8,64,196]{2,1,0:T(8,128)S(1)} fusion(bf16[8,64,384]{2,1,0:T(8,128)(2,1)} %squeeze.15, bf16[8,196,384]{2,0,1:T(8,128)(2,1)} %param.9), kind=kOutput, calls=%fused_computation.25 | convolution fusion | flops 77070336 | bytes 1998848 | tf_op jit(solution)/shard_map/bpd,bsd->bsp/dot_general | solution.py:82
  109.9 2.1 %multiply_reduce_fusion.1 = (f32[8,64]{1,0:T(8,128)S(1)}, f32[8,196]{1,0:T(8,128)S(1)}, f32[8,64,196]{2,1,0:T(8,128)S(1)}) fusion(f32[8,64]{1,0:T(8,128)S(1)} %get-tuple-element.14, f32[8,64,196]{2,1,0:T(8,128)S(1)} %get-tuple-element.20, f32[8,64]{1,0:T(8,128)S(1)} %get-tuple-element.16, f32[8,64,196]{2,1,0:T(8,128)S(1)} %fusion.11, ...), kind=kOutput, calls=%fused_computation.39 | convolution fusion | flops 77871072 | bytes 2826624 | tf_op jit(solution)/shard_map/bpd,bsd->bsp/dot_general | solution.py:83
  112.8 3.2 %collective-permute-start.2 = (f32[384,64]{0,1:T(8,128)S(1)}, f32[384,64]{0,1:T(8,128)S(1)}, u32[]{:S(2)}, u32[]{:S(2)}) collective-permute-start(f32[384,64]{0,1:T(8,128)S(1)} %convolution_bitcast_fusion.3), channel_id=1, source_target_pairs={{0,3},{1,2},{2,1},{3,0},{4,7},{5,6},{6,5},{7,4},{8,11},{9,10},{10,... | collective-permute-start | bytes 294920 | tf_op jit(solution)/shard_map/ppermute | solution.py:17
  116.0 1.0 collective-permute-start
  117.0 3.4 %collective-permute-done.2 = f32[384,64]{0,1:T(8,128)S(1)} collective-permute-done((f32[384,64]{0,1:T(8,128)S(1)}, f32[384,64]{0,1:T(8,128)S(1)}, u32[]{:S(2)}, u32[]{:S(2)}) %collective-permute-start.2) | collective-permute-done | bytes 98336 | tf_op jit(solution)/shard_map/ppermute | solution.py:17
  120.5 2.6 %collective-permute-done.1 = f32[384,64]{0,1:T(8,128)S(1)} collective-permute-done((f32[384,64]{0,1:T(8,128)S(1)}, f32[384,64]{0,1:T(8,128)S(1)}, u32[]{:S(2)}, u32[]{:S(2)}) %collective-permute-start.1) | collective-permute-done | bytes 98336 | tf_op jit(solution)/shard_map/ppermute | solution.py:17
  124.1 1.2 collective-permute-start.3
  125.4 2.7 %collective-permute-done.5 = f32[384,64]{0,1:T(8,128)S(1)} collective-permute-done((f32[384,64]{0,1:T(8,128)S(1)}, f32[384,64]{0,1:T(8,128)S(1)}, u32[]{:S(2)}, u32[]{:S(2)}) %collective-permute-start.5) | collective-permute-done | bytes 98336 | tf_op jit(solution)/shard_map/ppermute | solution.py:17
  128.1 4.0 %collective-permute-done.3 = f32[384,64]{0,1:T(8,128)S(1)} collective-permute-done((f32[384,64]{0,1:T(8,128)S(1)}, f32[384,64]{0,1:T(8,128)S(1)}, u32[]{:S(2)}, u32[]{:S(2)}) %collective-permute-start.3) | collective-permute-done | bytes 98336 | tf_op jit(solution)/shard_map/ppermute | solution.py:17
  132.1 2.9 %collective-permute-start.8 = (f32[384,64]{0,1:T(8,128)S(1)}, f32[384,64]{0,1:T(8,128)S(1)}, u32[]{:S(2)}, u32[]{:S(2)}) collective-permute-start(f32[384,64]{0,1:T(8,128)S(1)} %add_add_fusion.2), channel_id=1, source_target_pairs={{0,48},{1,49},{2,50},{3,51},{4,52},{5,53},{6,54},{7,55},{8,56},{9,... | collective-permute-start | bytes 294920 | tf_op jit(solution)/shard_map/ppermute | solution.py:17
  136.3 1.0 fusion.24
  137.3 2.2 %collective-permute-done.8 = f32[384,64]{0,1:T(8,128)S(1)} collective-permute-done((f32[384,64]{0,1:T(8,128)S(1)}, f32[384,64]{0,1:T(8,128)S(1)}, u32[]{:S(2)}, u32[]{:S(2)}) %collective-permute-start.8) | collective-permute-done | bytes 98336 | tf_op jit(solution)/shard_map/ppermute | solution.py:17
  139.5 2.6 %collective-permute-done.7 = f32[384,64]{0,1:T(8,128)S(1)} collective-permute-done((f32[384,64]{0,1:T(8,128)S(1)}, f32[384,64]{0,1:T(8,128)S(1)}, u32[]{:S(2)}, u32[]{:S(2)}) %collective-permute-start.7) | collective-permute-done | bytes 98336 | tf_op jit(solution)/shard_map/ppermute | solution.py:17
  142.7 4.0 %collective-permute-start.10 = (f32[384,64]{0,1:T(8,128)S(1)}, f32[384,64]{0,1:T(8,128)S(1)}, u32[]{:S(2)}, u32[]{:S(2)}) collective-permute-start(f32[384,64]{0,1:T(8,128)S(1)} %add_add_fusion.1), channel_id=1, source_target_pairs={{0,128},{1,129},{2,130},{3,131},{4,132},{5,133},{6,134},{7,135},{8... | collective-permute-start | bytes 294920 | tf_op jit(solution)/shard_map/ppermute | solution.py:17
  146.7 2.1 %collective-permute-start.9 = (f32[384,64]{0,1:T(8,128)S(1)}, f32[384,64]{0,1:T(8,128)S(1)}, u32[]{:S(2)}, u32[]{:S(2)}) collective-permute-start(f32[384,64]{0,1:T(8,128)S(1)} %add_add_fusion.1), channel_id=1, source_target_pairs={{0,64},{1,65},{2,66},{3,67},{4,68},{5,69},{6,70},{7,71},{8,72},{9,... | collective-permute-start | bytes 294920 | tf_op jit(solution)/shard_map/ppermute | solution.py:17
  149.4 1.2 copy.34
  150.6 9.7 %collective-permute-done.10 = f32[384,64]{0,1:T(8,128)S(1)} collective-permute-done((f32[384,64]{0,1:T(8,128)S(1)}, f32[384,64]{0,1:T(8,128)S(1)}, u32[]{:S(2)}, u32[]{:S(2)}) %collective-permute-start.10) | collective-permute-done | bytes 98336 | tf_op jit(solution)/shard_map/ppermute | solution.py:17
  161.7 1.8 %convert_element_type.63 = f32[2,192,384]{2,1,0:T(8,128)} convert(bf16[2,192,384]{2,1,0:T(8,128)(2,1)} %reduce-scatter.5.cloned.1.call-done) | non-fusion elementwise | flops 147456 | bytes 884736 | tf_op jit(solution)/shard_map/convert_element_type | solution.py:81
  164.2 1.8 %convert_element_type.61 = f32[2,384,192]{1,2,0:T(8,128)} convert(bf16[2,384,192]{1,2,0:T(8,128)(2,1)} %reduce-scatter.3.cloned.1.call-done) | non-fusion elementwise | flops 147456 | bytes 884736 | tf_op jit(solution)/shard_map/convert_element_type | solution.py:78
  (46 shorter events, 11.4 us)
Async XLA Ops:
  7.2 39.4 %copy-start = (bf16[2,384,1536]{2,1,0:T(8,128)(2,1)S(1)}, bf16[2,384,1536]{2,1,0:T(8,128)(2,1)}, u32[]{:S(2)}) copy-start(bf16[2,384,1536]{2,1,0:T(8,128)(2,1)} %param.7) | copy-start | bytes 7077892
  7.2 154.5 %reduce-scatter.5.cloned.1.call-start = ((), (), s32[]{:S(2)}) async-start(), calls=%async_computation.5 | async-start | bytes 2654208 | tf_op jit(solution)/shard_map/reduce_scatter | solution.py:79
  9.4 2.2 %copy-start.5 = (bf16[8,196,384]{2,0,1:T(8,128)(2,1)S(1)}, bf16[8,196,384]{2,0,1:T(8,128)(2,1)}, u32[]{:S(2)}) copy-start(bf16[8,196,384]{2,0,1:T(8,128)(2,1)} %param.9) | copy-start | bytes 3612676
  46.5 1.0 copy-start.1
  47.5 1.7 copy-start.3
  52.0 112.2 %reduce-scatter.3.cloned.1.call-start = ((), (), s32[]{:S(2)}) async-start(), calls=%async_computation.4 | async-start | bytes 2654208 | tf_op jit(solution)/shard_map/reduce_scatter | solution.py:76
  57.3 1.1 copy-start.2
  109.9 2.5 %copy-start.4 = (bf16[8,196,384]{2,0,1:T(8,128)(2,1)S(1)}, bf16[8,196,384]{2,0,1:T(8,128)(2,1)}, u32[]{:S(2)}) copy-start(bf16[8,196,384]{2,0,1:T(8,128)(2,1)} %param.5) | copy-start | bytes 3612676
  112.8 35.9 %copy-start.6 = (bf16[384,64]{0,1:T(8,128)(2,1)S(1)}, bf16[384,64]{0,1:T(8,128)(2,1)}, u32[]{:S(2)}) copy-start(bf16[384,64]{0,1:T(8,128)(2,1)} %param.6) | copy-start | bytes 147460
  112.8 7.6 %collective-permute-start.2 = (f32[384,64]{0,1:T(8,128)S(1)}, f32[384,64]{0,1:T(8,128)S(1)}, u32[]{:S(2)}, u32[]{:S(2)}) collective-permute-start(f32[384,64]{0,1:T(8,128)S(1)} %convolution_bitcast_fusion.3), channel_id=1, source_target_pairs={{0,3},{1,2},{2,1},{3,0},{4,7},{5,6},{6,5},{7,4},{8,11},{9,10},{10,... | collective-permute-start | bytes 294920 | tf_op jit(solution)/shard_map/ppermute | solution.py:17
  116.0 7.1 %collective-permute-start.1 = (f32[384,64]{0,1:T(8,128)S(1)}, f32[384,64]{0,1:T(8,128)S(1)}, u32[]{:S(2)}, u32[]{:S(2)}) collective-permute-start(f32[384,64]{0,1:T(8,128)S(1)} %convolution_bitcast_fusion.3), channel_id=1, source_target_pairs={{0,2},{1,3},{2,0},{3,1},{4,6},{5,7},{6,4},{7,5},{8,10},{9,11},{10,... | collective-permute-start | bytes 294920 | tf_op jit(solution)/shard_map/ppermute | solution.py:17
  116.0 7.1 %collective-permute-start = (f32[384,64]{0,1:T(8,128)S(1)}, f32[384,64]{0,1:T(8,128)S(1)}, u32[]{:S(2)}, u32[]{:S(2)}) collective-permute-start(f32[384,64]{0,1:T(8,128)S(1)} %convolution_bitcast_fusion.3), channel_id=1, source_target_pairs={{0,1},{1,0},{2,3},{3,2},{4,5},{5,4},{6,7},{7,6},{8,9},{9,8},{10,11... | collective-permute-start | bytes 294920 | tf_op jit(solution)/shard_map/ppermute | solution.py:17
  123.1 4.9 %collective-permute-start.5 = (f32[384,64]{0,1:T(8,128)S(1)}, f32[384,64]{0,1:T(8,128)S(1)}, u32[]{:S(2)}, u32[]{:S(2)}) collective-permute-start(f32[384,64]{0,1:T(8,128)S(1)} %add_add_fusion.3), channel_id=1, source_target_pairs={{0,12},{1,13},{2,14},{3,15},{4,8},{5,9},{6,10},{7,11},{8,4},{9,5},... | collective-permute-start | bytes 294920 | tf_op jit(solution)/shard_map/ppermute | solution.py:17
  123.2 4.8 %collective-permute-start.4 = (f32[384,64]{0,1:T(8,128)S(1)}, f32[384,64]{0,1:T(8,128)S(1)}, u32[]{:S(2)}, u32[]{:S(2)}) collective-permute-start(f32[384,64]{0,1:T(8,128)S(1)} %add_add_fusion.3), channel_id=1, source_target_pairs={{0,8},{1,9},{2,10},{3,11},{4,12},{5,13},{6,14},{7,15},{8,0},{9,1},... | collective-permute-start | bytes 294920 | tf_op jit(solution)/shard_map/ppermute | solution.py:17
  124.1 7.9 %collective-permute-start.3 = (f32[384,64]{0,1:T(8,128)S(1)}, f32[384,64]{0,1:T(8,128)S(1)}, u32[]{:S(2)}, u32[]{:S(2)}) collective-permute-start(f32[384,64]{0,1:T(8,128)S(1)} %add_add_fusion.3), channel_id=1, source_target_pairs={{0,4},{1,5},{2,6},{3,7},{4,0},{5,1},{6,2},{7,3},{8,12},{9,13},{10,... | collective-permute-start | bytes 294920 | tf_op jit(solution)/shard_map/ppermute | solution.py:17
  132.1 7.4 %collective-permute-start.8 = (f32[384,64]{0,1:T(8,128)S(1)}, f32[384,64]{0,1:T(8,128)S(1)}, u32[]{:S(2)}, u32[]{:S(2)}) collective-permute-start(f32[384,64]{0,1:T(8,128)S(1)} %add_add_fusion.2), channel_id=1, source_target_pairs={{0,48},{1,49},{2,50},{3,51},{4,52},{5,53},{6,54},{7,55},{8,56},{9,... | collective-permute-start | bytes 294920 | tf_op jit(solution)/shard_map/ppermute | solution.py:17
  135.0 7.1 %collective-permute-start.7 = (f32[384,64]{0,1:T(8,128)S(1)}, f32[384,64]{0,1:T(8,128)S(1)}, u32[]{:S(2)}, u32[]{:S(2)}) collective-permute-start(f32[384,64]{0,1:T(8,128)S(1)} %add_add_fusion.2), channel_id=1, source_target_pairs={{0,32},{1,33},{2,34},{3,35},{4,36},{5,37},{6,38},{7,39},{8,40},{9,... | collective-permute-start | bytes 294920 | tf_op jit(solution)/shard_map/ppermute | solution.py:17
  135.7 6.4 %collective-permute-start.6 = (f32[384,64]{0,1:T(8,128)S(1)}, f32[384,64]{0,1:T(8,128)S(1)}, u32[]{:S(2)}, u32[]{:S(2)}) collective-permute-start(f32[384,64]{0,1:T(8,128)S(1)} %add_add_fusion.2), channel_id=1, source_target_pairs={{0,16},{1,17},{2,18},{3,19},{4,20},{5,21},{6,22},{7,23},{8,24},{9,... | collective-permute-start | bytes 294920 | tf_op jit(solution)/shard_map/ppermute | solution.py:17
  142.2 8.4 %collective-permute-start.11 = (f32[384,64]{0,1:T(8,128)S(1)}, f32[384,64]{0,1:T(8,128)S(1)}, u32[]{:S(2)}, u32[]{:S(2)}) collective-permute-start(f32[384,64]{0,1:T(8,128)S(1)} %add_add_fusion.1), channel_id=1, source_target_pairs={{0,192},{1,193},{2,194},{3,195},{4,196},{5,197},{6,198},{7,199},{8... | collective-permute-start | bytes 294920 | tf_op jit(solution)/shard_map/ppermute | solution.py:17
  142.7 17.6 %collective-permute-start.10 = (f32[384,64]{0,1:T(8,128)S(1)}, f32[384,64]{0,1:T(8,128)S(1)}, u32[]{:S(2)}, u32[]{:S(2)}) collective-permute-start(f32[384,64]{0,1:T(8,128)S(1)} %add_add_fusion.1), channel_id=1, source_target_pairs={{0,128},{1,129},{2,130},{3,131},{4,132},{5,133},{6,134},{7,135},{8... | collective-permute-start | bytes 294920 | tf_op jit(solution)/shard_map/ppermute | solution.py:17
  146.7 14.3 %collective-permute-start.9 = (f32[384,64]{0,1:T(8,128)S(1)}, f32[384,64]{0,1:T(8,128)S(1)}, u32[]{:S(2)}, u32[]{:S(2)}) collective-permute-start(f32[384,64]{0,1:T(8,128)S(1)} %add_add_fusion.1), channel_id=1, source_target_pairs={{0,64},{1,65},{2,66},{3,67},{4,68},{5,69},{6,70},{7,71},{8,72},{9,... | collective-permute-start | bytes 294920 | tf_op jit(solution)/shard_map/ppermute | solution.py:17
Sparse Core Ops, SparseCore 0:
  52.1 55.0 reduce-scatter.4
  109.8 54.3 reduce-scatter.2

commit v8 on v7

--- a/solution.py
+++ b/solution.py
@@ -51,15 +51,16 @@
     )
     slots_here, grads_here = sent[0], sent[1]
     hidden = jnp.einsum("rjd,jdf->rjf", slots_here, expert_in, preferred_element_type=jnp.float32)
-    activated, gelu_back = jax.vjp(jax.nn.gelu, hidden)
-    activated_low = activated.astype(jnp.bfloat16)
+    activated_low = jax.nn.gelu(hidden).astype(jnp.bfloat16)
     outputs_here = jnp.einsum(
         "rjf,jfd->rjd", activated_low, expert_out, preferred_element_type=jnp.float32
     ).astype(jnp.bfloat16)
     act_grad = jnp.einsum(
         "rjd,jfd->rjf", grads_here, expert_out, preferred_element_type=jnp.float32
     )
-    hidden_grad = gelu_back(act_grad)[0].astype(jnp.bfloat16)
+    slots_again, act_grad = lax.optimization_barrier((slots_here, act_grad))
+    hidden = jnp.einsum("rjd,jdf->rjf", slots_again, expert_in, preferred_element_type=jnp.float32)
+    hidden_grad = jax.vjp(jax.nn.gelu, hidden)[1](act_grad)[0].astype(jnp.bfloat16)
     input_grad_here = jnp.einsum(
         "rjf,jdf->rjd", hidden_grad, expert_in, preferred_element_type=jnp.float32
     ).astype(jnp.bfloat16)

time: 175 us -> 174 us (level)
  matrix products: 27.8 us -> 24 us
    dot_general x1, matrix products: 4.62 us -> 0.98 us  [on_device(): jnp.einsum('rjf,jfd->rjd', activated_low, expert_out, preferred_element_t...]
    dot_general x0 -> x1, matrix products: none -> 2.73 us  [on_device(): jnp.einsum('rjd,jdf->rjf', slots_again, expert_in, preferred_element_type...]
    dot_general x1, matrix products: 5.2 us -> 2.94 us  [on_device(): jnp.einsum('rjd,jfd->rjf', grads_here, expert_out, preferred_element_type...]
  transfers between devices with their start and end apart: 14 -> 14, of which waited for: 9 -> 8; matrix products, arithmetic and copies ran while one was open for 17% -> 17% of each run, Pallas kernels for 0% -> 0%
where the time goes in v8:
time: 174 us; the launch traced here: 171 us
  blocking collectives  70.2 us (40%)
  waiting for transfers between devices  29.7 us (17%)
  matrix products  24 us (14%)
  starting transfers between devices  17.3 us (10%)
  between operations  14.3 us (8%)
  local copies, waits for them, and re-layouts  9.38 us (5%)
  other arithmetic  6.17 us (4%)
    all_to_all x1, blocking collectives, on_device(): lax.all_to_all(jnp.stack([outputs_here, input_grad_here]), 'expert', spli...  36.5 us
    all_to_all x1, blocking collectives, on_device(): lax.all_to_all(jnp.stack([slots, slot_grads]), 'expert', split_axis=2, co...  33.7 us
    ppermute x12, waiting for transfers between devices, _sum_everywhere(): lax.ppermute(term, axes, [(i, i ^ m << low) for i in range(count)])  27.8 us
    ppermute x12, starting transfers between devices, _sum_everywhere(): lax.ppermute(term, axes, [(i, i ^ m << low) for i in range(count)])  17.2 us
  transfers between devices with their start and end apart: 14, of which 8 were waited for; matrix products, arithmetic and copies ran while one was open for 17% of the time, Pallas kernels for 0%

profile of v8, /device:TPU:32, one launch (start us, length us, event | category | flops | bytes accessed | tf_op | source)
XLA Modules:
  0.0 171.1 jit_solution(17684727182022217043)
XLA Ops:
  7.2 2.2 %fusion.40 = (f32[8,64]{1,0:T(8,128)S(1)}, f32[8,196]{1,0:T(8,128)S(1)}, f32[8,64,196]{2,1,0:T(8,128)S(1)}) fusion(bf16[8,196,384]{2,0,1:T(8,128)(2,1)} %param.5, bf16[384,64]{0,1:T(8,128)(2,1)} %param.6), kind=kOutput, calls=%fused_computation.67 | convolution fusion | flops 77268960 | bytes 1663104 | tf_op jit(solution)/shard_map/bpd,ds->bsp/dot_general | solution.py:38
  11.8 33.7 %all_to_all.30 = bf16[2,8,64,384]{3,1,0,2:T(8,128)(2,1)S(1)} all-to-all(bf16[2,8,64,384]{3,1,0,2:T(8,128)(2,1)S(1)} %copy.25), channel_id=1, replica_groups=mesh['expert'=32,'dp'=8] {'expert'}, dimensions={2} | all-to-all | bytes 1572864 | tf_op jit(solution)/shard_map/all_to_all | solution.py:49
  45.6 1.3 fusion.14
  47.0 1.1 copy-done.4
  48.1 2.4 %convolution_convert_fusion = bf16[2,1536,384]{2,1,0:T(8,128)(2,1)} fusion(bf16[256,2,1536]{2,0,1:T(8,128)(2,1)S(1)} %fusion.14, bf16[2,32,8,2,384]{4,2,1,3,0:T(8,128)(2,1)S(1)} %bitcast.81), kind=kOutput, calls=%fused_computation.3 | convolution fusion | flops 605159424 | bytes 4325376 | tf_op jit(solution)/shard_map/rjf,rjd->jfd/dot_general | solution.py:74
  51.7 2.9 %convolution_bitcast_fusion.1 = f32[256,2,1536]{2,0,1:T(8,128)S(1)} fusion(bf16[2,1536,384]{2,1,0:T(8,128)(2,1)} %param.8, bf16[2,32,8,2,384]{4,2,1,3,0:T(8,128)(2,1)} %bitcast.83), kind=kOutput, calls=%fused_computation.6 | convolution fusion | flops 603979776 | bytes 5898240 | tf_op jit(solution)/shard_map/rjd,jfd->rjf/dot_general | solution.py:58
  55.6 2.7 %fusion.6 = bf16[256,2,1536]{2,0,1:T(8,128)(2,1)S(1)} fusion(f32[256,2,1536]{2,0,1:T(8,128)S(1)} %convolution_bitcast_fusion.1, bf16[256,2,384]{2,0,1:T(8,128)(2,1)S(1)} %slice_bitcast_fusion.1, bf16[2,384,1536]{2,1,0:T(8,128)(2,1)S(1)} %copy-done), kind=kOutput, calls=%fused_computation.14 | convolution fusion | flops 619708416 | bytes 7471104 | tf_op jit(solution)/shard_map/rjd,jdf->rjf/dot_general | solution.py:62
  58.4 1.7 %fusion.16 = bf16[1,256,2,384]{3,1,2,0:T(8,128)(2,1)} fusion(bf16[256,2,1536]{2,0,1:T(8,128)(2,1)S(1)} %fusion.6, bf16[2,384,1536]{2,1,0:T(8,128)(2,1)S(1)} %copy-done), kind=kOutput, calls=%fused_computation.30 | convolution fusion | flops 604176384 | bytes 4325376 | tf_op jit(solution)/shard_map/rjf,jdf->rjd/dot_general | solution.py:64
  60.1 2.5 %convolution_convert_fusion.1 = bf16[2,384,1536]{1,2,0:T(8,128)(2,1)} fusion(bf16[256,2,1536]{2,0,1:T(8,128)(2,1)S(1)} %fusion.6, bf16[2,32,8,2,384]{4,2,1,3,0:T(8,128)(2,1)S(1)} %bitcast.84), kind=kOutput, calls=%fused_computation.4 | convolution fusion | flops 605159424 | bytes 4325376 | tf_op jit(solution)/shard_map/rjd,rjf->jdf/dot_general | solution.py:71
  62.6 1.1 pad_maximum_fusion.1
  64.5 36.5 %all_to_all.31 = bf16[2,256,2,384]{3,2,0,1:T(2,128)(2,1)S(1)} all-to-all(bf16[2,256,2,384]{3,2,0,1:T(2,128)(2,1)S(1)} %copy.27), channel_id=1, replica_groups=mesh['expert'=32,'dp'=8] {'expert'}, dimensions={1} | all-to-all | bytes 1572864 | tf_op jit(solution)/shard_map/all_to_all | solution.py:67
  101.7 1.5 fusion.41
  104.0 1.1 squeeze.14
  105.2 2.0 %fusion.19 = f32[8,64,196]{2,1,0:T(8,128)S(1)} fusion(bf16[8,64,384]{2,1,0:T(8,128)(2,1)} %squeeze.15, bf16[8,196,384]{2,0,1:T(8,128)(2,1)} %param.9), kind=kOutput, calls=%fused_computation.34 | convolution fusion | flops 77070336 | bytes 1998848 | tf_op jit(solution)/shard_map/bpd,bsd->bsp/dot_general | solution.py:83
  107.3 2.1 %multiply_reduce_fusion.1 = (f32[8,64]{1,0:T(8,128)S(1)}, f32[8,196]{1,0:T(8,128)S(1)}, f32[8,64,196]{2,1,0:T(8,128)S(1)}) fusion(f32[8,64]{1,0:T(8,128)S(1)} %get-tuple-element.18, f32[8,64,196]{2,1,0:T(8,128)S(1)} %get-tuple-element.24, f32[8,64]{1,0:T(8,128)S(1)} %get-tuple-element.20, f32[8,64,196]{2,1,0:T(8,128)S(1)} %fusion.19, ...), kind=kOutput, calls=%fused_computation.48 | convolution fusion | flops 77871072 | bytes 2826624 | tf_op jit(solution)/shard_map/bpd,bsd->bsp/dot_general | solution.py:84
  110.2 3.0 %collective-permute-start.2 = (f32[384,64]{0,1:T(8,128)S(1)}, f32[384,64]{0,1:T(8,128)S(1)}, u32[]{:S(2)}, u32[]{:S(2)}) collective-permute-start(f32[384,64]{0,1:T(8,128)S(1)} %convolution_bitcast_fusion.4), channel_id=1, source_target_pairs={{0,3},{1,2},{2,1},{3,0},{4,7},{5,6},{6,5},{7,4},{8,11},{9,10},{10,... | collective-permute-start | bytes 294920 | tf_op jit(solution)/shard_map/ppermute | solution.py:17
  113.2 1.2 collective-permute-start
  114.3 2.0 %collective-permute-done.2 = f32[384,64]{0,1:T(8,128)S(1)} collective-permute-done((f32[384,64]{0,1:T(8,128)S(1)}, f32[384,64]{0,1:T(8,128)S(1)}, u32[]{:S(2)}, u32[]{:S(2)}) %collective-permute-start.2) | collective-permute-done | bytes 98336 | tf_op jit(solution)/shard_map/ppermute | solution.py:17
  116.3 3.1 %collective-permute-done.1 = f32[384,64]{0,1:T(8,128)S(1)} collective-permute-done((f32[384,64]{0,1:T(8,128)S(1)}, f32[384,64]{0,1:T(8,128)S(1)}, u32[]{:S(2)}, u32[]{:S(2)}) %collective-permute-start.1) | collective-permute-done | bytes 98336 | tf_op jit(solution)/shard_map/ppermute | solution.py:17
  119.5 1.6 collective-permute-start.4
  121.7 4.2 %collective-permute-done.5 = f32[384,64]{0,1:T(8,128)S(1)} collective-permute-done((f32[384,64]{0,1:T(8,128)S(1)}, f32[384,64]{0,1:T(8,128)S(1)}, u32[]{:S(2)}, u32[]{:S(2)}) %collective-permute-start.5) | collective-permute-done | bytes 98336 | tf_op jit(solution)/shard_map/ppermute | solution.py:17
  125.9 2.9 %collective-permute-done.3 = f32[384,64]{0,1:T(8,128)S(1)} collective-permute-done((f32[384,64]{0,1:T(8,128)S(1)}, f32[384,64]{0,1:T(8,128)S(1)}, u32[]{:S(2)}, u32[]{:S(2)}) %collective-permute-start.3) | collective-permute-done | bytes 98336 | tf_op jit(solution)/shard_map/ppermute | solution.py:17
  128.8 3.3 %collective-permute-start.8 = (f32[384,64]{0,1:T(8,128)S(1)}, f32[384,64]{0,1:T(8,128)S(1)}, u32[]{:S(2)}, u32[]{:S(2)}) collective-permute-start(f32[384,64]{0,1:T(8,128)S(1)} %add_add_fusion.2), channel_id=1, source_target_pairs={{0,48},{1,49},{2,50},{3,51},{4,52},{5,53},{6,54},{7,55},{8,56},{9,... | collective-permute-start | bytes 294920 | tf_op jit(solution)/shard_map/ppermute | solution.py:17
  134.1 2.6 %collective-permute-done.8 = f32[384,64]{0,1:T(8,128)S(1)} collective-permute-done((f32[384,64]{0,1:T(8,128)S(1)}, f32[384,64]{0,1:T(8,128)S(1)}, u32[]{:S(2)}, u32[]{:S(2)}) %collective-permute-start.8) | collective-permute-done | bytes 98336 | tf_op jit(solution)/shard_map/ppermute | solution.py:17
  136.7 2.5 %collective-permute-done.7 = f32[384,64]{0,1:T(8,128)S(1)} collective-permute-done((f32[384,64]{0,1:T(8,128)S(1)}, f32[384,64]{0,1:T(8,128)S(1)}, u32[]{:S(2)}, u32[]{:S(2)}) %collective-permute-start.7) | collective-permute-done | bytes 98336 | tf_op jit(solution)/shard_map/ppermute | solution.py:17
  139.3 5.1 %collective-permute-start.10 = (f32[384,64]{0,1:T(8,128)S(1)}, f32[384,64]{0,1:T(8,128)S(1)}, u32[]{:S(2)}, u32[]{:S(2)}) collective-permute-start(f32[384,64]{0,1:T(8,128)S(1)} %add_add_fusion.1), channel_id=1, source_target_pairs={{0,128},{1,129},{2,130},{3,131},{4,132},{5,133},{6,134},{7,135},{8... | collective-permute-start | bytes 294920 | tf_op jit(solution)/shard_map/ppermute | solution.py:17
  144.4 1.4 collective-permute-start.9
  146.4 1.2 copy.34
  147.6 10.5 %collective-permute-done.10 = f32[384,64]{0,1:T(8,128)S(1)} collective-permute-done((f32[384,64]{0,1:T(8,128)S(1)}, f32[384,64]{0,1:T(8,128)S(1)}, u32[]{:S(2)}, u32[]{:S(2)}) %collective-permute-start.10) | collective-permute-done | bytes 98336 | tf_op jit(solution)/shard_map/ppermute | solution.py:17
  158.8 1.8 %convert_element_type.63 = f32[2,192,384]{2,1,0:T(8,128)} convert(bf16[2,192,384]{2,1,0:T(8,128)(2,1)} %reduce-scatter.5.cloned.1.call-done) | non-fusion elementwise | flops 147456 | bytes 884736 | tf_op jit(solution)/shard_map/convert_element_type | solution.py:82
  160.6 1.9 %reduce-scatter.3.cloned.1.call-done = bf16[2,384,192]{1,2,0:T(8,128)(2,1)} async-done(((bf16[2,384,1536]{1,2,0:T(8,128)(2,1)}), bf16[2,384,192]{1,2,0:T(8,128)(2,1)}) %reduce-scatter.3.cloned.1.call-update) | async-done | bytes 294928 | tf_op jit(solution)/shard_map/reduce_scatter | solution.py:77
  162.4 1.8 %convert_element_type.61 = f32[2,384,192]{1,2,0:T(8,128)} convert(bf16[2,384,192]{1,2,0:T(8,128)(2,1)} %reduce-scatter.3.cloned.1.call-done) | non-fusion elementwise | flops 147456 | bytes 884736 | tf_op jit(solution)/shard_map/convert_element_type | solution.py:79
  (54 shorter events, 11.8 us)
Async XLA Ops:
  7.2 38.4 %copy-start = (bf16[2,384,1536]{2,1,0:T(8,128)(2,1)S(1)}, bf16[2,384,1536]{2,1,0:T(8,128)(2,1)}, u32[]{:S(2)}) copy-start(bf16[2,384,1536]{2,1,0:T(8,128)(2,1)} %param.7) | copy-start | bytes 7077892
  7.2 151.6 %reduce-scatter.5.cloned.1.call-start = ((), (), s32[]{:S(2)}) async-start(), calls=%async_computation.5 | async-start | bytes 2654208 | tf_op jit(solution)/shard_map/reduce_scatter | solution.py:80
  7.2 2.5 %copy-start.6 = (bf16[8,196,384]{2,0,1:T(8,128)(2,1)S(1)}, bf16[8,196,384]{2,0,1:T(8,128)(2,1)}, u32[]{:S(2)}) copy-start(bf16[8,196,384]{2,0,1:T(8,128)(2,1)} %param.5) | copy-start | bytes 3612676
  9.4 1.3 copy-start.8
  45.6 1.4 copy-start.2
  47.0 1.1 copy-start.4
  50.6 111.8 %reduce-scatter.3.cloned.1.call-start = ((), (), s32[]{:S(2)}) async-start(), calls=%async_computation.4 | async-start | bytes 2654208 | tf_op jit(solution)/shard_map/reduce_scatter | solution.py:77
  51.7 3.0 %copy-start.1 = (bf16[2,1536,384]{2,1,0:T(8,128)(2,1)S(1)}, bf16[2,1536,384]{2,1,0:T(8,128)(2,1)}, u32[]{:S(2)}) copy-start(bf16[2,1536,384]{2,1,0:T(8,128)(2,1)} %param.8) | copy-start | bytes 7077892
  51.7 3.0 %copy-start.5 = (bf16[256,2,1536]{2,0,1:T(8,128)(2,1)S(1)}, bf16[256,2,1536]{2,0,1:T(8,128)(2,1)}, u32[]{:S(2)}) copy-start(bf16[256,2,1536]{2,0,1:T(8,128)(2,1)} %copy-done.4) | copy-start | bytes 4718596
  58.4 1.7 %copy-start.3 = (bf16[2,8,32,2,384]{4,1,2,3,0:T(8,128)(2,1)S(1)}, bf16[2,8,32,2,384]{4,1,2,3,0:T(8,128)(2,1)}, u32[]{:S(2)}) copy-start(bf16[2,8,32,2,384]{4,1,2,3,0:T(8,128)(2,1)} %copy-done.2) | copy-start | bytes 2359300
  107.2 2.5 %copy-start.7 = (bf16[8,196,384]{2,0,1:T(8,128)(2,1)S(1)}, bf16[8,196,384]{2,0,1:T(8,128)(2,1)}, u32[]{:S(2)}) copy-start(bf16[8,196,384]{2,0,1:T(8,128)(2,1)} %param.5) | copy-start | bytes 3612676
  110.1 35.7 %copy-start.9 = (bf16[384,64]{0,1:T(8,128)(2,1)S(1)}, bf16[384,64]{0,1:T(8,128)(2,1)}, u32[]{:S(2)}) copy-start(bf16[384,64]{0,1:T(8,128)(2,1)} %param.6) | copy-start | bytes 147460
  110.2 6.2 %collective-permute-start.2 = (f32[384,64]{0,1:T(8,128)S(1)}, f32[384,64]{0,1:T(8,128)S(1)}, u32[]{:S(2)}, u32[]{:S(2)}) collective-permute-start(f32[384,64]{0,1:T(8,128)S(1)} %convolution_bitcast_fusion.4), channel_id=1, source_target_pairs={{0,3},{1,2},{2,1},{3,0},{4,7},{5,6},{6,5},{7,4},{8,11},{9,10},{10,... | collective-permute-start | bytes 294920 | tf_op jit(solution)/shard_map/ppermute | solution.py:17
  113.1 6.2 %collective-permute-start.1 = (f32[384,64]{0,1:T(8,128)S(1)}, f32[384,64]{0,1:T(8,128)S(1)}, u32[]{:S(2)}, u32[]{:S(2)}) collective-permute-start(f32[384,64]{0,1:T(8,128)S(1)} %convolution_bitcast_fusion.4), channel_id=1, source_target_pairs={{0,2},{1,3},{2,0},{3,1},{4,6},{5,7},{6,4},{7,5},{8,10},{9,11},{10,... | collective-permute-start | bytes 294920 | tf_op jit(solution)/shard_map/ppermute | solution.py:17
  113.2 6.2 %collective-permute-start = (f32[384,64]{0,1:T(8,128)S(1)}, f32[384,64]{0,1:T(8,128)S(1)}, u32[]{:S(2)}, u32[]{:S(2)}) collective-permute-start(f32[384,64]{0,1:T(8,128)S(1)} %convolution_bitcast_fusion.4), channel_id=1, source_target_pairs={{0,1},{1,0},{2,3},{3,2},{4,5},{5,4},{6,7},{7,6},{8,9},{9,8},{10,11... | collective-permute-start | bytes 294920 | tf_op jit(solution)/shard_map/ppermute | solution.py:17
  119.4 6.4 %collective-permute-start.5 = (f32[384,64]{0,1:T(8,128)S(1)}, f32[384,64]{0,1:T(8,128)S(1)}, u32[]{:S(2)}, u32[]{:S(2)}) collective-permute-start(f32[384,64]{0,1:T(8,128)S(1)} %add_add_fusion.3), channel_id=1, source_target_pairs={{0,12},{1,13},{2,14},{3,15},{4,8},{5,9},{6,10},{7,11},{8,4},{9,5},... | collective-permute-start | bytes 294920 | tf_op jit(solution)/shard_map/ppermute | solution.py:17
  119.5 6.3 %collective-permute-start.4 = (f32[384,64]{0,1:T(8,128)S(1)}, f32[384,64]{0,1:T(8,128)S(1)}, u32[]{:S(2)}, u32[]{:S(2)}) collective-permute-start(f32[384,64]{0,1:T(8,128)S(1)} %add_add_fusion.3), channel_id=1, source_target_pairs={{0,8},{1,9},{2,10},{3,11},{4,12},{5,13},{6,14},{7,15},{8,0},{9,1},... | collective-permute-start | bytes 294920 | tf_op jit(solution)/shard_map/ppermute | solution.py:17
  121.1 7.6 %collective-permute-start.3 = (f32[384,64]{0,1:T(8,128)S(1)}, f32[384,64]{0,1:T(8,128)S(1)}, u32[]{:S(2)}, u32[]{:S(2)}) collective-permute-start(f32[384,64]{0,1:T(8,128)S(1)} %add_add_fusion.3), channel_id=1, source_target_pairs={{0,4},{1,5},{2,6},{3,7},{4,0},{5,1},{6,2},{7,3},{8,12},{9,13},{10,... | collective-permute-start | bytes 294920 | tf_op jit(solution)/shard_map/ppermute | solution.py:17
  128.8 7.9 %collective-permute-start.8 = (f32[384,64]{0,1:T(8,128)S(1)}, f32[384,64]{0,1:T(8,128)S(1)}, u32[]{:S(2)}, u32[]{:S(2)}) collective-permute-start(f32[384,64]{0,1:T(8,128)S(1)} %add_add_fusion.2), channel_id=1, source_target_pairs={{0,48},{1,49},{2,50},{3,51},{4,52},{5,53},{6,54},{7,55},{8,56},{9,... | collective-permute-start | bytes 294920 | tf_op jit(solution)/shard_map/ppermute | solution.py:17
  132.0 7.2 %collective-permute-start.7 = (f32[384,64]{0,1:T(8,128)S(1)}, f32[384,64]{0,1:T(8,128)S(1)}, u32[]{:S(2)}, u32[]{:S(2)}) collective-permute-start(f32[384,64]{0,1:T(8,128)S(1)} %add_add_fusion.2), channel_id=1, source_target_pairs={{0,32},{1,33},{2,34},{3,35},{4,36},{5,37},{6,38},{7,39},{8,40},{9,... | collective-permute-start | bytes 294920 | tf_op jit(solution)/shard_map/ppermute | solution.py:17
  132.9 6.3 %collective-permute-start.6 = (f32[384,64]{0,1:T(8,128)S(1)}, f32[384,64]{0,1:T(8,128)S(1)}, u32[]{:S(2)}, u32[]{:S(2)}) collective-permute-start(f32[384,64]{0,1:T(8,128)S(1)} %add_add_fusion.2), channel_id=1, source_target_pairs={{0,16},{1,17},{2,18},{3,19},{4,20},{5,21},{6,22},{7,23},{8,24},{9,... | collective-permute-start | bytes 294920 | tf_op jit(solution)/shard_map/ppermute | solution.py:17
  139.2 8.4 %collective-permute-start.11 = (f32[384,64]{0,1:T(8,128)S(1)}, f32[384,64]{0,1:T(8,128)S(1)}, u32[]{:S(2)}, u32[]{:S(2)}) collective-permute-start(f32[384,64]{0,1:T(8,128)S(1)} %add_add_fusion.1), channel_id=1, source_target_pairs={{0,192},{1,193},{2,194},{3,195},{4,196},{5,197},{6,198},{7,199},{8... | collective-permute-start | bytes 294920 | tf_op jit(solution)/shard_map/ppermute | solution.py:17
  139.3 18.7 %collective-permute-start.10 = (f32[384,64]{0,1:T(8,128)S(1)}, f32[384,64]{0,1:T(8,128)S(1)}, u32[]{:S(2)}, u32[]{:S(2)}) collective-permute-start(f32[384,64]{0,1:T(8,128)S(1)} %add_add_fusion.1), channel_id=1, source_target_pairs={{0,128},{1,129},{2,130},{3,131},{4,132},{5,133},{6,134},{7,135},{8... | collective-permute-start | bytes 294920 | tf_op jit(solution)/shard_map/ppermute | solution.py:17
  144.4 13.7 %collective-permute-start.9 = (f32[384,64]{0,1:T(8,128)S(1)}, f32[384,64]{0,1:T(8,128)S(1)}, u32[]{:S(2)}, u32[]{:S(2)}) collective-permute-start(f32[384,64]{0,1:T(8,128)S(1)} %add_add_fusion.1), channel_id=1, source_target_pairs={{0,64},{1,65},{2,66},{3,67},{4,68},{5,69},{6,70},{7,71},{8,72},{9,... | collective-permute-start | bytes 294920 | tf_op jit(solution)/shard_map/ppermute | solution.py:17
Sparse Core Ops, SparseCore 0:
  50.7 54.6 reduce-scatter.4
  107.9 54.4 reduce-scatter.2

commit v9 on v8

--- a/solution.py
+++ b/solution.py
@@ -8,20 +8,10 @@
     count = 1
     for name in axes:
         count *= lax.axis_size(name)
-    bits = count.bit_length() - 1
-    assert 1 << bits == count
-    low = 0
-    while low < bits:
-        width = min(2, bits - low)
-        got = [term] + [
-            lax.ppermute(term, axes, [(i, i ^ (m << low)) for i in range(count)])
-            for m in range(1, 1 << width)
-        ]
-        while len(got) > 1:
-            got = [got[2 * j] + got[2 * j + 1] for j in range(len(got) // 2)]
-        term = got[0]
-        low += width
-    return term
+    pieces = term.reshape(count, term.size // count)
+    mine = jnp.sum(lax.all_to_all(pieces, axes, 0, 0, tiled=True), axis=0, keepdims=True)
+    spread = jnp.broadcast_to(mine, pieces.shape)
+    return lax.all_to_all(spread, axes, 0, 0, tiled=True).reshape(term.shape)
 
 
 def _reduced(value):

time: 174 us -> 175 us (level)
  waiting for transfers between devices: 29.7 us -> 18.7 us
  local copies, waits for them, and re-layouts: 9.38 us -> 16.1 us
  matrix products: 24 us -> 29.3 us
    ppermute x12 -> x0, waiting for transfers between devices: 27.8 us -> none  [_sum_everywhere(): lax.ppermute(term, axes, [(i, i ^ m << low) for i in range(count)])]
    all_to_all x0 -> x2, waiting for transfers between devices: none -> 18.7 us  [the longest x1 9.54 us: _sum_everywhere(): lax.all_to_all(pieces, axes, 0, 0, tiled=True)]
    ppermute x12 -> x0, starting transfers between devices: 17.2 us -> none  [_sum_everywhere(): lax.ppermute(term, axes, [(i, i ^ m << low) for i in range(count)])]
    all_to_all x0 -> x2, starting transfers between devices: none -> 16.5 us  [the longest x1 10 us: _sum_everywhere(): lax.all_to_all(pieces, axes, 0, 0, tiled=True)]
    dot_general x1, matrix products: 0.98 us -> 3.23 us  [on_device(): jnp.einsum('rjf,jfd->rjd', activated_low, expert_out, preferred_element_t...]
    all_to_all x0 -> x2, local copies, waits for them, and re-layouts: none -> 2.21 us  [the longest x1 1.7 us: _sum_everywhere(): lax.all_to_all(pieces, axes, 0, 0, tiled=True)]
    unnamed x21 -> x22, local copies, waits for them, and re-layouts: 2.77 us -> 4.72 us
    reduce_scatter x1, waiting for transfers between devices: 1.86 us -> 0.01 us  [on_device(): lax.psum_scatter(first_term.astype(jnp.bfloat16), 'dp', scatter_dimension...]
  transfers between devices with their start and end apart: 14 -> 4, of which waited for: 8 -> 2; matrix products, arithmetic and copies ran while one was open for 17% -> 22% of each run, Pallas kernels for 0% -> 0%
where the time goes in v9:
time: 175 us; the launch traced here: 172 us
  blocking collectives  69.9 us (40%)
  matrix products  29.3 us (17%)
  waiting for transfers between devices  18.7 us (11%)
  starting transfers between devices  16.5 us (9%)
  local copies, waits for them, and re-layouts  16.1 us (9%)
  between operations  14.3 us (8%)
  other arithmetic  7.3 us (4%)
    all_to_all x1, blocking collectives, on_device(): lax.all_to_all(jnp.stack([outputs_here, input_grad_here]), 'expert', spli...  36.1 us
    all_to_all x1, blocking collectives, on_device(): lax.all_to_all(jnp.stack([slots, slot_grads]), 'expert', split_axis=2, co...  33.7 us
    all_to_all x1, starting transfers between devices, _sum_everywhere(): lax.all_to_all(pieces, axes, 0, 0, tiled=True)  10 us
    all_to_all x1, waiting for transfers between devices, _sum_everywhere(): lax.all_to_all(pieces, axes, 0, 0, tiled=True)  9.54 us
    all_to_all x1, waiting for transfers between devices, _sum_everywhere(): return lax.all_to_all(spread, axes, 0, 0, tiled=True).reshape(term.shape)  9.11 us
    all_to_all x1, starting transfers between devices, _sum_everywhere(): return lax.all_to_all(spread, axes, 0, 0, tiled=True).reshape(term.shape)  6.45 us
    unnamed x22, local copies, waits for them, and re-layouts  4.72 us
  transfers between devices with their start and end apart: 4, of which 2 were waited for; matrix products, arithmetic and copies ran while one was open for 22% of the time, Pallas kernels for 0%

profile of v9, /device:TPU:32, one launch (start us, length us, event | category | flops | bytes accessed | tf_op | source)
XLA Modules:
  0.0 172.1 jit_solution(7046085735982661727)
XLA Ops:
  7.2 2.2 %fusion.40 = (f32[8,64]{1,0:T(8,128)S(1)}, f32[8,196]{1,0:T(8,128)S(1)}, f32[8,64,196]{2,1,0:T(8,128)S(1)}) fusion(bf16[8,196,384]{2,0,1:T(8,128)(2,1)} %param.5, bf16[384,64]{0,1:T(8,128)(2,1)} %param.6), kind=kOutput, calls=%fused_computation.63 | convolution fusion | flops 77268960 | bytes 1663104 | tf_op jit(solution)/shard_map/bpd,ds->bsp/dot_general | solution.py:28
  11.8 33.7 %all_to_all.45 = bf16[2,8,64,384]{3,1,0,2:T(8,128)(2,1)S(1)} all-to-all(bf16[2,8,64,384]{3,1,0,2:T(8,128)(2,1)S(1)} %copy.40), channel_id=1, replica_groups=mesh['expert'=32,'dp'=8] {'expert'}, dimensions={2} | all-to-all | bytes 1572864 | tf_op jit(solution)/shard_map/all_to_all | solution.py:39
  45.6 1.3 fusion.14
  47.0 1.2 copy-done.3
  48.2 2.4 %convolution_convert_fusion = bf16[2,1536,384]{2,1,0:T(8,128)(2,1)} fusion(bf16[256,2,1536]{2,0,1:T(8,128)(2,1)S(1)} %fusion.14, bf16[2,32,8,2,384]{4,2,1,3,0:T(8,128)(2,1)S(1)} %bitcast.82), kind=kOutput, calls=%fused_computation.3 | convolution fusion | flops 605159424 | bytes 4325376 | tf_op jit(solution)/shard_map/rjf,rjd->jfd/dot_general | solution.py:64
  50.7 1.0 slice_bitcast_fusion.1
  51.7 2.8 %convolution_bitcast_fusion.1 = f32[256,2,1536]{2,0,1:T(8,128)S(1)} fusion(bf16[2,1536,384]{2,1,0:T(8,128)(2,1)} %param.8, bf16[2,32,8,2,384]{4,2,1,3,0:T(8,128)(2,1)} %bitcast.84), kind=kOutput, calls=%fused_computation.6 | convolution fusion | flops 603979776 | bytes 5898240 | tf_op jit(solution)/shard_map/rjd,jfd->rjf/dot_general | solution.py:48
  54.6 2.7 %fusion.6 = bf16[256,2,1536]{2,0,1:T(8,128)(2,1)S(1)} fusion(f32[256,2,1536]{2,0,1:T(8,128)S(1)} %convolution_bitcast_fusion.1, bf16[256,2,384]{2,0,1:T(8,128)(2,1)S(1)} %slice_bitcast_fusion.1, bf16[2,384,1536]{2,1,0:T(8,128)(2,1)S(1)} %copy-done), kind=kOutput, calls=%fused_computation.14 | convolution fusion | flops 619708416 | bytes 7471104 | tf_op jit(solution)/shard_map/rjd,jdf->rjf/dot_general | solution.py:52
  57.3 1.1 copy-done.4
  58.5 2.4 %convolution_convert_fusion.1 = bf16[2,384,1536]{1,2,0:T(8,128)(2,1)} fusion(bf16[256,2,1536]{2,0,1:T(8,128)(2,1)S(1)} %fusion.6, bf16[2,32,8,2,384]{4,2,1,3,0:T(8,128)(2,1)S(1)} %bitcast.85), kind=kOutput, calls=%fused_computation.4 | convolution fusion | flops 605159424 | bytes 4325376 | tf_op jit(solution)/shard_map/rjd,rjf->jdf/dot_general | solution.py:61
  60.9 3.2 %fusion.15 = bf16[1,256,2,384]{3,1,2,0:T(8,128)(2,1)S(1)} fusion(bf16[256,2,1536]{2,0,1:T(8,128)(2,1)} %copy-done.3, bf16[2,1536,384]{2,1,0:T(8,128)(2,1)} %param.8), kind=kOutput, calls=%fused_computation.29 | convolution fusion | flops 604176384 | bytes 4325376 | tf_op jit(solution)/shard_map/rjf,jfd->rjd/dot_general | solution.py:45
  64.2 1.0 fusion.16
  66.1 36.1 %all_to_all.46 = bf16[2,256,2,384]{3,2,0,1:T(2,128)(2,1)S(1)} all-to-all(bf16[2,256,2,384]{3,2,0,1:T(2,128)(2,1)S(1)} %copy.42), channel_id=1, replica_groups=mesh['expert'=32,'dp'=8] {'expert'}, dimensions={1} | all-to-all | bytes 1572864 | tf_op jit(solution)/shard_map/all_to_all | solution.py:57
  102.9 1.5 fusion.41
  105.3 1.1 squeeze.14
  106.4 2.0 %fusion.19 = f32[8,64,196]{2,1,0:T(8,128)S(1)} fusion(bf16[8,64,384]{2,1,0:T(8,128)(2,1)} %squeeze.15, bf16[8,196,384]{2,0,1:T(8,128)(2,1)} %param.9), kind=kOutput, calls=%fused_computation.34 | convolution fusion | flops 77070336 | bytes 1998848 | tf_op jit(solution)/shard_map/bpd,bsd->bsp/dot_general | solution.py:73
  108.5 2.1 %multiply_reduce_fusion.1 = (f32[8,64]{1,0:T(8,128)S(1)}, f32[8,196]{1,0:T(8,128)S(1)}, f32[8,64,196]{2,1,0:T(8,128)S(1)}) fusion(f32[8,64]{1,0:T(8,128)S(1)} %get-tuple-element.22, f32[8,64,196]{2,1,0:T(8,128)S(1)} %get-tuple-element.28, f32[8,64]{1,0:T(8,128)S(1)} %get-tuple-element.24, f32[8,64,196]{2,1,0:T(8,128)S(1)} %fusion.19, ...), kind=kOutput, calls=%fused_computation.48 | convolution fusion | flops 77871072 | bytes 2826624 | tf_op jit(solution)/shard_map/bpd,bsd->bsp/dot_general | solution.py:74
  110.6 1.0 add_convert_fusion.1
  111.7 1.0 convolution_bitcast_fusion.4
  112.7 1.7 copy.49
  114.4 1.7 all_to_all.38
  116.1 10.0 %all-to-all-start.2 = ((f32[256,1,96]{2,1,0:T(1,128)}), f32[256,1,96]{2,1,0:T(1,128)}, u32[]{:S(2)}, u32[]{:S(2)}) async-start(f32[256,1,96]{2,1,0:T(1,128)} %bitcast.89), calls=%async_computation.4 | async-start | bytes 262144 | tf_op jit(solution)/shard_map/all_to_all | solution.py:12
  126.1 2.5 %fusion.32 = f32[8,196,384]{2,1,0:T(8,128)} fusion(bf16[8,64,384]{2,1,0:T(8,128)(2,1)S(1)} %squeeze.14, f32[8,64,196]{2,1,0:T(8,128)S(1)} %get-tuple-element.28, f32[8,64]{1,0:T(8,128)S(1)} %get-tuple-element.22, f32[8,64]{1,0:T(8,128)S(1)} %get-tuple-element.24), kind=kOutput, calls=%fused_computation.58 | convolution fusion | flops 77371392 | bytes 3207168 | tf_op jit(solution)/shard_map/bsp,bsd->bpd/dot_general | solution.py:84
  128.6 9.5 %all-to-all-done.2 = f32[256,1,96]{2,1,0:T(1,128)} async-done(((f32[256,1,96]{2,1,0:T(1,128)}), f32[256,1,96]{2,1,0:T(1,128)}, u32[]{:S(2)}, u32[]{:S(2)}) %all-to-all-start.2) | async-done | bytes 98336 | tf_op jit(solution)/shard_map/all_to_all | solution.py:12
  138.2 1.2 reduce_sum.49
  140.1 6.5 %all-to-all-start.3 = ((f32[256,1,96]{2,1,0:T(1,128)}), f32[256,1,96]{2,1,0:T(1,128)S(1)}, u32[]{:S(2)}, u32[]{:S(2)}) async-start(f32[256,1,96]{2,1,0:T(1,128)} %broadcast_in_dim.30), calls=%async_computation.5 | async-start | bytes 262144 | tf_op jit(solution)/shard_map/all_to_all | solution.py:14
  146.6 2.4 %add_convert_fusion = bf16[8,196,384]{2,1,0:T(8,128)(2,1)S(1)} fusion(f32[8,196,384]{2,1,0:T(8,128)} %fusion.32, bf16[8,64,196]{2,1,0:T(8,128)(2,1)S(1)} %add_convert_fusion.1, bf16[384,64]{0,1:T(8,128)(2,1)} %param.6), kind=kOutput, calls=%fused_computation.23 | convolution fusion | flops 78274560 | bytes 3862528 | tf_op jit(solution)/shard_map/bsp,ds->bpd/dot_general | solution.py:87
  148.9 1.2 copy.51
  150.1 9.1 %all-to-all-done.3 = f32[256,1,96]{2,1,0:T(1,128)S(1)} async-done(((f32[256,1,96]{2,1,0:T(1,128)}), f32[256,1,96]{2,1,0:T(1,128)S(1)}, u32[]{:S(2)}, u32[]{:S(2)}) %all-to-all-start.3) | async-done | bytes 98336 | tf_op jit(solution)/shard_map/all_to_all | solution.py:14
  159.7 1.0 reduce.4
  161.6 1.8 %convert_element_type.63 = f32[2,192,384]{2,1,0:T(8,128)} convert(bf16[2,192,384]{2,1,0:T(8,128)(2,1)} %reduce-scatter.5.cloned.1.call-done) | non-fusion elementwise | flops 147456 | bytes 884736 | tf_op jit(solution)/shard_map/convert_element_type | solution.py:72
  163.4 1.8 %convert_element_type.61 = f32[2,384,192]{1,2,0:T(8,128)} convert(bf16[2,384,192]{1,2,0:T(8,128)(2,1)} %reduce-scatter.3.cloned.1.call-done) | non-fusion elementwise | flops 147456 | bytes 884736 | tf_op jit(solution)/shard_map/convert_element_type | solution.py:69
  (38 shorter events, 7.2 us)
Async XLA Ops:
  7.2 38.4 %copy-start = (bf16[2,384,1536]{2,1,0:T(8,128)(2,1)S(1)}, bf16[2,384,1536]{2,1,0:T(8,128)(2,1)}, u32[]{:S(2)}) copy-start(bf16[2,384,1536]{2,1,0:T(8,128)(2,1)} %param.7) | copy-start | bytes 7077892
  7.2 154.4 %reduce-scatter.5.cloned.1.call-start = ((), (), s32[]{:S(2)}) async-start(), calls=%async_computation.7 | async-start | bytes 2654208 | tf_op jit(solution)/shard_map/reduce_scatter | solution.py:70
  7.2 2.5 %copy-start.6 = (bf16[8,196,384]{2,0,1:T(8,128)(2,1)S(1)}, bf16[8,196,384]{2,0,1:T(8,128)(2,1)}, u32[]{:S(2)}) copy-start(bf16[8,196,384]{2,0,1:T(8,128)(2,1)} %param.5) | copy-start | bytes 3612676
  9.4 1.3 copy-start.8
  9.7 98.8 %copy-start.9 = (f32[8,196]{1,0:T(8,128)}, f32[8,196]{1,0:T(8,128)S(1)}, u32[]{:S(2)}) copy-start(f32[8,196]{1,0:T(8,128)S(1)} %get-tuple-element.23) | copy-start | bytes 18820
  45.6 1.4 copy-start.1
  47.0 1.2 copy-start.3
  50.6 112.8 %reduce-scatter.3.cloned.1.call-start = ((), (), s32[]{:S(2)}) async-start(), calls=%async_computation.6 | async-start | bytes 2654208 | tf_op jit(solution)/shard_map/reduce_scatter | solution.py:67
  54.5 3.9 %copy-start.2 = (bf16[2,8,32,2,384]{4,1,2,3,0:T(8,128)(2,1)S(1)}, bf16[2,8,32,2,384]{4,1,2,3,0:T(8,128)(2,1)}, u32[]{:S(2)}) copy-start(bf16[2,8,32,2,384]{4,1,2,3,0:T(8,128)(2,1)} %copy-done.1) | copy-start | bytes 2359300
  57.3 1.2 copy-start.4
  60.9 3.2 %copy-start.5 = (bf16[256,2,1536]{2,0,1:T(8,128)(2,1)S(1)}, bf16[256,2,1536]{2,0,1:T(8,128)(2,1)}, u32[]{:S(2)}) copy-start(bf16[256,2,1536]{2,0,1:T(8,128)(2,1)} %copy-done.4) | copy-start | bytes 4718596
  108.5 3.2 %copy-start.7 = (bf16[8,196,384]{2,0,1:T(8,128)(2,1)S(1)}, bf16[8,196,384]{2,0,1:T(8,128)(2,1)}, u32[]{:S(2)}) copy-start(bf16[8,196,384]{2,0,1:T(8,128)(2,1)} %param.5) | copy-start | bytes 3612676
  116.1 22.1 %all-to-all-start.2 = ((f32[256,1,96]{2,1,0:T(1,128)}), f32[256,1,96]{2,1,0:T(1,128)}, u32[]{:S(2)}, u32[]{:S(2)}) async-start(f32[256,1,96]{2,1,0:T(1,128)} %bitcast.89), calls=%async_computation.4 | async-start | bytes 262144 | tf_op jit(solution)/shard_map/all_to_all | solution.py:12
  140.1 19.1 %all-to-all-start.3 = ((f32[256,1,96]{2,1,0:T(1,128)}), f32[256,1,96]{2,1,0:T(1,128)S(1)}, u32[]{:S(2)}, u32[]{:S(2)}) async-start(f32[256,1,96]{2,1,0:T(1,128)} %broadcast_in_dim.30), calls=%async_computation.5 | async-start | bytes 262144 | tf_op jit(solution)/shard_map/all_to_all | solution.py:14
Sparse Core Ops, SparseCore 0:
  50.8 54.9 reduce-scatter.4
  108.3 50.1 reduce-scatter.2

commit v10 on v9

--- a/solution.py
+++ b/solution.py
@@ -4,14 +4,30 @@
 from jax.sharding import PartitionSpec as P
 
 
+def _tree(got):
+    while len(got) > 1:
+        got = [got[2 * j] + got[2 * j + 1] for j in range(len(got) // 2)]
+    return got[0]
+
+
 def _sum_everywhere(term, axes):
     count = 1
     for name in axes:
         count *= lax.axis_size(name)
-    pieces = term.reshape(count, term.size // count)
-    mine = jnp.sum(lax.all_to_all(pieces, axes, 0, 0, tiled=True), axis=0, keepdims=True)
-    spread = jnp.broadcast_to(mine, pieces.shape)
-    return lax.all_to_all(spread, axes, 0, 0, tiled=True).reshape(term.shape)
+    bits = count.bit_length() - 1
+    assert 1 << bits == count and bits % 2 == 0
+    pairs = lambda m: [(i, i ^ m) for i in range(count)]
+    low = lax.axis_index(axes) % 4
+    pieces = term.reshape(4, term.size // 4)
+    got = [lax.dynamic_index_in_dim(pieces, low, 0, keepdims=False)]
+    for m in range(1, 4):
+        part = lax.dynamic_index_in_dim(pieces, low ^ m, 0, keepdims=False)
+        got.append(lax.ppermute(part, axes, pairs(m)))
+    mine = _tree(got)
+    for shift in range(2, bits, 2):
+        mine = _tree([mine] + [lax.ppermute(mine, axes, pairs(m << shift)) for m in range(1, 4)])
+    got = [mine] + [lax.ppermute(mine, axes, pairs(m)) for m in range(1, 4)]
+    return jnp.stack([lax.select_n(low ^ q, *got) for q in range(4)]).reshape(term.shape)
 
 
 def _reduced(value):

time: 175 us -> 167 us (0.954); the launches traced: 172 us -> 166 us
  blocking collectives: 69.9 us -> 33.8 us
  waiting for transfers between devices: 18.7 us -> 42.3 us
  starting transfers between devices: 16.5 us -> 26.8 us
  matrix products: 29.3 us -> 25.5 us
    all_to_all x1 -> x0, blocking collectives: 36.1 us -> none  [on_device(): lax.all_to_all(jnp.stack([outputs_here, input_grad_here]), 'expert', spli...]
    ppermute x0 -> x15, starting transfers between devices: none -> 21.9 us  [the longest x9 12.9 us: _sum_everywhere(): lax.ppermute(mine, axes, pairs(m << shift))]
    ppermute x0 -> x15, waiting for transfers between devices: none -> 14.4 us  [the longest x9 9.73 us: _sum_everywhere(): lax.ppermute(mine, axes, pairs(m << shift))]
    all_to_all x2 -> x1, starting transfers between devices: 16.5 us -> 4.64 us  [on_device(): lax.all_to_all(jnp.stack([outputs_here, input_grad_here]), 'expert', spli...]
    all_to_all x2 -> x1, waiting for transfers between devices: 18.7 us -> 27.9 us  [on_device(): lax.all_to_all(jnp.stack([outputs_here, input_grad_here]), 'expert', spli...]
    dot_general x1, matrix products: 3.23 us -> 0.98 us  [on_device(): jnp.einsum('rjf,jfd->rjd', activated_low, expert_out, preferred_element_t...]
    all_to_all x2 -> x0, local copies, waits for them, and re-layouts: 2.21 us -> none  [the longest x1 1.7 us: _sum_everywhere(): lax.all_to_all(pieces, axes, 0, 0, tiled=True)]
    unnamed x22 -> x24, local copies, waits for them, and re-layouts: 4.72 us -> 3.63 us
  transfers between devices with their start and end apart: 4 -> 18, of which waited for: 2 -> 11; matrix products, arithmetic and copies ran while one was open for 22% -> 23% of each run, Pallas kernels for 0% -> 0%
where the time goes in v10:
time: 167 us; the launch traced here: 166 us
  waiting for transfers between devices  42.3 us (25%)
  blocking collectives  33.8 us (20%)
  starting transfers between devices  26.8 us (16%)
  matrix products  25.5 us (15%)
  local copies, waits for them, and re-layouts  17 us (10%)
  between operations  14.4 us (9%)
  other arithmetic  6.69 us (4%)
    all_to_all x1, blocking collectives, on_device(): lax.all_to_all(jnp.stack([slots, slot_grads]), 'expert', split_axis=2, co...  33.8 us
    all_to_all x1, waiting for transfers between devices, on_device(): lax.all_to_all(jnp.stack([outputs_here, input_grad_here]), 'expert', spli...  27.9 us
    ppermute x9, starting transfers between devices, _sum_everywhere(): lax.ppermute(mine, axes, pairs(m << shift))  12.9 us
    ppermute x9, waiting for transfers between devices, _sum_everywhere(): lax.ppermute(mine, axes, pairs(m << shift))  9.73 us
    ppermute x3, starting transfers between devices, _sum_everywhere(): got.append(lax.ppermute(part, axes, pairs(m)))  4.79 us
    all_to_all x1, starting transfers between devices, on_device(): lax.all_to_all(jnp.stack([outputs_here, input_grad_here]), 'expert', spli...  4.64 us
    ppermute x3, starting transfers between devices, _sum_everywhere(): got = [mine] + [lax.ppermute(mine, axes, pairs(m)) for m in range(1, 4)]  4.18 us
    dot_general x1, matrix products, on_device(): jnp.einsum('rjd,rjf->jdf', slots_here, hidden_grad, preferred_element_typ...  4.01 us
  transfers between devices with their start and end apart: 18, of which 11 were waited for; matrix products, arithmetic and copies ran while one was open for 23% of the time, Pallas kernels for 0%

profile of v10, /device:TPU:32, one launch (start us, length us, event | category | flops | bytes accessed | tf_op | source)
XLA Modules:
  0.0 166.3 jit_solution(1533195942028132040)
XLA Ops:
  7.2 2.2 %fusion.40 = (f32[8,64]{1,0:T(8,128)S(1)}, f32[8,196]{1,0:T(8,128)S(1)}, f32[8,64,196]{2,1,0:T(8,128)S(1)}) fusion(bf16[8,196,384]{2,0,1:T(8,128)(2,1)} %param.5, bf16[384,64]{0,1:T(8,128)(2,1)} %param.6), kind=kOutput, calls=%fused_computation.76 | convolution fusion | flops 77268960 | bytes 1663104 | tf_op jit(solution)/shard_map/bpd,ds->bsp/dot_general | solution.py:44
  11.8 33.8 %all_to_all.30 = bf16[2,8,64,384]{3,1,0,2:T(8,128)(2,1)S(1)} all-to-all(bf16[2,8,64,384]{3,1,0,2:T(8,128)(2,1)S(1)} %copy.40), channel_id=1, replica_groups=mesh['expert'=32,'dp'=8] {'expert'}, dimensions={2} | all-to-all | bytes 1572864 | tf_op jit(solution)/shard_map/all_to_all | solution.py:55
  45.6 1.3 fusion.14
  48.1 2.5 %convolution_convert_fusion = bf16[2,1536,384]{2,1,0:T(8,128)(2,1)} fusion(bf16[256,2,1536]{2,0,1:T(8,128)(2,1)S(1)} %fusion.14, bf16[2,32,8,2,384]{4,2,1,3,0:T(8,128)(2,1)S(1)} %bitcast.89), kind=kOutput, calls=%fused_computation.3 | convolution fusion | flops 605159424 | bytes 4325376 | tf_op jit(solution)/shard_map/rjf,rjd->jfd/dot_general | solution.py:80
  51.7 2.9 %convolution_bitcast_fusion.1 = f32[256,2,1536]{2,0,1:T(8,128)S(1)} fusion(bf16[2,1536,384]{2,1,0:T(8,128)(2,1)} %param.8, bf16[2,32,8,2,384]{4,2,1,3,0:T(8,128)(2,1)} %bitcast.91), kind=kOutput, calls=%fused_computation.6 | convolution fusion | flops 603979776 | bytes 5898240 | tf_op jit(solution)/shard_map/rjd,jfd->rjf/dot_general | solution.py:64
  55.6 2.7 %fusion.6 = bf16[256,2,1536]{2,0,1:T(8,128)(2,1)S(1)} fusion(f32[256,2,1536]{2,0,1:T(8,128)S(1)} %convolution_bitcast_fusion.1, bf16[256,2,384]{2,0,1:T(8,128)(2,1)S(1)} %slice_bitcast_fusion.1, bf16[2,384,1536]{2,1,0:T(8,128)(2,1)S(1)} %copy-done), kind=kOutput, calls=%fused_computation.14 | convolution fusion | flops 619708416 | bytes 7471104 | tf_op jit(solution)/shard_map/rjd,jdf->rjf/dot_general | solution.py:68
  59.6 1.7 %copy.42 = bf16[2,256,2,384]{3,2,0,1:T(2,128)(2,1)} copy(bf16[2,256,2,384]{3,1,2,0:T(8,128)(2,1)S(1)} %pad_maximum_fusion.1) | data formatting | bytes 1572864 | tf_op jit(solution)/shard_map/stack | solution.py:74
  61.3 4.6 %all-to-all-start.1 = ((bf16[2,256,2,384]{3,2,0,1:T(2,128)(2,1)}), bf16[2,256,2,384]{3,2,0,1:T(2,128)(2,1)}, u32[]{:S(2)}, u32[]{:S(2)}) async-start(bf16[2,256,2,384]{3,2,0,1:T(2,128)(2,1)} %copy.42), calls=%async_computation.1 | async-start | bytes 1572864 | tf_op jit(solution)/shard_map/all_to_all | solution.py:73
  66.1 4.0 %convolution_convert_fusion.1 = bf16[2,384,1536]{1,2,0:T(8,128)(2,1)} fusion(bf16[256,2,1536]{2,0,1:T(8,128)(2,1)} %copy-done.5, bf16[2,32,8,2,384]{4,2,1,3,0:T(8,128)(2,1)} %bitcast.92), kind=kOutput, calls=%fused_computation.4 | convolution fusion | flops 605159424 | bytes 4325376 | tf_op jit(solution)/shard_map/rjd,rjf->jdf/dot_general | solution.py:77
  70.2 27.9 %all-to-all-done.1 = bf16[2,256,2,384]{3,2,0,1:T(2,128)(2,1)} async-done(((bf16[2,256,2,384]{3,2,0,1:T(2,128)(2,1)}), bf16[2,256,2,384]{3,2,0,1:T(2,128)(2,1)}, u32[]{:S(2)}, u32[]{:S(2)}) %all-to-all-start.1) | async-done | bytes 786464 | tf_op jit(solution)/shard_map/all_to_all | solution.py:73
  98.1 1.9 %copy.72 = bf16[2,32,8,2,384]{4,3,1,2,0:T(2,128)(2,1)S(1)} copy(bf16[2,32,8,2,384]{4,3,0,2,1:T(2,128)(2,1)} %bitcast.23) | data formatting | bytes 1572864 | tf_op jit(solution)/shard_map/all_to_all | solution.py:73
  99.9 1.5 fusion.41
  103.4 2.0 %fusion.19 = f32[8,64,196]{2,1,0:T(8,128)S(1)} fusion(bf16[8,64,384]{2,1,0:T(8,128)(2,1)} %squeeze.28, bf16[8,196,384]{2,0,1:T(8,128)(2,1)} %param.9), kind=kOutput, calls=%fused_computation.34 | convolution fusion | flops 77070336 | bytes 1998848 | tf_op jit(solution)/shard_map/bpd,bsd->bsp/dot_general | solution.py:89
  105.5 2.1 %multiply_reduce_fusion.1 = (f32[8,64]{1,0:T(8,128)S(1)}, f32[8,196]{1,0:T(8,128)S(1)}, f32[8,64,196]{2,1,0:T(8,128)S(1)}) fusion(f32[8,64]{1,0:T(8,128)S(1)} %get-tuple-element.22, f32[8,64,196]{2,1,0:T(8,128)S(1)} %get-tuple-element.36, f32[8,64]{1,0:T(8,128)S(1)} %get-tuple-element.24, f32[8,64,196]{2,1,0:T(8,128)S(1)} %fusion.19, ...), kind=kOutput, calls=%fused_computation.48 | convolution fusion | flops 77871072 | bytes 2826624 | tf_op jit(solution)/shard_map/bpd,bsd->bsp/dot_general | solution.py:90
  109.7 1.7 %copy.49 = f32[384,64]{1,0:T(8,128)} copy(f32[384,64]{0,1:T(8,128)} %convolution_bitcast_fusion.4) | data formatting | bytes 196608 | tf_op jit(solution)/shard_map/bpd,bsp->ds/dot_general | solution.py:105
  111.4 1.7 %reshape.22 = f32[4,6144]{1,0:T(4,128)} reshape(f32[384,64]{1,0:T(8,128)} %copy.49) | data formatting | bytes 196608 | tf_op jit(solution)/shard_map/reshape | solution.py:21
  114.3 2.7 %collective-permute-start.2 = (f32[6144]{0:T(1024)S(1)}, f32[6144]{0:T(1024)S(1)}, u32[]{:S(2)}, u32[]{:S(2)}) collective-permute-start(f32[6144]{0:T(1024)S(1)} %bitcast.102), channel_id=1, source_target_pairs={{0,3},{1,2},{2,1},{3,0},{4,7},{5,6},{6,5},{7,4},{8,11},{9,10},{10,... | collective-permute-start | bytes 73736 | tf_op jit(solution)/shard_map/ppermute | solution.py:25
  117.0 2.0 %collective-permute-start.1 = (f32[6144]{0:T(1024)S(1)}, f32[6144]{0:T(1024)S(1)}, u32[]{:S(2)}, u32[]{:S(2)}) collective-permute-start(f32[6144]{0:T(1024)S(1)} %bitcast.100), channel_id=1, source_target_pairs={{0,2},{1,3},{2,0},{3,1},{4,6},{5,7},{6,4},{7,5},{8,10},{9,11},{10,... | collective-permute-start | bytes 73736 | tf_op jit(solution)/shard_map/ppermute | solution.py:25
  119.4 1.4 collective-permute-done
  120.9 1.5 collective-permute-done.1
  123.3 1.3 collective-permute-start.3
  125.7 1.4 collective-permute-done.3
  127.7 2.6 %collective-permute-start.8 = (f32[6144]{0:T(1024)}, f32[6144]{0:T(1024)}, u32[]{:S(2)}, u32[]{:S(2)}) collective-permute-start(f32[6144]{0:T(1024)} %add_add_fusion.2), channel_id=1, source_target_pairs={{0,48},{1,49},{2,50},{3,51},{4,52},{5,53},{6,54},{7,55},{8,56},{9,... | collective-permute-start | bytes 73736 | tf_op jit(solution)/shard_map/ppermute | solution.py:28
  133.1 2.9 %collective-permute-done.7 = f32[6144]{0:T(1024)} collective-permute-done((f32[6144]{0:T(1024)}, f32[6144]{0:T(1024)}, u32[]{:S(2)}, u32[]{:S(2)}) %collective-permute-start.7) | collective-permute-done | bytes 24608 | tf_op jit(solution)/shard_map/ppermute | solution.py:28
  137.6 4.5 %collective-permute-start.10 = (f32[6144]{0:T(1024)S(1)}, f32[6144]{0:T(1024)S(1)}, u32[]{:S(2)}, u32[]{:S(2)}) collective-permute-start(f32[6144]{0:T(1024)S(1)} %add_add_fusion.1), channel_id=1, source_target_pairs={{0,128},{1,129},{2,130},{3,131},{4,132},{5,133},{6,134},{7,135},{8... | collective-permute-start | bytes 73736 | tf_op jit(solution)/shard_map/ppermute | solution.py:28
  144.4 1.8 %collective-permute-done.10 = f32[6144]{0:T(1024)S(1)} collective-permute-done((f32[6144]{0:T(1024)S(1)}, f32[6144]{0:T(1024)S(1)}, u32[]{:S(2)}, u32[]{:S(2)}) %collective-permute-start.10) | collective-permute-done | bytes 24608 | tf_op jit(solution)/shard_map/ppermute | solution.py:28
  146.2 1.3 collective-permute-done.9
  147.5 2.0 %collective-permute-start.14 = (f32[6144]{0:T(1024)S(1)}, f32[6144]{0:T(1024)S(1)}, u32[]{:S(2)}, u32[]{:S(2)}) collective-permute-start(f32[6144]{0:T(1024)S(1)} %add_add_fusion), channel_id=1, source_target_pairs={{0,3},{1,2},{2,1},{3,0},{4,7},{5,6},{6,5},{7,4},{8,11},{9,10},{10,... | collective-permute-start | bytes 73736 | tf_op jit(solution)/shard_map/ppermute | solution.py:29
  149.5 1.5 collective-permute-start.13
  153.5 1.3 collective-permute-done.13
  155.9 1.8 %convert_element_type.63 = f32[2,192,384]{2,1,0:T(8,128)} convert(bf16[2,192,384]{2,1,0:T(8,128)(2,1)} %reduce-scatter.5.cloned.1.call-done) | non-fusion elementwise | flops 147456 | bytes 884736 | tf_op jit(solution)/shard_map/convert_element_type | solution.py:88
  157.7 1.8 %convert_element_type.61 = f32[2,384,192]{1,2,0:T(8,128)} convert(bf16[2,384,192]{1,2,0:T(8,128)(2,1)} %reduce-scatter.3.cloned.1.call-done) | non-fusion elementwise | flops 147456 | bytes 884736 | tf_op jit(solution)/shard_map/convert_element_type | solution.py:85
  (70 shorter events, 25.5 us)
Async XLA Ops:
  7.2 38.4 %copy-start = (bf16[2,384,1536]{2,1,0:T(8,128)(2,1)S(1)}, bf16[2,384,1536]{2,1,0:T(8,128)(2,1)}, u32[]{:S(2)}) copy-start(bf16[2,384,1536]{2,1,0:T(8,128)(2,1)} %param.7) | copy-start | bytes 7077892
  7.2 148.7 %reduce-scatter.5.cloned.1.call-start = ((), (), s32[]{:S(2)}) async-start(), calls=%async_computation.5 | async-start | bytes 2654208 | tf_op jit(solution)/shard_map/reduce_scatter | solution.py:86
  7.2 2.5 %copy-start.6 = (bf16[8,196,384]{2,0,1:T(8,128)(2,1)S(1)}, bf16[8,196,384]{2,0,1:T(8,128)(2,1)}, u32[]{:S(2)}) copy-start(bf16[8,196,384]{2,0,1:T(8,128)(2,1)} %param.5) | copy-start | bytes 3612676
  9.4 1.3 copy-start.8
  9.7 95.8 %copy-start.10 = (f32[8,196]{1,0:T(8,128)}, f32[8,196]{1,0:T(8,128)S(1)}, u32[]{:S(2)}) copy-start(f32[8,196]{1,0:T(8,128)S(1)} %get-tuple-element.23) | copy-start | bytes 18820
  45.6 1.4 copy-start.2
  47.0 1.1 copy-start.3
  51.7 3.0 %copy-start.1 = (bf16[2,1536,384]{2,1,0:T(8,128)(2,1)S(1)}, bf16[2,1536,384]{2,1,0:T(8,128)(2,1)}, u32[]{:S(2)}) copy-start(bf16[2,1536,384]{2,1,0:T(8,128)(2,1)} %param.8) | copy-start | bytes 7077892
  51.7 3.0 %copy-start.4 = (bf16[256,2,1536]{2,0,1:T(8,128)(2,1)S(1)}, bf16[256,2,1536]{2,0,1:T(8,128)(2,1)}, u32[]{:S(2)}) copy-start(bf16[256,2,1536]{2,0,1:T(8,128)(2,1)} %copy-done.3) | copy-start | bytes 4718596
  58.4 1.2 copy-start.5
  61.3 36.8 %all-to-all-start.1 = ((bf16[2,256,2,384]{3,2,0,1:T(2,128)(2,1)}), bf16[2,256,2,384]{3,2,0,1:T(2,128)(2,1)}, u32[]{:S(2)}, u32[]{:S(2)}) async-start(bf16[2,256,2,384]{3,2,0,1:T(2,128)(2,1)} %copy.42), calls=%async_computation.1 | async-start | bytes 1572864 | tf_op jit(solution)/shard_map/all_to_all | solution.py:73
  65.9 91.8 %reduce-scatter.3.cloned.1.call-start = ((), (), s32[]{:S(2)}) async-start(), calls=%async_computation.4 | async-start | bytes 2654208 | tf_op jit(solution)/shard_map/reduce_scatter | solution.py:83
  105.5 3.2 %copy-start.7 = (bf16[8,196,384]{2,0,1:T(8,128)(2,1)S(1)}, bf16[8,196,384]{2,0,1:T(8,128)(2,1)}, u32[]{:S(2)}) copy-start(bf16[8,196,384]{2,0,1:T(8,128)(2,1)} %param.5) | copy-start | bytes 3612676
  114.3 5.1 %collective-permute-start.2 = (f32[6144]{0:T(1024)S(1)}, f32[6144]{0:T(1024)S(1)}, u32[]{:S(2)}, u32[]{:S(2)}) collective-permute-start(f32[6144]{0:T(1024)S(1)} %bitcast.102), channel_id=1, source_target_pairs={{0,3},{1,2},{2,1},{3,0},{4,7},{5,6},{6,5},{7,4},{8,11},{9,10},{10,... | collective-permute-start | bytes 73736 | tf_op jit(solution)/shard_map/ppermute | solution.py:25
  117.0 3.8 %collective-permute-start = (f32[6144]{0:T(1024)S(1)}, f32[6144]{0:T(1024)S(1)}, u32[]{:S(2)}, u32[]{:S(2)}) collective-permute-start(f32[6144]{0:T(1024)S(1)} %bitcast.101), channel_id=1, source_target_pairs={{0,1},{1,0},{2,3},{3,2},{4,5},{5,4},{6,7},{7,6},{8,9},{9,8},{10,11... | collective-permute-start | bytes 73736 | tf_op jit(solution)/shard_map/ppermute | solution.py:25
  117.0 5.3 %collective-permute-start.1 = (f32[6144]{0:T(1024)S(1)}, f32[6144]{0:T(1024)S(1)}, u32[]{:S(2)}, u32[]{:S(2)}) collective-permute-start(f32[6144]{0:T(1024)S(1)} %bitcast.100), channel_id=1, source_target_pairs={{0,2},{1,3},{2,0},{3,1},{4,6},{5,7},{6,4},{7,5},{8,10},{9,11},{10,... | collective-permute-start | bytes 73736 | tf_op jit(solution)/shard_map/ppermute | solution.py:25
  122.4 3.3 %collective-permute-start.5 = (f32[6144]{0:T(1024)S(1)}, f32[6144]{0:T(1024)S(1)}, u32[]{:S(2)}, u32[]{:S(2)}) collective-permute-start(f32[6144]{0:T(1024)S(1)} %add_add_fusion.3), channel_id=1, source_target_pairs={{0,12},{1,13},{2,14},{3,15},{4,8},{5,9},{6,10},{7,11},{8,4},{9,5},... | collective-permute-start | bytes 73736 | tf_op jit(solution)/shard_map/ppermute | solution.py:28
  122.5 3.2 %collective-permute-start.4 = (f32[6144]{0:T(1024)S(1)}, f32[6144]{0:T(1024)S(1)}, u32[]{:S(2)}, u32[]{:S(2)}) collective-permute-start(f32[6144]{0:T(1024)S(1)} %add_add_fusion.3), channel_id=1, source_target_pairs={{0,8},{1,9},{2,10},{3,11},{4,12},{5,13},{6,14},{7,15},{8,0},{9,1},... | collective-permute-start | bytes 73736 | tf_op jit(solution)/shard_map/ppermute | solution.py:28
  123.3 3.8 %collective-permute-start.3 = (f32[6144]{0:T(1024)S(1)}, f32[6144]{0:T(1024)S(1)}, u32[]{:S(2)}, u32[]{:S(2)}) collective-permute-start(f32[6144]{0:T(1024)S(1)} %add_add_fusion.3), channel_id=1, source_target_pairs={{0,4},{1,5},{2,6},{3,7},{4,0},{5,1},{6,2},{7,3},{8,12},{9,13},{10,... | collective-permute-start | bytes 73736 | tf_op jit(solution)/shard_map/ppermute | solution.py:28
  127.7 5.4 %collective-permute-start.8 = (f32[6144]{0:T(1024)}, f32[6144]{0:T(1024)}, u32[]{:S(2)}, u32[]{:S(2)}) collective-permute-start(f32[6144]{0:T(1024)} %add_add_fusion.2), channel_id=1, source_target_pairs={{0,48},{1,49},{2,50},{3,51},{4,52},{5,53},{6,54},{7,55},{8,56},{9,... | collective-permute-start | bytes 73736 | tf_op jit(solution)/shard_map/ppermute | solution.py:28
  130.3 5.6 %collective-permute-start.7 = (f32[6144]{0:T(1024)}, f32[6144]{0:T(1024)}, u32[]{:S(2)}, u32[]{:S(2)}) collective-permute-start(f32[6144]{0:T(1024)} %add_add_fusion.2), channel_id=1, source_target_pairs={{0,32},{1,33},{2,34},{3,35},{4,36},{5,37},{6,38},{7,39},{8,40},{9,... | collective-permute-start | bytes 73736 | tf_op jit(solution)/shard_map/ppermute | solution.py:28
  130.9 5.0 %collective-permute-start.6 = (f32[6144]{0:T(1024)}, f32[6144]{0:T(1024)}, u32[]{:S(2)}, u32[]{:S(2)}) collective-permute-start(f32[6144]{0:T(1024)} %add_add_fusion.2), channel_id=1, source_target_pairs={{0,16},{1,17},{2,18},{3,19},{4,20},{5,21},{6,22},{7,23},{8,24},{9,... | collective-permute-start | bytes 73736 | tf_op jit(solution)/shard_map/ppermute | solution.py:28
  131.8 19.9 %copy-start.9 = (bf16[384,64]{0,1:T(8,128)(2,1)S(1)}, bf16[384,64]{0,1:T(8,128)(2,1)}, u32[]{:S(2)}) copy-start(bf16[384,64]{0,1:T(8,128)(2,1)} %param.6) | copy-start | bytes 147460
  136.7 7.6 %collective-permute-start.11 = (f32[6144]{0:T(1024)S(1)}, f32[6144]{0:T(1024)S(1)}, u32[]{:S(2)}, u32[]{:S(2)}) collective-permute-start(f32[6144]{0:T(1024)S(1)} %add_add_fusion.1), channel_id=1, source_target_pairs={{0,192},{1,193},{2,194},{3,195},{4,196},{5,197},{6,198},{7,199},{8... | collective-permute-start | bytes 73736 | tf_op jit(solution)/shard_map/ppermute | solution.py:28
  137.6 8.6 %collective-permute-start.10 = (f32[6144]{0:T(1024)S(1)}, f32[6144]{0:T(1024)S(1)}, u32[]{:S(2)}, u32[]{:S(2)}) collective-permute-start(f32[6144]{0:T(1024)S(1)} %add_add_fusion.1), channel_id=1, source_target_pairs={{0,128},{1,129},{2,130},{3,131},{4,132},{5,133},{6,134},{7,135},{8... | collective-permute-start | bytes 73736 | tf_op jit(solution)/shard_map/ppermute | solution.py:28
  142.1 5.4 %collective-permute-start.9 = (f32[6144]{0:T(1024)S(1)}, f32[6144]{0:T(1024)S(1)}, u32[]{:S(2)}, u32[]{:S(2)}) collective-permute-start(f32[6144]{0:T(1024)S(1)} %add_add_fusion.1), channel_id=1, source_target_pairs={{0,64},{1,65},{2,66},{3,67},{4,68},{5,69},{6,70},{7,71},{8,72},{9,... | collective-permute-start | bytes 73736 | tf_op jit(solution)/shard_map/ppermute | solution.py:28
  147.5 6.0 %collective-permute-start.14 = (f32[6144]{0:T(1024)S(1)}, f32[6144]{0:T(1024)S(1)}, u32[]{:S(2)}, u32[]{:S(2)}) collective-permute-start(f32[6144]{0:T(1024)S(1)} %add_add_fusion), channel_id=1, source_target_pairs={{0,3},{1,2},{2,1},{3,0},{4,7},{5,6},{6,5},{7,4},{8,11},{9,10},{10,... | collective-permute-start | bytes 73736 | tf_op jit(solution)/shard_map/ppermute | solution.py:29
  149.5 5.4 %collective-permute-start.13 = (f32[6144]{0:T(1024)S(1)}, f32[6144]{0:T(1024)S(1)}, u32[]{:S(2)}, u32[]{:S(2)}) collective-permute-start(f32[6144]{0:T(1024)S(1)} %add_add_fusion), channel_id=1, source_target_pairs={{0,2},{1,3},{2,0},{3,1},{4,6},{5,7},{6,4},{7,5},{8,10},{9,11},{10,... | collective-permute-start | bytes 73736 | tf_op jit(solution)/shard_map/ppermute | solution.py:29
  151.0 3.8 %collective-permute-start.12 = (f32[6144]{0:T(1024)S(1)}, f32[6144]{0:T(1024)S(1)}, u32[]{:S(2)}, u32[]{:S(2)}) collective-permute-start(f32[6144]{0:T(1024)S(1)} %add_add_fusion), channel_id=1, source_target_pairs={{0,1},{1,0},{2,3},{3,2},{4,5},{5,4},{6,7},{7,6},{8,9},{9,8},{10,11... | collective-permute-start | bytes 73736 | tf_op jit(solution)/shard_map/ppermute | solution.py:29
Sparse Core Ops, SparseCore 0:
  50.7 54.9 reduce-scatter.4
  108.3 47.9 reduce-scatter.2

commit v11 on v10

--- a/solution.py
+++ b/solution.py
@@ -102,8 +102,8 @@
     )
     second_part = jnp.einsum("bsp,ds->bpd", logit_low, router, preferred_element_type=jnp.float32)
     grad_tokens = (first_part + second_part).astype(jnp.bfloat16)
-    router_term = jnp.einsum("bpd,bsp->ds", tokens, logit_low, preferred_element_type=jnp.float32)
-    grad_router = _sum_everywhere(router_term, ("expert", "dp"))
+    router_term = jnp.einsum("bsp,bpd->sd", logit_low, tokens, preferred_element_type=jnp.float32)
+    grad_router = _sum_everywhere(router_term, ("expert", "dp")).T
     return (grad_tokens, grad_in, grad_out, grad_router)
 
 

time: 167 us -> 166 us (level)
  local copies, waits for them, and re-layouts: 17 us -> 14.9 us
    dot_general x1 -> x0, local copies, waits for them, and re-layouts: 1.7 us -> none  [on_device(): jnp.einsum('bpd,bsp->ds', tokens, logit_low, preferred_element_type=jnp.f...]
    unnamed x24 -> x23, local copies, waits for them, and re-layouts: 3.63 us -> 2.87 us
  transfers between devices with their start and end apart: 18 -> 18, of which waited for: 11 -> 13; matrix products, arithmetic and copies ran while one was open for 23% -> 22% of each run, Pallas kernels for 0% -> 0%
where the time goes in v11:
time: 166 us; the launch traced here: 165 us
  waiting for transfers between devices  42.7 us (26%)
  blocking collectives  33.8 us (20%)
  starting transfers between devices  26.8 us (16%)
  matrix products  25.5 us (15%)
  local copies, waits for them, and re-layouts  14.9 us (9%)
  between operations  14.4 us (9%)
  other arithmetic  6.69 us (4%)
    all_to_all x1, blocking collectives, on_device(): lax.all_to_all(jnp.stack([slots, slot_grads]), 'expert', split_axis=2, co...  33.8 us
    all_to_all x1, waiting for transfers between devices, on_device(): lax.all_to_all(jnp.stack([outputs_here, input_grad_here]), 'expert', spli...  27.9 us
    ppermute x9, starting transfers between devices, _sum_everywhere(): lax.ppermute(mine, axes, pairs(m << shift))  12.9 us
    ppermute x9, waiting for transfers between devices, _sum_everywhere(): lax.ppermute(mine, axes, pairs(m << shift))  10.2 us
    ppermute x3, starting transfers between devices, _sum_everywhere(): got.append(lax.ppermute(part, axes, pairs(m)))  4.79 us
    all_to_all x1, starting transfers between devices, on_device(): lax.all_to_all(jnp.stack([outputs_here, input_grad_here]), 'expert', spli...  4.64 us
    ppermute x3, starting transfers between devices, _sum_everywhere(): got = [mine] + [lax.ppermute(mine, axes, pairs(m)) for m in range(1, 4)]  4.18 us
    dot_general x1, matrix products, on_device(): jnp.einsum('rjd,rjf->jdf', slots_here, hidden_grad, preferred_element_typ...  4.01 us
  transfers between devices with their start and end apart: 18, of which 13 were waited for; matrix products, arithmetic and copies ran while one was open for 22% of the time, Pallas kernels for 0%

profile of v11, /device:TPU:32, one launch (start us, length us, event | category | flops | bytes accessed | tf_op | source)
XLA Modules:
  0.0 164.7 jit_solution(5400934047974509433)
XLA Ops:
  7.2 2.2 %fusion.40 = (f32[8,64]{1,0:T(8,128)S(1)}, f32[8,196]{1,0:T(8,128)S(1)}, f32[8,64,196]{2,1,0:T(8,128)S(1)}) fusion(bf16[8,196,384]{2,0,1:T(8,128)(2,1)} %param.5, bf16[384,64]{0,1:T(8,128)(2,1)} %param.6), kind=kOutput, calls=%fused_computation.76 | convolution fusion | flops 77268960 | bytes 1663104 | tf_op jit(solution)/shard_map/bpd,ds->bsp/dot_general | solution.py:44
  11.8 33.8 %all_to_all.30 = bf16[2,8,64,384]{3,1,0,2:T(8,128)(2,1)S(1)} all-to-all(bf16[2,8,64,384]{3,1,0,2:T(8,128)(2,1)S(1)} %copy.25), channel_id=1, replica_groups=mesh['expert'=32,'dp'=8] {'expert'}, dimensions={2} | all-to-all | bytes 1572864 | tf_op jit(solution)/shard_map/all_to_all | solution.py:55
  45.6 1.3 fusion.14
  48.1 2.5 %convolution_convert_fusion = bf16[2,1536,384]{2,1,0:T(8,128)(2,1)} fusion(bf16[256,2,1536]{2,0,1:T(8,128)(2,1)S(1)} %fusion.14, bf16[2,32,8,2,384]{4,2,1,3,0:T(8,128)(2,1)S(1)} %bitcast.88), kind=kOutput, calls=%fused_computation.3 | convolution fusion | flops 605159424 | bytes 4325376 | tf_op jit(solution)/shard_map/rjf,rjd->jfd/dot_general | solution.py:80
  51.7 2.9 %convolution_bitcast_fusion.1 = f32[256,2,1536]{2,0,1:T(8,128)S(1)} fusion(bf16[2,1536,384]{2,1,0:T(8,128)(2,1)} %param.8, bf16[2,32,8,2,384]{4,2,1,3,0:T(8,128)(2,1)} %bitcast.90), kind=kOutput, calls=%fused_computation.6 | convolution fusion | flops 603979776 | bytes 5898240 | tf_op jit(solution)/shard_map/rjd,jfd->rjf/dot_general | solution.py:64
  55.6 2.7 %fusion.6 = bf16[256,2,1536]{2,0,1:T(8,128)(2,1)S(1)} fusion(f32[256,2,1536]{2,0,1:T(8,128)S(1)} %convolution_bitcast_fusion.1, bf16[256,2,384]{2,0,1:T(8,128)(2,1)S(1)} %slice_bitcast_fusion.1, bf16[2,384,1536]{2,1,0:T(8,128)(2,1)S(1)} %copy-done), kind=kOutput, calls=%fused_computation.14 | convolution fusion | flops 619708416 | bytes 7471104 | tf_op jit(solution)/shard_map/rjd,jdf->rjf/dot_general | solution.py:68
  59.6 1.7 %copy.27 = bf16[2,256,2,384]{3,2,0,1:T(2,128)(2,1)} copy(bf16[2,256,2,384]{3,1,2,0:T(8,128)(2,1)S(1)} %pad_maximum_fusion.1) | data formatting | bytes 1572864 | tf_op jit(solution)/shard_map/stack | solution.py:74
  61.3 4.6 %all-to-all-start.1 = ((bf16[2,256,2,384]{3,2,0,1:T(2,128)(2,1)}), bf16[2,256,2,384]{3,2,0,1:T(2,128)(2,1)}, u32[]{:S(2)}, u32[]{:S(2)}) async-start(bf16[2,256,2,384]{3,2,0,1:T(2,128)(2,1)} %copy.27), calls=%async_computation.1 | async-start | bytes 1572864 | tf_op jit(solution)/shard_map/all_to_all | solution.py:73
  66.1 4.0 %convolution_convert_fusion.1 = bf16[2,384,1536]{1,2,0:T(8,128)(2,1)} fusion(bf16[256,2,1536]{2,0,1:T(8,128)(2,1)} %copy-done.5, bf16[2,32,8,2,384]{4,2,1,3,0:T(8,128)(2,1)} %bitcast.91), kind=kOutput, calls=%fused_computation.4 | convolution fusion | flops 605159424 | bytes 4325376 | tf_op jit(solution)/shard_map/rjd,rjf->jdf/dot_general | solution.py:77
  70.2 27.9 %all-to-all-done.1 = bf16[2,256,2,384]{3,2,0,1:T(2,128)(2,1)} async-done(((bf16[2,256,2,384]{3,2,0,1:T(2,128)(2,1)}), bf16[2,256,2,384]{3,2,0,1:T(2,128)(2,1)}, u32[]{:S(2)}, u32[]{:S(2)}) %all-to-all-start.1) | async-done | bytes 786464 | tf_op jit(solution)/shard_map/all_to_all | solution.py:73
  98.1 1.9 %copy.55 = bf16[2,32,8,2,384]{4,3,1,2,0:T(2,128)(2,1)S(1)} copy(bf16[2,32,8,2,384]{4,3,0,2,1:T(2,128)(2,1)} %bitcast.23) | data formatting | bytes 1572864 | tf_op jit(solution)/shard_map/all_to_all | solution.py:73
  99.9 1.5 fusion.41
  103.4 2.0 %fusion.19 = f32[8,64,196]{2,1,0:T(8,128)S(1)} fusion(bf16[8,64,384]{2,1,0:T(8,128)(2,1)} %squeeze.28, bf16[8,196,384]{2,0,1:T(8,128)(2,1)} %param.9), kind=kOutput, calls=%fused_computation.34 | convolution fusion | flops 77070336 | bytes 1998848 | tf_op jit(solution)/shard_map/bpd,bsd->bsp/dot_general | solution.py:89
  105.5 2.1 %multiply_reduce_fusion.1 = (f32[8,64]{1,0:T(8,128)S(1)}, f32[8,196]{1,0:T(8,128)S(1)}, f32[8,64,196]{2,1,0:T(8,128)S(1)}) fusion(f32[8,64]{1,0:T(8,128)S(1)} %get-tuple-element.18, f32[8,64,196]{2,1,0:T(8,128)S(1)} %get-tuple-element.32, f32[8,64]{1,0:T(8,128)S(1)} %get-tuple-element.20, f32[8,64,196]{2,1,0:T(8,128)S(1)} %fusion.19, ...), kind=kOutput, calls=%fused_computation.48 | convolution fusion | flops 77871072 | bytes 2826624 | tf_op jit(solution)/shard_map/bpd,bsd->bsp/dot_general | solution.py:90
  109.7 1.6 reshape.22
  111.3 1.2 constant_dynamic-slice_fusion.2
  112.5 2.7 %collective-permute-start.2 = (f32[6144]{0:T(1024)S(1)}, f32[6144]{0:T(1024)S(1)}, u32[]{:S(2)}, u32[]{:S(2)}) collective-permute-start(f32[6144]{0:T(1024)S(1)} %bitcast.102), channel_id=1, source_target_pairs={{0,3},{1,2},{2,1},{3,0},{4,7},{5,6},{6,5},{7,4},{8,11},{9,10},{10,... | collective-permute-start | bytes 73736 | tf_op jit(solution)/shard_map/ppermute | solution.py:25
  115.2 2.0 %collective-permute-start.1 = (f32[6144]{0:T(1024)S(1)}, f32[6144]{0:T(1024)S(1)}, u32[]{:S(2)}, u32[]{:S(2)}) collective-permute-start(f32[6144]{0:T(1024)S(1)} %bitcast.100), channel_id=1, source_target_pairs={{0,2},{1,3},{2,0},{3,1},{4,6},{5,7},{6,4},{7,5},{8,10},{9,11},{10,... | collective-permute-start | bytes 73736 | tf_op jit(solution)/shard_map/ppermute | solution.py:25
  117.6 1.4 collective-permute-done
  119.1 1.5 collective-permute-done.1
  121.4 1.3 collective-permute-start.3
  122.8 1.4 collective-permute-done.5
  125.9 2.8 %collective-permute-start.8 = (f32[6144]{0:T(1024)}, f32[6144]{0:T(1024)}, u32[]{:S(2)}, u32[]{:S(2)}) collective-permute-start(f32[6144]{0:T(1024)} %add_add_fusion.2), channel_id=1, source_target_pairs={{0,48},{1,49},{2,50},{3,51},{4,52},{5,53},{6,54},{7,55},{8,56},{9,... | collective-permute-start | bytes 73736 | tf_op jit(solution)/shard_map/ppermute | solution.py:28
  130.0 1.3 collective-permute-done.8
  131.2 3.1 %collective-permute-done.7 = f32[6144]{0:T(1024)} collective-permute-done((f32[6144]{0:T(1024)}, f32[6144]{0:T(1024)}, u32[]{:S(2)}, u32[]{:S(2)}) %collective-permute-start.7) | collective-permute-done | bytes 24608 | tf_op jit(solution)/shard_map/ppermute | solution.py:28
  135.5 5.2 %collective-permute-start.10 = (f32[6144]{0:T(1024)S(1)}, f32[6144]{0:T(1024)S(1)}, u32[]{:S(2)}, u32[]{:S(2)}) collective-permute-start(f32[6144]{0:T(1024)S(1)} %add_add_fusion.1), channel_id=1, source_target_pairs={{0,128},{1,129},{2,130},{3,131},{4,132},{5,133},{6,134},{7,135},{8... | collective-permute-start | bytes 73736 | tf_op jit(solution)/shard_map/ppermute | solution.py:28
  144.0 2.2 %collective-permute-done.9 = f32[6144]{0:T(1024)S(1)} collective-permute-done((f32[6144]{0:T(1024)S(1)}, f32[6144]{0:T(1024)S(1)}, u32[]{:S(2)}, u32[]{:S(2)}) %collective-permute-start.9) | collective-permute-done | bytes 24608 | tf_op jit(solution)/shard_map/ppermute | solution.py:28
  147.3 1.9 %collective-permute-start.13 = (f32[6144]{0:T(1024)S(1)}, f32[6144]{0:T(1024)S(1)}, u32[]{:S(2)}, u32[]{:S(2)}) collective-permute-start(f32[6144]{0:T(1024)S(1)} %add_add_fusion), channel_id=1, source_target_pairs={{0,2},{1,3},{2,0},{3,1},{4,6},{5,7},{6,4},{7,5},{8,10},{9,11},{10,... | collective-permute-start | bytes 73736 | tf_op jit(solution)/shard_map/ppermute | solution.py:29
  149.2 1.2 collective-permute-start.12
  151.0 1.2 copy.34
  154.0 1.8 %convert_element_type.63 = f32[2,192,384]{2,1,0:T(8,128)} convert(bf16[2,192,384]{2,1,0:T(8,128)(2,1)} %reduce-scatter.5.cloned.1.call-done) | non-fusion elementwise | flops 147456 | bytes 884736 | tf_op jit(solution)/shard_map/convert_element_type | solution.py:88
  156.1 1.8 %convert_element_type.61 = f32[2,384,192]{1,2,0:T(8,128)} convert(bf16[2,384,192]{1,2,0:T(8,128)(2,1)} %reduce-scatter.3.cloned.1.call-done) | non-fusion elementwise | flops 147456 | bytes 884736 | tf_op jit(solution)/shard_map/convert_element_type | solution.py:85
  (68 shorter events, 23.5 us)
Async XLA Ops:
  7.2 38.4 %copy-start = (bf16[2,384,1536]{2,1,0:T(8,128)(2,1)S(1)}, bf16[2,384,1536]{2,1,0:T(8,128)(2,1)}, u32[]{:S(2)}) copy-start(bf16[2,384,1536]{2,1,0:T(8,128)(2,1)} %param.7) | copy-start | bytes 7077892
  7.2 146.9 %reduce-scatter.5.cloned.1.call-start = ((), (), s32[]{:S(2)}) async-start(), calls=%async_computation.5 | async-start | bytes 2654208 | tf_op jit(solution)/shard_map/reduce_scatter | solution.py:86
  7.2 2.5 %copy-start.6 = (bf16[8,196,384]{2,0,1:T(8,128)(2,1)S(1)}, bf16[8,196,384]{2,0,1:T(8,128)(2,1)}, u32[]{:S(2)}) copy-start(bf16[8,196,384]{2,0,1:T(8,128)(2,1)} %param.5) | copy-start | bytes 3612676
  9.4 1.3 copy-start.8
  9.7 95.8 %copy-start.10 = (f32[8,196]{1,0:T(8,128)}, f32[8,196]{1,0:T(8,128)S(1)}, u32[]{:S(2)}) copy-start(f32[8,196]{1,0:T(8,128)S(1)} %get-tuple-element.19) | copy-start | bytes 18820
  45.6 1.4 copy-start.2
  47.0 1.1 copy-start.3
  51.7 3.0 %copy-start.1 = (bf16[2,1536,384]{2,1,0:T(8,128)(2,1)S(1)}, bf16[2,1536,384]{2,1,0:T(8,128)(2,1)}, u32[]{:S(2)}) copy-start(bf16[2,1536,384]{2,1,0:T(8,128)(2,1)} %param.8) | copy-start | bytes 7077892
  51.7 3.0 %copy-start.4 = (bf16[256,2,1536]{2,0,1:T(8,128)(2,1)S(1)}, bf16[256,2,1536]{2,0,1:T(8,128)(2,1)}, u32[]{:S(2)}) copy-start(bf16[256,2,1536]{2,0,1:T(8,128)(2,1)} %copy-done.3) | copy-start | bytes 4718596
  58.4 1.2 copy-start.5
  61.3 36.8 %all-to-all-start.1 = ((bf16[2,256,2,384]{3,2,0,1:T(2,128)(2,1)}), bf16[2,256,2,384]{3,2,0,1:T(2,128)(2,1)}, u32[]{:S(2)}, u32[]{:S(2)}) async-start(bf16[2,256,2,384]{3,2,0,1:T(2,128)(2,1)} %copy.27), calls=%async_computation.1 | async-start | bytes 1572864 | tf_op jit(solution)/shard_map/all_to_all | solution.py:73
  65.9 90.2 %reduce-scatter.3.cloned.1.call-start = ((), (), s32[]{:S(2)}) async-start(), calls=%async_computation.4 | async-start | bytes 2654208 | tf_op jit(solution)/shard_map/reduce_scatter | solution.py:83
  105.5 3.2 %copy-start.7 = (bf16[8,196,384]{2,0,1:T(8,128)(2,1)S(1)}, bf16[8,196,384]{2,0,1:T(8,128)(2,1)}, u32[]{:S(2)}) copy-start(bf16[8,196,384]{2,0,1:T(8,128)(2,1)} %param.5) | copy-start | bytes 3612676
  112.5 5.1 %collective-permute-start.2 = (f32[6144]{0:T(1024)S(1)}, f32[6144]{0:T(1024)S(1)}, u32[]{:S(2)}, u32[]{:S(2)}) collective-permute-start(f32[6144]{0:T(1024)S(1)} %bitcast.102), channel_id=1, source_target_pairs={{0,3},{1,2},{2,1},{3,0},{4,7},{5,6},{6,5},{7,4},{8,11},{9,10},{10,... | collective-permute-start | bytes 73736 | tf_op jit(solution)/shard_map/ppermute | solution.py:25
  115.2 3.8 %collective-permute-start = (f32[6144]{0:T(1024)S(1)}, f32[6144]{0:T(1024)S(1)}, u32[]{:S(2)}, u32[]{:S(2)}) collective-permute-start(f32[6144]{0:T(1024)S(1)} %bitcast.101), channel_id=1, source_target_pairs={{0,1},{1,0},{2,3},{3,2},{4,5},{5,4},{6,7},{7,6},{8,9},{9,8},{10,11... | collective-permute-start | bytes 73736 | tf_op jit(solution)/shard_map/ppermute | solution.py:25
  115.2 5.3 %collective-permute-start.1 = (f32[6144]{0:T(1024)S(1)}, f32[6144]{0:T(1024)S(1)}, u32[]{:S(2)}, u32[]{:S(2)}) collective-permute-start(f32[6144]{0:T(1024)S(1)} %bitcast.100), channel_id=1, source_target_pairs={{0,2},{1,3},{2,0},{3,1},{4,6},{5,7},{6,4},{7,5},{8,10},{9,11},{10,... | collective-permute-start | bytes 73736 | tf_op jit(solution)/shard_map/ppermute | solution.py:25
  120.6 3.6 %collective-permute-start.5 = (f32[6144]{0:T(1024)S(1)}, f32[6144]{0:T(1024)S(1)}, u32[]{:S(2)}, u32[]{:S(2)}) collective-permute-start(f32[6144]{0:T(1024)S(1)} %add_add_fusion.3), channel_id=1, source_target_pairs={{0,12},{1,13},{2,14},{3,15},{4,8},{5,9},{6,10},{7,11},{8,4},{9,5},... | collective-permute-start | bytes 73736 | tf_op jit(solution)/shard_map/ppermute | solution.py:28
  120.7 3.5 %collective-permute-start.4 = (f32[6144]{0:T(1024)S(1)}, f32[6144]{0:T(1024)S(1)}, u32[]{:S(2)}, u32[]{:S(2)}) collective-permute-start(f32[6144]{0:T(1024)S(1)} %add_add_fusion.3), channel_id=1, source_target_pairs={{0,8},{1,9},{2,10},{3,11},{4,12},{5,13},{6,14},{7,15},{8,0},{9,1},... | collective-permute-start | bytes 73736 | tf_op jit(solution)/shard_map/ppermute | solution.py:28
  121.4 3.8 %collective-permute-start.3 = (f32[6144]{0:T(1024)S(1)}, f32[6144]{0:T(1024)S(1)}, u32[]{:S(2)}, u32[]{:S(2)}) collective-permute-start(f32[6144]{0:T(1024)S(1)} %add_add_fusion.3), channel_id=1, source_target_pairs={{0,4},{1,5},{2,6},{3,7},{4,0},{5,1},{6,2},{7,3},{8,12},{9,13},{10,... | collective-permute-start | bytes 73736 | tf_op jit(solution)/shard_map/ppermute | solution.py:28
  125.9 5.4 %collective-permute-start.8 = (f32[6144]{0:T(1024)}, f32[6144]{0:T(1024)}, u32[]{:S(2)}, u32[]{:S(2)}) collective-permute-start(f32[6144]{0:T(1024)} %add_add_fusion.2), channel_id=1, source_target_pairs={{0,48},{1,49},{2,50},{3,51},{4,52},{5,53},{6,54},{7,55},{8,56},{9,... | collective-permute-start | bytes 73736 | tf_op jit(solution)/shard_map/ppermute | solution.py:28
  128.7 5.6 %collective-permute-start.7 = (f32[6144]{0:T(1024)}, f32[6144]{0:T(1024)}, u32[]{:S(2)}, u32[]{:S(2)}) collective-permute-start(f32[6144]{0:T(1024)} %add_add_fusion.2), channel_id=1, source_target_pairs={{0,32},{1,33},{2,34},{3,35},{4,36},{5,37},{6,38},{7,39},{8,40},{9,... | collective-permute-start | bytes 73736 | tf_op jit(solution)/shard_map/ppermute | solution.py:28
  129.5 4.8 %collective-permute-start.6 = (f32[6144]{0:T(1024)}, f32[6144]{0:T(1024)}, u32[]{:S(2)}, u32[]{:S(2)}) collective-permute-start(f32[6144]{0:T(1024)} %add_add_fusion.2), channel_id=1, source_target_pairs={{0,16},{1,17},{2,18},{3,19},{4,20},{5,21},{6,22},{7,23},{8,24},{9,... | collective-permute-start | bytes 73736 | tf_op jit(solution)/shard_map/ppermute | solution.py:28
  130.0 20.4 %copy-start.9 = (bf16[384,64]{0,1:T(8,128)(2,1)S(1)}, bf16[384,64]{0,1:T(8,128)(2,1)}, u32[]{:S(2)}) copy-start(bf16[384,64]{0,1:T(8,128)(2,1)} %param.6) | copy-start | bytes 147460
  135.2 7.6 %collective-permute-start.11 = (f32[6144]{0:T(1024)S(1)}, f32[6144]{0:T(1024)S(1)}, u32[]{:S(2)}, u32[]{:S(2)}) collective-permute-start(f32[6144]{0:T(1024)S(1)} %add_add_fusion.1), channel_id=1, source_target_pairs={{0,192},{1,193},{2,194},{3,195},{4,196},{5,197},{6,198},{7,199},{8... | collective-permute-start | bytes 73736 | tf_op jit(solution)/shard_map/ppermute | solution.py:28
  135.5 8.4 %collective-permute-start.10 = (f32[6144]{0:T(1024)S(1)}, f32[6144]{0:T(1024)S(1)}, u32[]{:S(2)}, u32[]{:S(2)}) collective-permute-start(f32[6144]{0:T(1024)S(1)} %add_add_fusion.1), channel_id=1, source_target_pairs={{0,128},{1,129},{2,130},{3,131},{4,132},{5,133},{6,134},{7,135},{8... | collective-permute-start | bytes 73736 | tf_op jit(solution)/shard_map/ppermute | solution.py:28
  140.8 5.4 %collective-permute-start.9 = (f32[6144]{0:T(1024)S(1)}, f32[6144]{0:T(1024)S(1)}, u32[]{:S(2)}, u32[]{:S(2)}) collective-permute-start(f32[6144]{0:T(1024)S(1)} %add_add_fusion.1), channel_id=1, source_target_pairs={{0,64},{1,65},{2,66},{3,67},{4,68},{5,69},{6,70},{7,71},{8,72},{9,... | collective-permute-start | bytes 73736 | tf_op jit(solution)/shard_map/ppermute | solution.py:28
  146.2 6.0 %collective-permute-start.14 = (f32[6144]{0:T(1024)S(1)}, f32[6144]{0:T(1024)S(1)}, u32[]{:S(2)}, u32[]{:S(2)}) collective-permute-start(f32[6144]{0:T(1024)S(1)} %add_add_fusion), channel_id=1, source_target_pairs={{0,3},{1,2},{2,1},{3,0},{4,7},{5,6},{6,5},{7,4},{8,11},{9,10},{10,... | collective-permute-start | bytes 73736 | tf_op jit(solution)/shard_map/ppermute | solution.py:29
  147.3 5.5 %collective-permute-start.13 = (f32[6144]{0:T(1024)S(1)}, f32[6144]{0:T(1024)S(1)}, u32[]{:S(2)}, u32[]{:S(2)}) collective-permute-start(f32[6144]{0:T(1024)S(1)} %add_add_fusion), channel_id=1, source_target_pairs={{0,2},{1,3},{2,0},{3,1},{4,6},{5,7},{6,4},{7,5},{8,10},{9,11},{10,... | collective-permute-start | bytes 73736 | tf_op jit(solution)/shard_map/ppermute | solution.py:29
  149.2 4.0 %collective-permute-start.12 = (f32[6144]{0:T(1024)S(1)}, f32[6144]{0:T(1024)S(1)}, u32[]{:S(2)}, u32[]{:S(2)}) collective-permute-start(f32[6144]{0:T(1024)S(1)} %add_add_fusion), channel_id=1, source_target_pairs={{0,1},{1,0},{2,3},{3,2},{4,5},{5,4},{6,7},{7,6},{8,9},{9,8},{10,11... | collective-permute-start | bytes 73736 | tf_op jit(solution)/shard_map/ppermute | solution.py:29
Sparse Core Ops, SparseCore 0:
  50.7 54.9 reduce-scatter.4
  108.3 47.7 reduce-scatter.2

commit v12 on v11

--- a/solution.py
+++ b/solution.py
@@ -17,16 +17,16 @@
     bits = count.bit_length() - 1
     assert 1 << bits == count and bits % 2 == 0
     pairs = lambda m: [(i, i ^ m) for i in range(count)]
-    low = lax.axis_index(axes) % 4
+    low = lax.axis_index(axes) // 4 % 4
     pieces = term.reshape(4, term.size // 4)
     got = [lax.dynamic_index_in_dim(pieces, low, 0, keepdims=False)]
     for m in range(1, 4):
         part = lax.dynamic_index_in_dim(pieces, low ^ m, 0, keepdims=False)
-        got.append(lax.ppermute(part, axes, pairs(m)))
+        got.append(lax.ppermute(part, axes, pairs(m << 2)))
     mine = _tree(got)
-    for shift in range(2, bits, 2):
+    for shift in [0] + list(range(4, bits, 2)):
         mine = _tree([mine] + [lax.ppermute(mine, axes, pairs(m << shift)) for m in range(1, 4)])
-    got = [mine] + [lax.ppermute(mine, axes, pairs(m)) for m in range(1, 4)]
+    got = [mine] + [lax.ppermute(mine, axes, pairs(m << 2)) for m in range(1, 4)]
     return jnp.stack([lax.select_n(low ^ q, *got) for q in range(4)]).reshape(term.shape)
 
 

time: 166 us -> 166 us (level)
  starting transfers between devices: 26.8 us -> 23.9 us
  waiting for transfers between devices: 42.7 us -> 45.3 us
    ppermute x6, starting transfers between devices: 8.97 us -> 4.17 us  [the longest x3 2.22 us: _sum_everywhere(): lax.ppermute(mine, axes, pairs(m << 2))]
    reduce_scatter x1, waiting for transfers between devices: 0.22 us -> 3.5 us  [on_device(): lax.psum_scatter(first_term.astype(jnp.bfloat16), 'dp', scatter_dimension...]
    ppermute x9, starting transfers between devices: 12.9 us -> 14.9 us  [_sum_everywhere(): lax.ppermute(mine, axes, pairs(m << shift))]
  transfers between devices with their start and end apart: 18 -> 18, of which waited for: 13 -> 11; matrix products, arithmetic and copies ran while one was open for 22% -> 22% of each run, Pallas kernels for 0% -> 0%
where the time goes in v12:
time: 166 us; the launch traced here: 165 us
  waiting for transfers between devices  45.3 us (27%)
  blocking collectives  33.8 us (20%)
  matrix products  25.5 us (15%)
  starting transfers between devices  23.9 us (14%)
  local copies, waits for them, and re-layouts  14.9 us (9%)
  between operations  14.4 us (9%)
  other arithmetic  6.69 us (4%)
    all_to_all x1, blocking collectives, on_device(): lax.all_to_all(jnp.stack([slots, slot_grads]), 'expert', split_axis=2, co...  33.8 us
    all_to_all x1, waiting for transfers between devices, on_device(): lax.all_to_all(jnp.stack([outputs_here, input_grad_here]), 'expert', spli...  27.9 us
    ppermute x9, starting transfers between devices, _sum_everywhere(): lax.ppermute(mine, axes, pairs(m << shift))  14.9 us
    ppermute x9, waiting for transfers between devices, _sum_everywhere(): lax.ppermute(mine, axes, pairs(m << shift))  10.9 us
    all_to_all x1, starting transfers between devices, on_device(): lax.all_to_all(jnp.stack([outputs_here, input_grad_here]), 'expert', spli...  4.64 us
    dot_general x1, matrix products, on_device(): jnp.einsum('rjd,rjf->jdf', slots_here, hidden_grad, preferred_element_typ...  4.01 us
    reduce_scatter x1, waiting for transfers between devices, on_device(): lax.psum_scatter(first_term.astype(jnp.bfloat16), 'dp', scatter_dimension...  3.5 us
  transfers between devices with their start and end apart: 18, of which 11 were waited for; matrix products, arithmetic and copies ran while one was open for 22% of the time, Pallas kernels for 0%

profile of v12, /device:TPU:32, one launch (start us, length us, event | category | flops | bytes accessed | tf_op | source)
XLA Modules:
  0.0 164.5 jit_solution(4198054501014724973)
XLA Ops:
  7.2 2.2 %fusion.40 = (f32[8,64]{1,0:T(8,128)S(1)}, f32[8,196]{1,0:T(8,128)S(1)}, f32[8,64,196]{2,1,0:T(8,128)S(1)}) fusion(bf16[8,196,384]{2,0,1:T(8,128)(2,1)} %param.5, bf16[384,64]{0,1:T(8,128)(2,1)} %param.6), kind=kOutput, calls=%fused_computation.76 | convolution fusion | flops 77268960 | bytes 1663104 | tf_op jit(solution)/shard_map/bpd,ds->bsp/dot_general | solution.py:44
  11.8 33.8 %all_to_all.30 = bf16[2,8,64,384]{3,1,0,2:T(8,128)(2,1)S(1)} all-to-all(bf16[2,8,64,384]{3,1,0,2:T(8,128)(2,1)S(1)} %copy.25), channel_id=1, replica_groups=mesh['expert'=32,'dp'=8] {'expert'}, dimensions={2} | all-to-all | bytes 1572864 | tf_op jit(solution)/shard_map/all_to_all | solution.py:55
  45.6 1.3 fusion.14
  48.1 2.5 %convolution_convert_fusion = bf16[2,1536,384]{2,1,0:T(8,128)(2,1)} fusion(bf16[256,2,1536]{2,0,1:T(8,128)(2,1)S(1)} %fusion.14, bf16[2,32,8,2,384]{4,2,1,3,0:T(8,128)(2,1)S(1)} %bitcast.88), kind=kOutput, calls=%fused_computation.3 | convolution fusion | flops 605159424 | bytes 4325376 | tf_op jit(solution)/shard_map/rjf,rjd->jfd/dot_general | solution.py:80
  51.7 2.9 %convolution_bitcast_fusion.1 = f32[256,2,1536]{2,0,1:T(8,128)S(1)} fusion(bf16[2,1536,384]{2,1,0:T(8,128)(2,1)} %param.8, bf16[2,32,8,2,384]{4,2,1,3,0:T(8,128)(2,1)} %bitcast.90), kind=kOutput, calls=%fused_computation.6 | convolution fusion | flops 603979776 | bytes 5898240 | tf_op jit(solution)/shard_map/rjd,jfd->rjf/dot_general | solution.py:64
  55.6 2.7 %fusion.6 = bf16[256,2,1536]{2,0,1:T(8,128)(2,1)S(1)} fusion(f32[256,2,1536]{2,0,1:T(8,128)S(1)} %convolution_bitcast_fusion.1, bf16[256,2,384]{2,0,1:T(8,128)(2,1)S(1)} %slice_bitcast_fusion.1, bf16[2,384,1536]{2,1,0:T(8,128)(2,1)S(1)} %copy-done), kind=kOutput, calls=%fused_computation.14 | convolution fusion | flops 619708416 | bytes 7471104 | tf_op jit(solution)/shard_map/rjd,jdf->rjf/dot_general | solution.py:68
  59.6 1.7 %copy.27 = bf16[2,256,2,384]{3,2,0,1:T(2,128)(2,1)} copy(bf16[2,256,2,384]{3,1,2,0:T(8,128)(2,1)S(1)} %pad_maximum_fusion.1) | data formatting | bytes 1572864 | tf_op jit(solution)/shard_map/stack | solution.py:74
  61.3 4.6 %all-to-all-start.1 = ((bf16[2,256,2,384]{3,2,0,1:T(2,128)(2,1)}), bf16[2,256,2,384]{3,2,0,1:T(2,128)(2,1)}, u32[]{:S(2)}, u32[]{:S(2)}) async-start(bf16[2,256,2,384]{3,2,0,1:T(2,128)(2,1)} %copy.27), calls=%async_computation.1 | async-start | bytes 1572864 | tf_op jit(solution)/shard_map/all_to_all | solution.py:73
  66.1 4.0 %convolution_convert_fusion.1 = bf16[2,384,1536]{1,2,0:T(8,128)(2,1)} fusion(bf16[256,2,1536]{2,0,1:T(8,128)(2,1)} %copy-done.5, bf16[2,32,8,2,384]{4,2,1,3,0:T(8,128)(2,1)} %bitcast.91), kind=kOutput, calls=%fused_computation.4 | convolution fusion | flops 605159424 | bytes 4325376 | tf_op jit(solution)/shard_map/rjd,rjf->jdf/dot_general | solution.py:77
  70.2 27.9 %all-to-all-done.1 = bf16[2,256,2,384]{3,2,0,1:T(2,128)(2,1)} async-done(((bf16[2,256,2,384]{3,2,0,1:T(2,128)(2,1)}), bf16[2,256,2,384]{3,2,0,1:T(2,128)(2,1)}, u32[]{:S(2)}, u32[]{:S(2)}) %all-to-all-start.1) | async-done | bytes 786464 | tf_op jit(solution)/shard_map/all_to_all | solution.py:73
  98.1 1.9 %copy.55 = bf16[2,32,8,2,384]{4,3,1,2,0:T(2,128)(2,1)S(1)} copy(bf16[2,32,8,2,384]{4,3,0,2,1:T(2,128)(2,1)} %bitcast.23) | data formatting | bytes 1572864 | tf_op jit(solution)/shard_map/all_to_all | solution.py:73
  99.9 1.5 fusion.41
  102.3 1.1 squeeze.27
  103.4 2.0 %fusion.19 = f32[8,64,196]{2,1,0:T(8,128)S(1)} fusion(bf16[8,64,384]{2,1,0:T(8,128)(2,1)} %squeeze.28, bf16[8,196,384]{2,0,1:T(8,128)(2,1)} %param.9), kind=kOutput, calls=%fused_computation.34 | convolution fusion | flops 77070336 | bytes 1998848 | tf_op jit(solution)/shard_map/bpd,bsd->bsp/dot_general | solution.py:89
  105.5 2.1 %multiply_reduce_fusion.1 = (f32[8,64]{1,0:T(8,128)S(1)}, f32[8,196]{1,0:T(8,128)S(1)}, f32[8,64,196]{2,1,0:T(8,128)S(1)}) fusion(f32[8,64]{1,0:T(8,128)S(1)} %get-tuple-element.18, f32[8,64,196]{2,1,0:T(8,128)S(1)} %get-tuple-element.32, f32[8,64]{1,0:T(8,128)S(1)} %get-tuple-element.20, f32[8,64,196]{2,1,0:T(8,128)S(1)} %fusion.19, ...), kind=kOutput, calls=%fused_computation.48 | convolution fusion | flops 77871072 | bytes 2826624 | tf_op jit(solution)/shard_map/bpd,bsd->bsp/dot_general | solution.py:90
  109.7 1.6 reshape.22
  111.3 1.2 constant_dynamic-slice_fusion.2
  114.4 1.4 collective-permute-done.2
  116.8 2.8 %collective-permute-start.5 = (f32[6144]{0:T(1024)S(1)}, f32[6144]{0:T(1024)S(1)}, u32[]{:S(2)}, u32[]{:S(2)}) collective-permute-start(f32[6144]{0:T(1024)S(1)} %add_add_fusion.3), channel_id=1, source_target_pairs={{0,3},{1,2},{2,1},{3,0},{4,7},{5,6},{6,5},{7,4},{8,11},{9,10},{10,... | collective-permute-start | bytes 73736 | tf_op jit(solution)/shard_map/ppermute | solution.py:28
  119.5 1.4 collective-permute-start.3
  121.9 3.4 %collective-permute-done.4 = f32[6144]{0:T(1024)S(1)} collective-permute-done((f32[6144]{0:T(1024)S(1)}, f32[6144]{0:T(1024)S(1)}, u32[]{:S(2)}, u32[]{:S(2)}) %collective-permute-start.4) | collective-permute-done | bytes 24608 | tf_op jit(solution)/shard_map/ppermute | solution.py:28
  125.9 2.3 %collective-permute-start.8 = (f32[6144]{0:T(1024)}, f32[6144]{0:T(1024)}, u32[]{:S(2)}, u32[]{:S(2)}) collective-permute-start(f32[6144]{0:T(1024)} %add_add_fusion.2), channel_id=1, source_target_pairs={{0,48},{1,49},{2,50},{3,51},{4,52},{5,53},{6,54},{7,55},{8,56},{9,... | collective-permute-start | bytes 73736 | tf_op jit(solution)/shard_map/ppermute | solution.py:28
  130.0 1.3 collective-permute-done.8
  131.3 2.6 %collective-permute-done.7 = f32[6144]{0:T(1024)} collective-permute-done((f32[6144]{0:T(1024)}, f32[6144]{0:T(1024)}, u32[]{:S(2)}, u32[]{:S(2)}) %collective-permute-start.7) | collective-permute-done | bytes 24608 | tf_op jit(solution)/shard_map/ppermute | solution.py:28
  134.9 4.7 %collective-permute-start.10 = (f32[6144]{0:T(1024)S(1)}, f32[6144]{0:T(1024)S(1)}, u32[]{:S(2)}, u32[]{:S(2)}) collective-permute-start(f32[6144]{0:T(1024)S(1)} %add_add_fusion.1), channel_id=1, source_target_pairs={{0,128},{1,129},{2,130},{3,131},{4,132},{5,133},{6,134},{7,135},{8... | collective-permute-start | bytes 73736 | tf_op jit(solution)/shard_map/ppermute | solution.py:28
  139.7 1.6 collective-permute-start.9
  143.4 1.6 collective-permute-done.9
  145.4 1.8 %collective-permute-start.12 = (f32[6144]{0:T(1024)S(1)}, f32[6144]{0:T(1024)S(1)}, u32[]{:S(2)}, u32[]{:S(2)}) collective-permute-start(f32[6144]{0:T(1024)S(1)} %add_add_fusion), channel_id=1, source_target_pairs={{0,4},{1,5},{2,6},{3,7},{4,0},{5,1},{6,2},{7,3},{8,12},{9,13},{10,... | collective-permute-start | bytes 73736 | tf_op jit(solution)/shard_map/ppermute | solution.py:29
  147.8 1.2 copy.34
  150.5 1.8 %convert_element_type.63 = f32[2,192,384]{2,1,0:T(8,128)} convert(bf16[2,192,384]{2,1,0:T(8,128)(2,1)} %reduce-scatter.5.cloned.1.call-done) | non-fusion elementwise | flops 147456 | bytes 884736 | tf_op jit(solution)/shard_map/convert_element_type | solution.py:88
  152.4 3.5 %reduce-scatter.3.cloned.1.call-done = bf16[2,384,192]{1,2,0:T(8,128)(2,1)} async-done(((bf16[2,384,1536]{1,2,0:T(8,128)(2,1)}), bf16[2,384,192]{1,2,0:T(8,128)(2,1)}) %reduce-scatter.3.cloned.1.call-update) | async-done | bytes 294928 | tf_op jit(solution)/shard_map/reduce_scatter | solution.py:83
  155.9 1.8 %convert_element_type.61 = f32[2,384,192]{1,2,0:T(8,128)} convert(bf16[2,384,192]{1,2,0:T(8,128)(2,1)} %reduce-scatter.3.cloned.1.call-done) | non-fusion elementwise | flops 147456 | bytes 884736 | tf_op jit(solution)/shard_map/convert_element_type | solution.py:85
  (68 shorter events, 21.9 us)
Async XLA Ops:
  7.2 38.4 %copy-start = (bf16[2,384,1536]{2,1,0:T(8,128)(2,1)S(1)}, bf16[2,384,1536]{2,1,0:T(8,128)(2,1)}, u32[]{:S(2)}) copy-start(bf16[2,384,1536]{2,1,0:T(8,128)(2,1)} %param.7) | copy-start | bytes 7077892
  7.2 143.4 %reduce-scatter.5.cloned.1.call-start = ((), (), s32[]{:S(2)}) async-start(), calls=%async_computation.5 | async-start | bytes 2654208 | tf_op jit(solution)/shard_map/reduce_scatter | solution.py:86
  7.2 2.5 %copy-start.6 = (bf16[8,196,384]{2,0,1:T(8,128)(2,1)S(1)}, bf16[8,196,384]{2,0,1:T(8,128)(2,1)}, u32[]{:S(2)}) copy-start(bf16[8,196,384]{2,0,1:T(8,128)(2,1)} %param.5) | copy-start | bytes 3612676
  9.4 1.3 copy-start.8
  9.7 95.8 %copy-start.10 = (f32[8,196]{1,0:T(8,128)}, f32[8,196]{1,0:T(8,128)S(1)}, u32[]{:S(2)}) copy-start(f32[8,196]{1,0:T(8,128)S(1)} %get-tuple-element.19) | copy-start | bytes 18820
  45.6 1.4 copy-start.2
  47.0 1.1 copy-start.3
  51.7 3.0 %copy-start.1 = (bf16[2,1536,384]{2,1,0:T(8,128)(2,1)S(1)}, bf16[2,1536,384]{2,1,0:T(8,128)(2,1)}, u32[]{:S(2)}) copy-start(bf16[2,1536,384]{2,1,0:T(8,128)(2,1)} %param.8) | copy-start | bytes 7077892
  51.7 3.0 %copy-start.4 = (bf16[256,2,1536]{2,0,1:T(8,128)(2,1)S(1)}, bf16[256,2,1536]{2,0,1:T(8,128)(2,1)}, u32[]{:S(2)}) copy-start(bf16[256,2,1536]{2,0,1:T(8,128)(2,1)} %copy-done.3) | copy-start | bytes 4718596
  58.4 1.2 copy-start.5
  61.3 36.8 %all-to-all-start.1 = ((bf16[2,256,2,384]{3,2,0,1:T(2,128)(2,1)}), bf16[2,256,2,384]{3,2,0,1:T(2,128)(2,1)}, u32[]{:S(2)}, u32[]{:S(2)}) async-start(bf16[2,256,2,384]{3,2,0,1:T(2,128)(2,1)} %copy.27), calls=%async_computation.1 | async-start | bytes 1572864 | tf_op jit(solution)/shard_map/all_to_all | solution.py:73
  65.9 89.9 %reduce-scatter.3.cloned.1.call-start = ((), (), s32[]{:S(2)}) async-start(), calls=%async_computation.4 | async-start | bytes 2654208 | tf_op jit(solution)/shard_map/reduce_scatter | solution.py:83
  105.5 3.2 %copy-start.7 = (bf16[8,196,384]{2,0,1:T(8,128)(2,1)S(1)}, bf16[8,196,384]{2,0,1:T(8,128)(2,1)}, u32[]{:S(2)}) copy-start(bf16[8,196,384]{2,0,1:T(8,128)(2,1)} %param.5) | copy-start | bytes 3612676
  112.5 3.3 %collective-permute-start.2 = (f32[6144]{0:T(1024)S(1)}, f32[6144]{0:T(1024)S(1)}, u32[]{:S(2)}, u32[]{:S(2)}) collective-permute-start(f32[6144]{0:T(1024)S(1)} %bitcast.102), channel_id=1, source_target_pairs={{0,12},{1,13},{2,14},{3,15},{4,8},{5,9},{6,10},{7,11},{8,4},{9,5},... | collective-permute-start | bytes 73736 | tf_op jit(solution)/shard_map/ppermute | solution.py:25
  112.9 3.8 %collective-permute-start = (f32[6144]{0:T(1024)S(1)}, f32[6144]{0:T(1024)S(1)}, u32[]{:S(2)}, u32[]{:S(2)}) collective-permute-start(f32[6144]{0:T(1024)S(1)} %bitcast.101), channel_id=1, source_target_pairs={{0,4},{1,5},{2,6},{3,7},{4,0},{5,1},{6,2},{7,3},{8,12},{9,13},{10,... | collective-permute-start | bytes 73736 | tf_op jit(solution)/shard_map/ppermute | solution.py:25
  113.6 3.2 %collective-permute-start.1 = (f32[6144]{0:T(1024)S(1)}, f32[6144]{0:T(1024)S(1)}, u32[]{:S(2)}, u32[]{:S(2)}) collective-permute-start(f32[6144]{0:T(1024)S(1)} %bitcast.100), channel_id=1, source_target_pairs={{0,8},{1,9},{2,10},{3,11},{4,12},{5,13},{6,14},{7,15},{8,0},{9,1},... | collective-permute-start | bytes 73736 | tf_op jit(solution)/shard_map/ppermute | solution.py:25
  116.8 5.1 %collective-permute-start.5 = (f32[6144]{0:T(1024)S(1)}, f32[6144]{0:T(1024)S(1)}, u32[]{:S(2)}, u32[]{:S(2)}) collective-permute-start(f32[6144]{0:T(1024)S(1)} %add_add_fusion.3), channel_id=1, source_target_pairs={{0,3},{1,2},{2,1},{3,0},{4,7},{5,6},{6,5},{7,4},{8,11},{9,10},{10,... | collective-permute-start | bytes 73736 | tf_op jit(solution)/shard_map/ppermute | solution.py:28
  119.5 5.8 %collective-permute-start.4 = (f32[6144]{0:T(1024)S(1)}, f32[6144]{0:T(1024)S(1)}, u32[]{:S(2)}, u32[]{:S(2)}) collective-permute-start(f32[6144]{0:T(1024)S(1)} %add_add_fusion.3), channel_id=1, source_target_pairs={{0,2},{1,3},{2,0},{3,1},{4,6},{5,7},{6,4},{7,5},{8,10},{9,11},{10,... | collective-permute-start | bytes 73736 | tf_op jit(solution)/shard_map/ppermute | solution.py:28
  119.5 5.8 %collective-permute-start.3 = (f32[6144]{0:T(1024)S(1)}, f32[6144]{0:T(1024)S(1)}, u32[]{:S(2)}, u32[]{:S(2)}) collective-permute-start(f32[6144]{0:T(1024)S(1)} %add_add_fusion.3), channel_id=1, source_target_pairs={{0,1},{1,0},{2,3},{3,2},{4,5},{5,4},{6,7},{7,6},{8,9},{9,8},{10,11... | collective-permute-start | bytes 73736 | tf_op jit(solution)/shard_map/ppermute | solution.py:28
  125.9 5.4 %collective-permute-start.8 = (f32[6144]{0:T(1024)}, f32[6144]{0:T(1024)}, u32[]{:S(2)}, u32[]{:S(2)}) collective-permute-start(f32[6144]{0:T(1024)} %add_add_fusion.2), channel_id=1, source_target_pairs={{0,48},{1,49},{2,50},{3,51},{4,52},{5,53},{6,54},{7,55},{8,56},{9,... | collective-permute-start | bytes 73736 | tf_op jit(solution)/shard_map/ppermute | solution.py:28
  128.3 5.6 %collective-permute-start.7 = (f32[6144]{0:T(1024)}, f32[6144]{0:T(1024)}, u32[]{:S(2)}, u32[]{:S(2)}) collective-permute-start(f32[6144]{0:T(1024)} %add_add_fusion.2), channel_id=1, source_target_pairs={{0,32},{1,33},{2,34},{3,35},{4,36},{5,37},{6,38},{7,39},{8,40},{9,... | collective-permute-start | bytes 73736 | tf_op jit(solution)/shard_map/ppermute | solution.py:28
  129.1 4.8 %collective-permute-start.6 = (f32[6144]{0:T(1024)}, f32[6144]{0:T(1024)}, u32[]{:S(2)}, u32[]{:S(2)}) collective-permute-start(f32[6144]{0:T(1024)} %add_add_fusion.2), channel_id=1, source_target_pairs={{0,16},{1,17},{2,18},{3,19},{4,20},{5,21},{6,22},{7,23},{8,24},{9,... | collective-permute-start | bytes 73736 | tf_op jit(solution)/shard_map/ppermute | solution.py:28
  130.0 17.2 %copy-start.9 = (bf16[384,64]{0,1:T(8,128)(2,1)S(1)}, bf16[384,64]{0,1:T(8,128)(2,1)}, u32[]{:S(2)}) copy-start(bf16[384,64]{0,1:T(8,128)(2,1)} %param.6) | copy-start | bytes 147460
  134.7 7.6 %collective-permute-start.11 = (f32[6144]{0:T(1024)S(1)}, f32[6144]{0:T(1024)S(1)}, u32[]{:S(2)}, u32[]{:S(2)}) collective-permute-start(f32[6144]{0:T(1024)S(1)} %add_add_fusion.1), channel_id=1, source_target_pairs={{0,192},{1,193},{2,194},{3,195},{4,196},{5,197},{6,198},{7,199},{8... | collective-permute-start | bytes 73736 | tf_op jit(solution)/shard_map/ppermute | solution.py:28
  134.9 8.4 %collective-permute-start.10 = (f32[6144]{0:T(1024)S(1)}, f32[6144]{0:T(1024)S(1)}, u32[]{:S(2)}, u32[]{:S(2)}) collective-permute-start(f32[6144]{0:T(1024)S(1)} %add_add_fusion.1), channel_id=1, source_target_pairs={{0,128},{1,129},{2,130},{3,131},{4,132},{5,133},{6,134},{7,135},{8... | collective-permute-start | bytes 73736 | tf_op jit(solution)/shard_map/ppermute | solution.py:28
  139.7 5.3 %collective-permute-start.9 = (f32[6144]{0:T(1024)S(1)}, f32[6144]{0:T(1024)S(1)}, u32[]{:S(2)}, u32[]{:S(2)}) collective-permute-start(f32[6144]{0:T(1024)S(1)} %add_add_fusion.1), channel_id=1, source_target_pairs={{0,64},{1,65},{2,66},{3,67},{4,68},{5,69},{6,70},{7,71},{8,72},{9,... | collective-permute-start | bytes 73736 | tf_op jit(solution)/shard_map/ppermute | solution.py:28
  145.0 4.0 %collective-permute-start.14 = (f32[6144]{0:T(1024)S(1)}, f32[6144]{0:T(1024)S(1)}, u32[]{:S(2)}, u32[]{:S(2)}) collective-permute-start(f32[6144]{0:T(1024)S(1)} %add_add_fusion), channel_id=1, source_target_pairs={{0,12},{1,13},{2,14},{3,15},{4,8},{5,9},{6,10},{7,11},{8,4},{9,5},... | collective-permute-start | bytes 73736 | tf_op jit(solution)/shard_map/ppermute | solution.py:29
  145.1 3.9 %collective-permute-start.13 = (f32[6144]{0:T(1024)S(1)}, f32[6144]{0:T(1024)S(1)}, u32[]{:S(2)}, u32[]{:S(2)}) collective-permute-start(f32[6144]{0:T(1024)S(1)} %add_add_fusion), channel_id=1, source_target_pairs={{0,8},{1,9},{2,10},{3,11},{4,12},{5,13},{6,14},{7,15},{8,0},{9,1},... | collective-permute-start | bytes 73736 | tf_op jit(solution)/shard_map/ppermute | solution.py:29
  145.4 4.3 %collective-permute-start.12 = (f32[6144]{0:T(1024)S(1)}, f32[6144]{0:T(1024)S(1)}, u32[]{:S(2)}, u32[]{:S(2)}) collective-permute-start(f32[6144]{0:T(1024)S(1)} %add_add_fusion), channel_id=1, source_target_pairs={{0,4},{1,5},{2,6},{3,7},{4,0},{5,1},{6,2},{7,3},{8,12},{9,13},{10,... | collective-permute-start | bytes 73736 | tf_op jit(solution)/shard_map/ppermute | solution.py:29
Sparse Core Ops, SparseCore 0:
  50.7 54.9 reduce-scatter.4
  108.3 47.5 reduce-scatter.2

commit v13 on v11

--- a/solution.py
+++ b/solution.py
@@ -77,8 +77,11 @@
     first_term = jnp.einsum(
         "rjd,rjf->jdf", slots_here, hidden_grad, preferred_element_type=jnp.float32
     )
+    slots_first, grads_first = lax.optimization_barrier((slots_here, grads_here))
+    early = jnp.einsum("rjd,jdf->rjf", slots_first, expert_in, preferred_element_type=jnp.float32)
     second_term = jnp.einsum(
-        "rjf,rjd->jfd", activated_low, grads_here, preferred_element_type=jnp.float32
+        "rjf,rjd->jfd", jax.nn.gelu(early).astype(jnp.bfloat16), grads_first,
+        preferred_element_type=jnp.float32,
     )
     grad_in = lax.psum_scatter(
         first_term.astype(jnp.bfloat16), "dp", scatter_dimension=2, tiled=True

time: 166 us -> 176 us (1.060)
  matrix products: 25.5 us -> 29.7 us
  starting transfers between devices: 26.8 us -> 30.7 us
    dot_general x1, matrix products: 0.98 us -> 4.57 us  [on_device(): jnp.einsum('rjf,jfd->rjd', activated_low, expert_out, preferred_element_t...]
    ppermute x9, starting transfers between devices: 12.9 us -> 16.2 us  [_sum_everywhere(): lax.ppermute(mine, axes, pairs(m << shift))]
    ppermute x3, waiting for transfers between devices: 3.28 us -> 6.58 us  [_sum_everywhere(): got.append(lax.ppermute(part, axes, pairs(m)))]
    dot_general x2 -> x1, matrix products: 3.81 us -> 4.61 us  [on_device(): jnp.einsum('rjf,rjd->jfd', jax.nn.gelu(early).astype(jnp.bfloat16), grads...]
    unnamed x23 -> x17, local copies, waits for them, and re-layouts: 2.87 us -> 3.65 us
  transfers between devices with their start and end apart: 18 -> 18, of which waited for: 13 -> 9; matrix products, arithmetic and copies ran while one was open for 22% -> 22% of each run, Pallas kernels for 0% -> 0%
where the time goes in v13:
time: 176 us; the launch traced here: 174 us
  waiting for transfers between devices  42.5 us (24%)
  blocking collectives  33.8 us (19%)
  starting transfers between devices  30.7 us (17%)
  matrix products  29.7 us (17%)
  local copies, waits for them, and re-layouts  15.5 us (9%)
  between operations  14.3 us (8%)
  other arithmetic  7.69 us (4%)
    all_to_all x1, blocking collectives, on_device(): lax.all_to_all(jnp.stack([slots, slot_grads]), 'expert', split_axis=2, co...  33.8 us
    all_to_all x1, waiting for transfers between devices, on_device(): lax.all_to_all(jnp.stack([outputs_here, input_grad_here]), 'expert', spli...  27.3 us
    ppermute x9, starting transfers between devices, _sum_everywhere(): lax.ppermute(mine, axes, pairs(m << shift))  16.2 us
    ppermute x9, waiting for transfers between devices, _sum_everywhere(): lax.ppermute(mine, axes, pairs(m << shift))  8.58 us
    ppermute x3, waiting for transfers between devices, _sum_everywhere(): got.append(lax.ppermute(part, axes, pairs(m)))  6.58 us
    ppermute x3, starting transfers between devices, _sum_everywhere(): got.append(lax.ppermute(part, axes, pairs(m)))  4.8 us
    ppermute x3, starting transfers between devices, _sum_everywhere(): got = [mine] + [lax.ppermute(mine, axes, pairs(m)) for m in range(1, 4)]  4.77 us
    all_to_all x1, starting transfers between devices, on_device(): lax.all_to_all(jnp.stack([outputs_here, input_grad_here]), 'expert', spli...  4.65 us
  transfers between devices with their start and end apart: 18, of which 9 were waited for; matrix products, arithmetic and copies ran while one was open for 22% of the time, Pallas kernels for 0%

profile of v13, /device:TPU:32, one launch (start us, length us, event | category | flops | bytes accessed | tf_op | source)
XLA Modules:
  0.0 174.2 jit_solution(2723541131884519264)
XLA Ops:
  7.2 2.2 %fusion.56 = (f32[8,64]{1,0:T(8,128)S(1)}, f32[8,196]{1,0:T(8,128)S(1)}, f32[8,64,196]{2,1,0:T(8,128)S(1)}) fusion(bf16[8,196,384]{2,0,1:T(8,128)(2,1)} %param.5, bf16[384,64]{0,1:T(8,128)(2,1)} %param.6), kind=kOutput, calls=%fused_computation.94 | convolution fusion | flops 77268960 | bytes 1663104 | tf_op jit(solution)/shard_map/bpd,ds->bsp/dot_general | solution.py:44
  11.8 33.8 %all_to_all.30 = bf16[2,8,64,384]{3,1,0,2:T(8,128)(2,1)S(1)} all-to-all(bf16[2,8,64,384]{3,1,0,2:T(8,128)(2,1)S(1)} %copy.25), channel_id=1, replica_groups=mesh['expert'=32,'dp'=8] {'expert'}, dimensions={2} | all-to-all | bytes 1572864 | tf_op jit(solution)/shard_map/all_to_all | solution.py:55
  47.3 4.6 %convolution_convert_fusion = bf16[2,1536,384]{2,1,0:T(8,128)(2,1)} fusion(bf16[256,2,384]{2,0,1:T(8,128)(2,1)} %get-tuple-element.11, bf16[256,2,384]{2,0,1:T(8,128)(2,1)S(1)} %get-tuple-element.10, bf16[2,384,1536]{2,1,0:T(8,128)(2,1)S(1)} %copy-done), kind=kOutput, calls=%fused_computation.4 | convolution fusion | flops 1216217088 | bytes 5505024 | tf_op jit(solution)/shard_map/rjf,rjd->jfd/dot_general | solution.py:82
  51.9 2.8 %convolution_bitcast_fusion.2 = f32[256,2,1536]{2,0,1:T(8,128)S(1)} fusion(bf16[2,1536,384]{2,1,0:T(8,128)(2,1)} %param.8, bf16[2,32,8,2,384]{4,2,1,3,0:T(8,128)(2,1)} %bitcast.99), kind=kOutput, calls=%fused_computation.8 | convolution fusion | flops 603979776 | bytes 5898240 | tf_op jit(solution)/shard_map/rjd,jfd->rjf/dot_general | solution.py:64
  54.8 2.7 %fusion.6 = bf16[256,2,1536]{2,0,1:T(8,128)(2,1)S(1)} fusion(f32[256,2,1536]{2,0,1:T(8,128)S(1)} %convolution_bitcast_fusion.2, bf16[256,2,384]{2,0,1:T(8,128)(2,1)S(1)} %get-tuple-element.10, bf16[2,384,1536]{2,1,0:T(8,128)(2,1)S(1)} %copy-done), kind=kOutput, calls=%fused_computation.16 | convolution fusion | flops 619708416 | bytes 7471104 | tf_op jit(solution)/shard_map/rjd,jdf->rjf/dot_general | solution.py:68
  57.5 1.2 copy-done.2
  59.6 4.6 %fusion.23 = bf16[1,256,2,384]{3,1,2,0:T(8,128)(2,1)} fusion(bf16[2,1536,384]{2,1,0:T(8,128)(2,1)} %param.8, bf16[2,384,1536]{2,1,0:T(8,128)(2,1)S(1)} %copy-done, bf16[2,32,8,2,384]{4,2,1,3,0:T(8,128)(2,1)} %bitcast.100), kind=kOutput, calls=%fused_computation.39 | convolution fusion | flops 1215234048 | bytes 5505024 | tf_op jit(solution)/shard_map/rjf,jfd->rjd/dot_general | solution.py:61
  65.3 1.7 copy.27
  67.0 4.6 %all-to-all-start.1 = ((bf16[2,256,2,384]{3,2,0,1:T(2,128)(2,1)}), bf16[2,256,2,384]{3,2,0,1:T(2,128)(2,1)}, u32[]{:S(2)}, u32[]{:S(2)}) async-start(bf16[2,256,2,384]{3,2,0,1:T(2,128)(2,1)} %copy.27), calls=%async_computation.1 | async-start | bytes 1572864 | tf_op jit(solution)/shard_map/all_to_all | solution.py:73
  71.9 4.0 %convolution_convert_fusion.1 = bf16[2,384,1536]{1,2,0:T(8,128)(2,1)} fusion(bf16[256,2,1536]{2,0,1:T(8,128)(2,1)} %copy-done.2, bf16[2,32,8,2,384]{4,2,1,3,0:T(8,128)(2,1)} %bitcast.101), kind=kOutput, calls=%fused_computation.5 | convolution fusion | flops 605159424 | bytes 4325376 | tf_op jit(solution)/shard_map/rjd,rjf->jdf/dot_general | solution.py:77
  75.9 27.3 %all-to-all-done.1 = bf16[2,256,2,384]{3,2,0,1:T(2,128)(2,1)} async-done(((bf16[2,256,2,384]{3,2,0,1:T(2,128)(2,1)}), bf16[2,256,2,384]{3,2,0,1:T(2,128)(2,1)}, u32[]{:S(2)}, u32[]{:S(2)}) %all-to-all-start.1) | async-done | bytes 786464 | tf_op jit(solution)/shard_map/all_to_all | solution.py:73
  103.2 1.9 %copy.55 = bf16[2,32,8,2,384]{4,3,1,2,0:T(2,128)(2,1)S(1)} copy(bf16[2,32,8,2,384]{4,3,0,2,1:T(2,128)(2,1)} %bitcast.23) | data formatting | bytes 1572864 | tf_op jit(solution)/shard_map/all_to_all | solution.py:73
  105.1 1.5 fusion.57
  107.4 1.1 squeeze.27
  108.6 2.0 %fusion.27 = f32[8,64,196]{2,1,0:T(8,128)S(1)} fusion(bf16[8,64,384]{2,1,0:T(8,128)(2,1)} %squeeze.28, bf16[8,196,384]{2,0,1:T(8,128)(2,1)} %param.9), kind=kOutput, calls=%fused_computation.44 | convolution fusion | flops 77070336 | bytes 1998848 | tf_op jit(solution)/shard_map/bpd,bsd->bsp/dot_general | solution.py:92
  110.6 2.1 %multiply_reduce_fusion.1 = (f32[8,64]{1,0:T(8,128)S(1)}, f32[8,196]{1,0:T(8,128)S(1)}, f32[8,64,196]{2,1,0:T(8,128)S(1)}) fusion(f32[8,64]{1,0:T(8,128)S(1)} %get-tuple-element.22, f32[8,64,196]{2,1,0:T(8,128)S(1)} %get-tuple-element.38, f32[8,64]{1,0:T(8,128)S(1)} %get-tuple-element.24, f32[8,64,196]{2,1,0:T(8,128)S(1)} %fusion.27, ...), kind=kOutput, calls=%fused_computation.58 | convolution fusion | flops 77871072 | bytes 2826624 | tf_op jit(solution)/shard_map/bpd,bsd->bsp/dot_general | solution.py:93
  114.8 1.6 reshape.22
  116.4 1.2 constant_dynamic-slice_fusion.2
  117.7 4.7 %collective-permute-start.1 = (f32[6144]{0:T(1024)S(1)}, f32[6144]{0:T(1024)S(1)}, u32[]{:S(2)}, u32[]{:S(2)}) collective-permute-start(f32[6144]{0:T(1024)S(1)} %bitcast.111), channel_id=1, source_target_pairs={{0,2},{1,3},{2,0},{3,1},{4,6},{5,7},{6,4},{7,5},{8,10},{9,11},{10,... | collective-permute-start | bytes 73736 | tf_op jit(solution)/shard_map/ppermute | solution.py:25
  122.4 2.1 %collective-permute-done.1 = f32[6144]{0:T(1024)S(1)} collective-permute-done((f32[6144]{0:T(1024)S(1)}, f32[6144]{0:T(1024)S(1)}, u32[]{:S(2)}, u32[]{:S(2)}) %collective-permute-start.1) | collective-permute-done | bytes 24608 | tf_op jit(solution)/shard_map/ppermute | solution.py:25
  124.5 4.5 %collective-permute-done.2 = f32[6144]{0:T(1024)S(1)} collective-permute-done((f32[6144]{0:T(1024)S(1)}, f32[6144]{0:T(1024)S(1)}, u32[]{:S(2)}, u32[]{:S(2)}) %collective-permute-start.2) | collective-permute-done | bytes 24608 | tf_op jit(solution)/shard_map/ppermute | solution.py:25
  129.0 4.7 %collective-permute-start.3 = (f32[6144]{0:T(1024)S(1)}, f32[6144]{0:T(1024)S(1)}, u32[]{:S(2)}, u32[]{:S(2)}) collective-permute-start(f32[6144]{0:T(1024)S(1)} %add_add_fusion.3), channel_id=1, source_target_pairs={{0,4},{1,5},{2,6},{3,7},{4,0},{5,1},{6,2},{7,3},{8,12},{9,13},{10,... | collective-permute-start | bytes 73736 | tf_op jit(solution)/shard_map/ppermute | solution.py:28
  134.0 1.9 %collective-permute-done.3 = f32[6144]{0:T(1024)S(1)} collective-permute-done((f32[6144]{0:T(1024)S(1)}, f32[6144]{0:T(1024)S(1)}, u32[]{:S(2)}, u32[]{:S(2)}) %collective-permute-start.3) | collective-permute-done | bytes 24608 | tf_op jit(solution)/shard_map/ppermute | solution.py:28
  138.4 3.1 %collective-permute-start.7 = (f32[6144]{0:T(1024)}, f32[6144]{0:T(1024)}, u32[]{:S(2)}, u32[]{:S(2)}) collective-permute-start(f32[6144]{0:T(1024)} %add_add_fusion.2), channel_id=1, source_target_pairs={{0,32},{1,33},{2,34},{3,35},{4,36},{5,37},{6,38},{7,39},{8,40},{9,... | collective-permute-start | bytes 73736 | tf_op jit(solution)/shard_map/ppermute | solution.py:28
  142.3 1.8 %collective-permute-done.7 = f32[6144]{0:T(1024)} collective-permute-done((f32[6144]{0:T(1024)}, f32[6144]{0:T(1024)}, u32[]{:S(2)}, u32[]{:S(2)}) %collective-permute-start.7) | collective-permute-done | bytes 24608 | tf_op jit(solution)/shard_map/ppermute | solution.py:28
  144.1 2.7 %collective-permute-done.8 = f32[6144]{0:T(1024)} collective-permute-done((f32[6144]{0:T(1024)}, f32[6144]{0:T(1024)}, u32[]{:S(2)}, u32[]{:S(2)}) %collective-permute-start.8) | collective-permute-done | bytes 24608 | tf_op jit(solution)/shard_map/ppermute | solution.py:28
  147.7 1.2 collective-permute-start.11
  148.9 5.3 %collective-permute-start.9 = (f32[6144]{0:T(1024)S(1)}, f32[6144]{0:T(1024)S(1)}, u32[]{:S(2)}, u32[]{:S(2)}) collective-permute-start(f32[6144]{0:T(1024)S(1)} %add_add_fusion.1), channel_id=1, source_target_pairs={{0,64},{1,65},{2,66},{3,67},{4,68},{5,69},{6,70},{7,71},{8,72},{9,... | collective-permute-start | bytes 73736 | tf_op jit(solution)/shard_map/ppermute | solution.py:28
  156.5 4.6 %collective-permute-start.14 = (f32[6144]{0:T(1024)S(1)}, f32[6144]{0:T(1024)S(1)}, u32[]{:S(2)}, u32[]{:S(2)}) collective-permute-start(f32[6144]{0:T(1024)S(1)} %add_add_fusion), channel_id=1, source_target_pairs={{0,3},{1,2},{2,1},{3,0},{4,7},{5,6},{6,5},{7,4},{8,11},{9,10},{10,... | collective-permute-start | bytes 73736 | tf_op jit(solution)/shard_map/ppermute | solution.py:29
  161.7 1.2 copy.34
  163.7 1.8 %convert_element_type.67 = f32[2,192,384]{2,1,0:T(8,128)} convert(bf16[2,192,384]{2,1,0:T(8,128)(2,1)} %reduce-scatter.5.cloned.1.call-done) | non-fusion elementwise | flops 147456 | bytes 884736 | tf_op jit(solution)/shard_map/convert_element_type | solution.py:91
  165.5 1.8 %convert_element_type.64 = f32[2,384,192]{1,2,0:T(8,128)} convert(bf16[2,384,192]{1,2,0:T(8,128)(2,1)} %reduce-scatter.3.cloned.1.call-done) | non-fusion elementwise | flops 147456 | bytes 884736 | tf_op jit(solution)/shard_map/convert_element_type | solution.py:88
  (61 shorter events, 17.7 us)
Async XLA Ops:
  7.2 40.1 %copy-start = (bf16[2,384,1536]{2,1,0:T(8,128)(2,1)S(1)}, bf16[2,384,1536]{2,1,0:T(8,128)(2,1)}, u32[]{:S(2)}) copy-start(bf16[2,384,1536]{2,1,0:T(8,128)(2,1)} %param.7) | copy-start | bytes 7077892
  7.2 156.5 %reduce-scatter.5.cloned.1.call-start = ((), (), s32[]{:S(2)}) async-start(), calls=%async_computation.5 | async-start | bytes 2654208 | tf_op jit(solution)/shard_map/reduce_scatter | solution.py:89
  7.2 2.5 %copy-start.3 = (bf16[8,196,384]{2,0,1:T(8,128)(2,1)S(1)}, bf16[8,196,384]{2,0,1:T(8,128)(2,1)}, u32[]{:S(2)}) copy-start(bf16[8,196,384]{2,0,1:T(8,128)(2,1)} %param.5) | copy-start | bytes 3612676
  9.4 1.3 copy-start.5
  9.7 100.9 %copy-start.7 = (f32[8,196]{1,0:T(8,128)}, f32[8,196]{1,0:T(8,128)S(1)}, u32[]{:S(2)}) copy-start(f32[8,196]{1,0:T(8,128)S(1)} %get-tuple-element.23) | copy-start | bytes 18820
  45.6 0.9 copy-start.1
  57.5 1.2 copy-start.2
  67.0 36.2 %all-to-all-start.1 = ((bf16[2,256,2,384]{3,2,0,1:T(2,128)(2,1)}), bf16[2,256,2,384]{3,2,0,1:T(2,128)(2,1)}, u32[]{:S(2)}, u32[]{:S(2)}) async-start(bf16[2,256,2,384]{3,2,0,1:T(2,128)(2,1)} %copy.27), calls=%async_computation.1 | async-start | bytes 1572864 | tf_op jit(solution)/shard_map/all_to_all | solution.py:73
  71.6 93.9 %reduce-scatter.3.cloned.1.call-start = ((), (), s32[]{:S(2)}) async-start(), calls=%async_computation.4 | async-start | bytes 2654208 | tf_op jit(solution)/shard_map/reduce_scatter | solution.py:86
  110.6 3.2 %copy-start.4 = (bf16[8,196,384]{2,0,1:T(8,128)(2,1)S(1)}, bf16[8,196,384]{2,0,1:T(8,128)(2,1)}, u32[]{:S(2)}) copy-start(bf16[8,196,384]{2,0,1:T(8,128)(2,1)} %param.5) | copy-start | bytes 3612676
  117.6 4.8 %collective-permute-start = (f32[6144]{0:T(1024)S(1)}, f32[6144]{0:T(1024)S(1)}, u32[]{:S(2)}, u32[]{:S(2)}) collective-permute-start(f32[6144]{0:T(1024)S(1)} %bitcast.112), channel_id=1, source_target_pairs={{0,1},{1,0},{2,3},{3,2},{4,5},{5,4},{6,7},{7,6},{8,9},{9,8},{10,11... | collective-permute-start | bytes 73736 | tf_op jit(solution)/shard_map/ppermute | solution.py:25
  117.7 6.8 %collective-permute-start.1 = (f32[6144]{0:T(1024)S(1)}, f32[6144]{0:T(1024)S(1)}, u32[]{:S(2)}, u32[]{:S(2)}) collective-permute-start(f32[6144]{0:T(1024)S(1)} %bitcast.111), channel_id=1, source_target_pairs={{0,2},{1,3},{2,0},{3,1},{4,6},{5,7},{6,4},{7,5},{8,10},{9,11},{10,... | collective-permute-start | bytes 73736 | tf_op jit(solution)/shard_map/ppermute | solution.py:25
  122.4 6.6 %collective-permute-start.2 = (f32[6144]{0:T(1024)S(1)}, f32[6144]{0:T(1024)S(1)}, u32[]{:S(2)}, u32[]{:S(2)}) collective-permute-start(f32[6144]{0:T(1024)S(1)} %bitcast.110), channel_id=1, source_target_pairs={{0,3},{1,2},{2,1},{3,0},{4,7},{5,6},{6,5},{7,4},{8,11},{9,10},{10,... | collective-permute-start | bytes 73736 | tf_op jit(solution)/shard_map/ppermute | solution.py:25
  129.0 6.9 %collective-permute-start.3 = (f32[6144]{0:T(1024)S(1)}, f32[6144]{0:T(1024)S(1)}, u32[]{:S(2)}, u32[]{:S(2)}) collective-permute-start(f32[6144]{0:T(1024)S(1)} %add_add_fusion.3), channel_id=1, source_target_pairs={{0,4},{1,5},{2,6},{3,7},{4,0},{5,1},{6,2},{7,3},{8,12},{9,13},{10,... | collective-permute-start | bytes 73736 | tf_op jit(solution)/shard_map/ppermute | solution.py:28
  133.7 2.1 %collective-permute-start.4 = (f32[6144]{0:T(1024)S(1)}, f32[6144]{0:T(1024)S(1)}, u32[]{:S(2)}, u32[]{:S(2)}) collective-permute-start(f32[6144]{0:T(1024)S(1)} %add_add_fusion.3), channel_id=1, source_target_pairs={{0,8},{1,9},{2,10},{3,11},{4,12},{5,13},{6,14},{7,15},{8,0},{9,1},... | collective-permute-start | bytes 73736 | tf_op jit(solution)/shard_map/ppermute | solution.py:28
  133.7 3.3 %collective-permute-start.5 = (f32[6144]{0:T(1024)S(1)}, f32[6144]{0:T(1024)S(1)}, u32[]{:S(2)}, u32[]{:S(2)}) collective-permute-start(f32[6144]{0:T(1024)S(1)} %add_add_fusion.3), channel_id=1, source_target_pairs={{0,12},{1,13},{2,14},{3,15},{4,8},{5,9},{6,10},{7,11},{8,4},{9,5},... | collective-permute-start | bytes 73736 | tf_op jit(solution)/shard_map/ppermute | solution.py:28
  137.6 4.7 %collective-permute-start.6 = (f32[6144]{0:T(1024)}, f32[6144]{0:T(1024)}, u32[]{:S(2)}, u32[]{:S(2)}) collective-permute-start(f32[6144]{0:T(1024)} %add_add_fusion.2), channel_id=1, source_target_pairs={{0,16},{1,17},{2,18},{3,19},{4,20},{5,21},{6,22},{7,23},{8,24},{9,... | collective-permute-start | bytes 73736 | tf_op jit(solution)/shard_map/ppermute | solution.py:28
  138.4 5.7 %collective-permute-start.7 = (f32[6144]{0:T(1024)}, f32[6144]{0:T(1024)}, u32[]{:S(2)}, u32[]{:S(2)}) collective-permute-start(f32[6144]{0:T(1024)} %add_add_fusion.2), channel_id=1, source_target_pairs={{0,32},{1,33},{2,34},{3,35},{4,36},{5,37},{6,38},{7,39},{8,40},{9,... | collective-permute-start | bytes 73736 | tf_op jit(solution)/shard_map/ppermute | solution.py:28
  141.4 5.4 %collective-permute-start.8 = (f32[6144]{0:T(1024)}, f32[6144]{0:T(1024)}, u32[]{:S(2)}, u32[]{:S(2)}) collective-permute-start(f32[6144]{0:T(1024)} %add_add_fusion.2), channel_id=1, source_target_pairs={{0,48},{1,49},{2,50},{3,51},{4,52},{5,53},{6,54},{7,55},{8,56},{9,... | collective-permute-start | bytes 73736 | tf_op jit(solution)/shard_map/ppermute | solution.py:28
  142.3 18.8 %copy-start.6 = (bf16[384,64]{0,1:T(8,128)(2,1)S(1)}, bf16[384,64]{0,1:T(8,128)(2,1)}, u32[]{:S(2)}) copy-start(bf16[384,64]{0,1:T(8,128)(2,1)} %param.6) | copy-start | bytes 147460
  147.6 8.3 %collective-permute-start.10 = (f32[6144]{0:T(1024)S(1)}, f32[6144]{0:T(1024)S(1)}, u32[]{:S(2)}, u32[]{:S(2)}) collective-permute-start(f32[6144]{0:T(1024)S(1)} %add_add_fusion.1), channel_id=1, source_target_pairs={{0,128},{1,129},{2,130},{3,131},{4,132},{5,133},{6,134},{7,135},{8... | collective-permute-start | bytes 73736 | tf_op jit(solution)/shard_map/ppermute | solution.py:28
  147.7 8.2 %collective-permute-start.11 = (f32[6144]{0:T(1024)S(1)}, f32[6144]{0:T(1024)S(1)}, u32[]{:S(2)}, u32[]{:S(2)}) collective-permute-start(f32[6144]{0:T(1024)S(1)} %add_add_fusion.1), channel_id=1, source_target_pairs={{0,192},{1,193},{2,194},{3,195},{4,196},{5,197},{6,198},{7,199},{8... | collective-permute-start | bytes 73736 | tf_op jit(solution)/shard_map/ppermute | solution.py:28
  148.9 7.4 %collective-permute-start.9 = (f32[6144]{0:T(1024)S(1)}, f32[6144]{0:T(1024)S(1)}, u32[]{:S(2)}, u32[]{:S(2)}) collective-permute-start(f32[6144]{0:T(1024)S(1)} %add_add_fusion.1), channel_id=1, source_target_pairs={{0,64},{1,65},{2,66},{3,67},{4,68},{5,69},{6,70},{7,71},{8,72},{9,... | collective-permute-start | bytes 73736 | tf_op jit(solution)/shard_map/ppermute | solution.py:28
  156.3 6.6 %collective-permute-start.12 = (f32[6144]{0:T(1024)S(1)}, f32[6144]{0:T(1024)S(1)}, u32[]{:S(2)}, u32[]{:S(2)}) collective-permute-start(f32[6144]{0:T(1024)S(1)} %add_add_fusion), channel_id=1, source_target_pairs={{0,1},{1,0},{2,3},{3,2},{4,5},{5,4},{6,7},{7,6},{8,9},{9,8},{10,11... | collective-permute-start | bytes 73736 | tf_op jit(solution)/shard_map/ppermute | solution.py:29
  156.4 6.5 %collective-permute-start.13 = (f32[6144]{0:T(1024)S(1)}, f32[6144]{0:T(1024)S(1)}, u32[]{:S(2)}, u32[]{:S(2)}) collective-permute-start(f32[6144]{0:T(1024)S(1)} %add_add_fusion), channel_id=1, source_target_pairs={{0,2},{1,3},{2,0},{3,1},{4,6},{5,7},{6,4},{7,5},{8,10},{9,11},{10,... | collective-permute-start | bytes 73736 | tf_op jit(solution)/shard_map/ppermute | solution.py:29
  156.5 6.4 %collective-permute-start.14 = (f32[6144]{0:T(1024)S(1)}, f32[6144]{0:T(1024)S(1)}, u32[]{:S(2)}, u32[]{:S(2)}) collective-permute-start(f32[6144]{0:T(1024)S(1)} %add_add_fusion), channel_id=1, source_target_pairs={{0,3},{1,2},{2,1},{3,0},{4,7},{5,6},{6,5},{7,4},{8,11},{9,10},{10,... | collective-permute-start | bytes 73736 | tf_op jit(solution)/shard_map/ppermute | solution.py:29
Sparse Core Ops, SparseCore 0:
  52.1 54.7 reduce-scatter.4
  109.4 47.7 reduce-scatter.2
